TPU v7x, 128 devices: a whole 4x4x4 slice. The times are simulated.
128 devices in a mesh: req: 16 (over y, z), tp: 8 (over x, core).
Axes of the slice: x: 4, y: 4, z: 4, core: 2. Of those that a mesh axis runs over, the one named last changes fastest.
Arguments:
- suffix_tokens: bfloat16 [256, 112, 2880], P('req'), may hold values from -40 to 40
- route_lengths: int32 [16, 16], replicated, may hold values from 1 to 112, 768 in all within a row
- dest_perm: int32 [16, 16], replicated, may hold values from 0 to 15, each once within a row
- attach_points: int32 [256], replicated, may hold values from 256 to 8192
- prefix_cache: bfloat16 [64, 128, 8, 128], P('req', None, 'tp'), may hold values from -120 to 120
- block_of_slot: int32 [64], replicated, may hold values from 0 to 63, each once
- sink_logits: float32 [64], P('tp'), may hold values from 0 to 6
- attn_gain: bfloat16 [2880], replicated, may hold values from 0.099609375 to 1.8984375
- w_query: bfloat16 [2880, 4096], P(None, 'tp'), may hold values from -0.109375 to 0.109375
- w_keyval: bfloat16 [2880, 8, 128], P(None, 'tp'), may hold values from -0.109375 to 0.109375
- w_out: bfloat16 [4096, 2880], P('tp'), may hold values from -0.09375 to 0.09375
- mlp_gain: bfloat16 [2880], replicated, may hold values from 0.099609375 to 1.8984375
- w_gate: bfloat16 [2880, 2880], P(None, 'tp'), may hold values from -0.109375 to 0.109375
- w_up: bfloat16 [2880, 2880], P(None, 'tp'), may hold values from -0.109375 to 0.109375
- w_down: bfloat16 [2880, 2880], P('tp'), may hold values from -0.109375 to 0.109375
Outputs:
- layer_out: bfloat16 [256, 112, 2880], P('req', None, 'tp')
Inputs may be any that keep to these rules, and one draw needn't show every extreme that they name: `route_lengths`: each row sums to 768, and the largest entry of each row is 112. `dest_perm`: each row is a permutation of the devices of req. `block_of_slot`: a permutation.
All inputs are finite; a program needn't handle non-finite values.
Results may differ from a plain program's by a relative error of at most 0.013.
Values may be sent and summed in bfloat16 or wider, within the bound.
No kernel may reach another device: no remote copies, remote signals or barrier semaphores. Data moves between devices by JAX's collectives and lax.ppermute only.
A program may use at most 192 MiB of HBM per device.

v0:
```python
import jax
import jax.numpy as jnp
from jax import lax
from jax.sharding import PartitionSpec as P

WINDOW = 128
CAP = 768


ROPE_BASE = 150000.0
EPSILON = 1e-05


def norm_rows(inputs, gains):
    widened = inputs.astype(jnp.float32)
    factor = lax.rsqrt(jnp.mean(widened * widened, axis=-1, keepdims=True) + EPSILON)
    return (widened * factor * gains.astype(jnp.float32)).astype(jnp.bfloat16)


def rotate(vectors, positions):
    half_dim = vectors.shape[-1] // 2
    frequency = ROPE_BASE ** (-(jnp.arange(half_dim).astype(jnp.float32) * 2.0 / vectors.shape[-1]))
    angles = positions.astype(jnp.float32)[:, None, None] * frequency
    cosine = jnp.cos(angles)
    sine_part = jnp.sin(angles)
    first_half = vectors[..., :half_dim]
    second = vectors[..., half_dim:]
    return jnp.concatenate(
        [first_half * cosine - second * sine_part, second * cosine + first_half * sine_part],
        axis=-1,
    )


def attend(query_slots, paired_slots, tail_rows, sink_logits):
    peers, slot_length = (query_slots.shape[0], query_slots.shape[1])
    value_heads = paired_slots.shape[2]
    head_dim = paired_slots.shape[3] // 2
    group_size = query_slots.shape[2] // value_heads
    window = tail_rows.shape[1]
    grouped_query = query_slots.reshape(peers, slot_length, value_heads, group_size, head_dim)
    near_keys = jnp.concatenate([tail_rows, paired_slots], axis=1)
    score_scale = head_dim ** (-0.5)
    near_scores = (
        jnp.einsum(
            "ntkgd,nskd->nkgts",
            grouped_query,
            near_keys[..., :head_dim],
            preferred_element_type=jnp.float32,
        )
        * score_scale
    )
    sink_scores = sink_logits.reshape(value_heads, group_size)[None, :, :, None, None]
    slot_steps = jnp.arange(slot_length)
    columns = jnp.arange(window + slot_length)
    allowed = jnp.where(
        columns[None, :] < window,
        columns[None, :] > slot_steps[:, None],
        columns[None, :] - window <= slot_steps[:, None],
    )
    near_scores = jnp.where(allowed, near_scores, -jnp.inf)
    largest = jnp.maximum(jnp.max(near_scores, axis=-1, keepdims=True), sink_scores)
    near_weights = jnp.exp(near_scores - largest)
    normalizer = jnp.sum(near_weights, axis=-1, keepdims=True) + jnp.exp(sink_scores - largest)
    near_weights = (near_weights / normalizer).astype(jnp.bfloat16)
    mixed = jnp.einsum(
        "nkgts,nskd->ntkgd",
        near_weights,
        near_keys[..., head_dim:],
        preferred_element_type=jnp.float32,
    )
    return mixed.astype(jnp.bfloat16).reshape(
        peers * slot_length, value_heads * group_size * head_dim
    )


def fetch_prefix(attach_slots, prefix_cache, block_of_slot, window):
    total_blocks = block_of_slot.shape[0]
    block_len = prefix_cache.shape[1]
    catalog = jnp.arange(total_blocks)
    home_row = jnp.sum(
        jnp.where(block_of_slot[None, :] == catalog[:, None], catalog[None, :], 0), axis=1
    )
    wanted = attach_slots[:, None] - window + jnp.arange(window)[None, :]
    block_id = wanted // block_len
    tail_store = jnp.sum(jnp.where(block_id[..., None] == catalog, home_row, 0), axis=-1)
    tail_offset = wanted - block_id * block_len
    trailing = prefix_cache.shape[2:]
    initial = jnp.zeros((attach_slots.shape[0], window) + trailing, jnp.bfloat16)
    shard_rows = lax.all_gather(prefix_cache, "req", axis=0, tiled=True)
    held_blocks = shard_rows.shape[0]
    flat_rows = shard_rows.reshape((held_blocks * block_len,) + trailing)
    inside = (tail_store >= 0) & (tail_store < held_blocks)
    picked = flat_rows[jnp.clip(tail_store, 0, held_blocks - 1) * block_len + tail_offset]
    return jnp.where(inside[..., None, None], picked, initial)


def local(
    suffix_tokens,
    route_lengths,
    dest_perm,
    attach_points,
    prefix_cache,
    block_of_slot,
    sink_logits,
    attn_gain,
    w_query,
    w_keyval,
    w_out,
    mlp_gain,
    w_gate,
    w_up,
    w_down,
):
    peers = lax.axis_size("req")
    splits = lax.axis_size("tp")
    request_index = lax.axis_index("req")
    tensor_index = lax.axis_index("tp")
    slot_count, slot_length, features = suffix_tokens.shape
    feature_share = features // splits
    value_heads = w_keyval.shape[1]
    head_dim = w_keyval.shape[2] // 2
    peer_ids = jnp.arange(peers)
    slot_steps = jnp.arange(slot_length)
    my_row = lax.dynamic_index_in_dim(dest_perm, request_index, 0, keepdims=False)
    attach_table = attach_points.reshape(peers, peers)
    arriving_lengths = lax.dynamic_index_in_dim(route_lengths, request_index, 0, keepdims=False)
    arriving = (dest_perm == request_index).astype(jnp.int32)
    arriving_attach = jnp.sum(attach_table * arriving, axis=1)
    send_order = jnp.sum(
        jnp.where(my_row[None, :] == peer_ids[:, None], peer_ids[None, :], 0), axis=1
    )
    run_ends = jnp.cumsum(arriving_lengths)
    starts = run_ends - arriving_lengths
    packed_ids = jnp.arange(CAP)
    source_of = jnp.sum((run_ends[None, :] <= packed_ids[:, None]).astype(jnp.int32), axis=1)
    source_hot = (source_of[:, None] == peer_ids[None, :]).astype(jnp.int32)
    token_index = packed_ids - jnp.sum(source_hot * starts[None, :], axis=1)
    positions = jnp.sum(source_hot * arriving_attach[None, :], axis=1) + token_index
    flat_index = source_of * slot_length + token_index
    slot_source = jnp.clip(starts[:, None] + slot_steps[None, :], 0, CAP - 1).reshape(-1)
    live_mask = slot_steps[None, :] < arriving_lengths[:, None]

    def to_slots(values):
        return values[slot_source].reshape((peers, slot_length) + values.shape[1:])

    tail_rows = fetch_prefix(arriving_attach, prefix_cache, block_of_slot, WINDOW)
    landed = lax.all_to_all(
        suffix_tokens[send_order], "req", split_axis=0, concat_axis=0, tiled=True
    )
    input_rows = landed.reshape(peers * slot_length, features)[flat_index]
    row_total = input_rows.shape[0]
    normed_in = norm_rows(input_rows, attn_gain)
    queries = jnp.dot(normed_in, w_query, preferred_element_type=jnp.float32).reshape(
        row_total, -1, head_dim
    )
    queries = rotate(queries, positions).astype(jnp.bfloat16)
    paired = jnp.dot(
        normed_in, w_keyval.reshape(features, -1), preferred_element_type=jnp.float32
    ).reshape(row_total, value_heads, 2 * head_dim)
    rotated = rotate(paired[..., :head_dim], positions)
    paired = jnp.concatenate([rotated, paired[..., head_dim:]], axis=-1).astype(jnp.bfloat16)
    attended = attend(to_slots(queries), to_slots(paired), tail_rows, sink_logits)[flat_index]
    partial_value = jnp.dot(attended, w_out, preferred_element_type=jnp.float32)
    summed = lax.psum(partial_value.astype(jnp.bfloat16), "tp").astype(jnp.float32)
    residual = (input_rows.astype(jnp.float32) + summed).astype(jnp.bfloat16)
    normed_mid = norm_rows(residual, mlp_gain)
    residual_part = lax.dynamic_slice_in_dim(
        residual, tensor_index * feature_share, feature_share, 1
    )
    gate_proj = jnp.dot(normed_mid, w_gate, preferred_element_type=jnp.float32)
    up_proj = jnp.dot(normed_mid, w_up, preferred_element_type=jnp.float32)
    hidden = (jax.nn.silu(gate_proj) * up_proj).astype(jnp.bfloat16)
    down_sum = lax.psum_scatter(
        jnp.dot(hidden, w_down, preferred_element_type=jnp.float32).astype(jnp.bfloat16),
        "tp",
        scatter_dimension=1,
        tiled=True,
    ).astype(jnp.float32)
    out_rows = (residual_part.astype(jnp.float32) + down_sum).astype(jnp.bfloat16)
    out_slots = jnp.where(live_mask[..., None], to_slots(out_rows), jnp.zeros((), jnp.bfloat16))
    returned = lax.all_to_all(out_slots, "req", split_axis=0, concat_axis=0, tiled=True)
    return returned[my_row]


def solution(mesh):
    in_specs = (
        P("req", None, None),
        P(),
        P(),
        P(),
        P("req", None, "tp", None),
        P(),
        P("tp"),
        P(),
        P(None, "tp"),
        P(None, "tp", None),
        P("tp", None),
        P(),
        P(None, "tp"),
        P(None, "tp"),
        P("tp", None),
    )
    out_specs = P("req", None, "tp")
    return jax.shard_map(local, mesh=mesh, in_specs=in_specs, out_specs=out_specs, check_vma=False)
```

profile of v0, /device:TPU:7, one launch (start us, length us, event | category | flops | bytes accessed | tf_op | source)
XLA Modules:
  0.0 531.1 jit_solution(8293416445364604269)
XLA Ops:
  6.5 0.8 fusion.62
  7.4 0.1 select_reduce_fusion.5
  7.5 9.7 %gather_fusion = bf16[16,112,2880]{2,1,0:T(8,128)(2,1)} fusion(bf16[16,112,2880]{2,1,0:T(8,128)(2,1)} %param.15, s32[1024]{0:T(1024)S(1)} %pad_clamp_fusion.3), kind=kCustom, calls=%fused_computation | custom fusion | bytes 20643904 | tf_op jit(solution)/shard_map/gather | solution.py:148
  17.2 8.0 %all-to-all-start = ((bf16[16,112,2880]{2,1,0:T(8,128)(2,1)}), bf16[16,112,2880]{2,1,0:T(8,128)(2,1)}, u32[]{:S(2)}, u32[]{:S(2)}) async-start(bf16[16,112,2880]{2,1,0:T(8,128)(2,1)} %gather_fusion), calls=%async_computation | async-start | bytes 21102592 | tf_op jit(solution)/shard_map/all_to_all | solution.py:147
  25.2 0.7 all-gather.2.cloned.1.call-update
  25.9 0.7 fusion.77
  26.6 0.1 copy.44
  26.8 0.1 reduce.2
  27.0 0.7 bitcast_subtract_fusion.1
  27.7 0.1 min.22
  27.8 0.1 select_reduce_fusion.4
  28.0 0.1 convert_reduce_fusion
  28.0 0.7 fusion.61
  28.7 0.1 select_reduce_fusion.1
  29.0 0.1 select_reduce_fusion.3
  29.1 0.1 add_select_fusion.1
  29.2 0.2 select_reduce_fusion
  29.4 0.1 fusion.52
  29.5 2.5 multiply_cosine_fusion
  32.0 176.3 %all-gather.2.cloned.1.call-done = bf16[64,128,1,128]{3,1,2,0:T(8,128)(2,1)} async-done(((bf16[4,128,1,128]{3,1,2,0:T(8,128)(2,1)}), bf16[64,128,1,128]{3,1,2,0:T(8,128)(2,1)}) %all-gather.2.cloned.1.call-update) | async-done | bytes 2097168 | tf_op jit(solution)/shard_map/all_gather | solution.py:89
  208.3 7.5 %gather_fusion.2 = bf16[2048,128]{1,0:T(8,128)(2,1)S(1)} fusion(bf16[8192,128]{1,0:T(8,128)(2,1)} %bitcast.90, s32[2048]{0:T(1024)S(1)} %fusion.52), kind=kCustom, calls=%fused_computation.2 | custom fusion | bytes 1056768 | tf_op jit(solution)/shard_map/gather | solution.py:93
  215.8 1.0 copy.46
  216.8 1.9 broadcast_select_fusion.1
  218.7 14.6 %gather_fusion.1 = bf16[768,2880]{1,0:T(8,128)(2,1)} fusion(bf16[1792,2880]{1,0:T(8,128)(2,1)} %bitcast.4, s32[1024]{0:T(1024)S(1)} %pad_clamp_fusion.2), kind=kCustom, calls=%fused_computation.1 | custom fusion | bytes 8850432 | tf_op jit(solution)/shard_map/gather | solution.py:150
  233.3 6.6 %copy.45 = bf16[768,2880]{0,1:T(8,128)(2,1)} copy(bf16[768,2880]{1,0:T(8,128)(2,1)} %gather_fusion.1) | data formatting | bytes 8847360 | tf_op jit(solution)/shard_map/gather | solution.py:150
  239.9 3.3 fusion.5
  243.3 0.2 copy-done.1
  243.5 2.6 fusion.24
  246.1 0.4 fusion.43
  246.6 0.2 copy.47
  246.8 16.1 %gather_fusion.3 = bf16[1792,128]{1,0:T(8,128)(2,1)} fusion(bf16[768,128]{1,0:T(8,128)(2,1)S(1)} %copy.47, s32[2048]{0:T(1024)S(1)} %pad_clamp_fusion), kind=kCustom, calls=%fused_computation.3 | custom fusion | bytes 924672 | tf_op jit(solution)/shard_map/gather | solution.py:144
  262.9 2.0 copy.48
  264.9 6.1 %fusion.20 = f32[768,512]{0,1:T(8,128)S(1)} fusion(bf16[2880,512]{1,0:T(8,128)(2,1)} %param.23, bf16[768,2880]{0,1:T(8,128)(2,1)} %copy.45, f32[2880]{0:T(1024)S(1)} %convert_element_type.90, f32[768]{0:T(1024)S(1)} %add_rsqrt_fusion.1), kind=kOutput, calls=%fused_computation.40 | convolution fusion | flops 2273771520 | bytes 8960256 | tf_op jit(solution)/shard_map/dot_general | solution.py:153
  271.0 1.3 fusion.69
  272.2 3.2 copy.62
  275.4 3.2 copy.63
  278.6 3.7 subtract_convert_fusion
  282.3 2.1 pad_maximum_fusion
  284.4 5.7 %gather_fusion.4 = bf16[1792,8,64]{2,1,0:T(8,128)(2,1)} fusion(bf16[768,8,64]{2,1,0:T(8,128)(2,1)} %pad_maximum_fusion, s32[2048]{0:T(1024)S(1)} %pad_clamp_fusion), kind=kCustom, calls=%fused_computation.4 | custom fusion | bytes 3677184 | tf_op jit(solution)/shard_map/gather | solution.py:144
  290.1 5.1 fusion.1
  295.4 5.3 fusion
  300.6 0.1 exponential_add_fusion
  300.7 6.6 %convert_bitcast_fusion = bf16[16,112,1,8,64]{1,4,3,0,2:T(8,128)(2,1)} fusion(f32[16,8,112]{2,1,0:T(8,128)S(1)} %exponential_add_fusion, f32[16,8,112]{2,1,0:T(8,128)S(1)} %broadcast_maximum_fusion, f32[16,240,112,8]{1,2,3,0:T(8,128)S(1)} %get-tuple-element.18, pred[112,240]{1,0:T(8,128)(4,1)S(1)} %fusion.41, bf16[16,128,1,128]{1,3,0,2:T(8,128)(2,1)S(1)} %copy-done.3, ...), kind=kOutput, calls=%fused_computation.34 | convolution fusion | flops 459505664 | bytes 16722176 | tf_op jit(solution)/shard_map/nkgts,nskd->ntkgd/dot_general | solution.py:65
  307.3 4.8 copy.60
  312.2 5.9 %reshape.650 = bf16[1792,512]{1,0:T(8,128)(2,1)} reshape(bf16[16,112,1,8,64]{4,3,1,0,2:T(8,128)(2,1)} %copy.60) | data formatting | bytes 3670016 | tf_op jit(solution)/shard_map/reshape | solution.py:71
  318.1 5.1 gather_fusion.5
  323.2 5.7 %convolution_convert_fusion = bf16[768,2880]{0,1:T(8,128)(2,1)} fusion(bf16[768,512]{1,0:T(8,128)(2,1)} %gather_fusion.5, bf16[512,2880]{0,1:T(8,128)(2,1)S(1)} %copy-done), kind=kOutput, calls=%fused_computation.28 | convolution fusion | flops 2267136000 | bytes 8159232 | tf_op jit(solution)/shard_map/dot_general | solution.py:163
  328.9 0.2 reduce-scatter.2.cloned.1.call-start
  329.1 0.4 copy-done.8
  329.6 91.0 %all-reduce.2.cloned.1.call-done = bf16[768,2880]{0,1:T(8,128)(2,1)} async-done(((bf16[768,2880]{0,1:T(8,128)(2,1)}), bf16[768,2880]{0,1:T(8,128)(2,1)}) %all-reduce.2.cloned.1.call-update) | async-done | bytes 4423696 | tf_op jit(solution)/shard_map/psum | solution.py:164
  420.6 5.5 %fusion.2 = (f32[768]{0:T(1024)S(1)}, bf16[768,2880]{0,1:T(8,128)(2,1)S(1)}) fusion(bf16[768,2880]{0,1:T(8,128)(2,1)} %all-reduce.2.cloned.1.call-done, bf16[768,2880]{0,1:T(8,128)(2,1)} %copy.45), kind=kLoop, calls=%fused_computation.18 | loop fusion | flops 15482112 | bytes 13274112 | tf_op jit(solution)/shard_map/reduce_sum | solution.py:16
  426.1 2.0 copy-done.2
  428.1 3.2 fusion.18
  431.4 11.4 %convolution_convert_fusion.1 = bf16[768,2880]{0,1:T(8,128)(2,1)} fusion(bf16[360,2880]{1,0:T(8,128)(2,1)} %param.29, bf16[2880,360]{0,1:T(8,128)(2,1)} %param.28, bf16[768,2880]{0,1:T(8,128)(2,1)} %copy-done.2, f32[2880]{0:T(1024)S(1)} %convert_element_type.103, f32[768]{0:T(1024)S(1)} %add_rsqrt_fusion, f32[768,360]{0,1:T(8,128)} %fusion.18), kind=kOutput, calls=%fused_computation.29 | convolution fusion | flops 3197767680 | bytes 14115072 | tf_op jit(solution)/shard_map/dot_general | solution.py:174
  442.8 0.7 fusion.76
  443.5 36.8 %reduce-scatter.2.cloned.1.call-done = bf16[768,360]{0,1:T(8,128)(2,1)} async-done(((bf16[768,2880]{0,1:T(8,128)(2,1)}), bf16[768,360]{0,1:T(8,128)(2,1)}) %reduce-scatter.2.cloned.1.call-update) | async-done | bytes 552976 | tf_op jit(solution)/shard_map/reduce_scatter | solution.py:173
  480.4 2.1 add_convert_fusion.1
  482.5 1.4 copy.55
  483.9 6.0 %gather_fusion.6 = bf16[1792,360]{1,0:T(8,128)(2,1)} fusion(bf16[768,360]{1,0:T(8,128)(2,1)S(1)} %copy.55, s32[2048]{0:T(1024)S(1)} %pad_clamp_fusion), kind=kCustom, calls=%fused_computation.6 | custom fusion | bytes 2587648 | tf_op jit(solution)/shard_map/gather | solution.py:144
  489.9 2.7 broadcast_select_fusion
  492.6 6.8 %all-to-all-start.1 = ((bf16[16,112,360]{2,1,0:T(8,128)(2,1)}), bf16[16,112,360]{2,1,0:T(8,128)(2,1)}, u32[]{:S(2)}, u32[]{:S(2)}) async-start(bf16[16,112,360]{2,1,0:T(8,128)(2,1)} %broadcast_select_fusion), calls=%async_computation.2 | async-start | bytes 2752512 | tf_op jit(solution)/shard_map/all_to_all | solution.py:181
  499.4 0.7 fusion.60
  500.1 20.9 %all-to-all-done.1 = bf16[16,112,360]{2,1,0:T(8,128)(2,1)} async-done(((bf16[16,112,360]{2,1,0:T(8,128)(2,1)}), bf16[16,112,360]{2,1,0:T(8,128)(2,1)}, u32[]{:S(2)}, u32[]{:S(2)}) %all-to-all-start.1) | async-done | bytes 1290272 | tf_op jit(solution)/shard_map/all_to_all | solution.py:181
  521.0 3.2 gather_fusion.7
  (54 shorter events, 0.7 us)
Async XLA Ops:
  6.5 316.6 %copy-start = (bf16[512,2880]{0,1:T(8,128)(2,1)S(1)}, bf16[512,2880]{0,1:T(8,128)(2,1)}, u32[]{:S(2)}) copy-start(bf16[512,2880]{0,1:T(8,128)(2,1)} %param.25) | copy-start | bytes 8847364
  17.2 9.7 %copy-start.10 = (s32[256]{0:T(256)S(1)}, s32[256]{0:T(256)}, u32[]{:S(2)}) copy-start(s32[256]{0:T(256)} %param.18) | copy-start | bytes 3076
  17.2 9.8 %copy-start.7 = (bf16[2880]{0:T(1024)(128)(2,1)S(1)}, bf16[2880]{0:T(1024)(128)(2,1)}, u32[]{:S(2)}) copy-start(bf16[2880]{0:T(1024)(128)(2,1)} %param.22) | copy-start | bytes 17284
  17.2 10.7 %copy-start.6 = (s32[16,16]{1,0:T(8,128)S(1)}, s32[16,16]{1,0:T(8,128)}, u32[]{:S(2)}) copy-start(s32[16,16]{1,0:T(8,128)} %param.17) | copy-start | bytes 3076
  17.2 11.8 %copy-start.12 = (s32[64]{0:T(128)S(1)}, s32[64]{0:T(128)}, u32[]{:S(2)}) copy-start(s32[64]{0:T(128)} %param.20) | copy-start | bytes 772
  17.2 201.5 %all-to-all-start = ((bf16[16,112,2880]{2,1,0:T(8,128)(2,1)}), bf16[16,112,2880]{2,1,0:T(8,128)(2,1)}, u32[]{:S(2)}, u32[]{:S(2)}) async-start(bf16[16,112,2880]{2,1,0:T(8,128)(2,1)} %gather_fusion), calls=%async_computation | async-start | bytes 21102592 | tf_op jit(solution)/shard_map/all_to_all | solution.py:147
  25.2 183.2 %all-gather.2.cloned.1.call-start = ((), (), s32[]{:S(2)}) async-start(), calls=%async_computation.3 | async-start | bytes 2228224 | tf_op jit(solution)/shard_map/all_gather | solution.py:89
  25.9 394.7 %all-reduce.2.cloned.1.call-start = ((), (), s32[]{:S(2)}) async-start(), calls=%async_computation.4 | async-start | bytes 8847360 | tf_op jit(solution)/shard_map/psum | solution.py:164
  239.9 3.6 copy-start.1
  272.2 6.4 %copy-start.5 = (f32[768,32]{1,0:T(8,128)S(1)}, f32[768,32]{1,0:T(8,128)}, u32[]{:S(2)}) copy-start(f32[768,32]{1,0:T(8,128)} %get-tuple-element.15) | copy-start | bytes 294916
  284.4 5.7 %copy-start.3 = (bf16[16,128,1,128]{1,3,0,2:T(8,128)(2,1)S(1)}, bf16[16,128,1,128]{1,3,0,2:T(8,128)(2,1)}, u32[]{:S(2)}) copy-start(bf16[16,128,1,128]{1,3,0,2:T(8,128)(2,1)} %broadcast_select_fusion.1) | copy-start | bytes 1572868
  290.1 5.1 copy-start.9
  295.4 5.4 %copy-start.4 = (bf16[16,112,1,128]{1,3,0,2:T(8,128)(2,1)S(1)}, bf16[16,112,1,128]{1,3,0,2:T(8,128)(2,1)}, u32[]{:S(2)}) copy-start(bf16[16,112,1,128]{1,3,0,2:T(8,128)(2,1)} %copy.48) | copy-start | bytes 1376260
  328.9 0.7 copy-start.8
  328.9 151.5 %reduce-scatter.2.cloned.1.call-start = ((), (), s32[]{:S(2)}) async-start(), calls=%async_computation.5 | async-start | bytes 4976640 | tf_op jit(solution)/shard_map/reduce_scatter | solution.py:173
  420.6 7.5 %copy-start.11 = (bf16[2880,360]{0,1:T(8,128)(2,1)S(1)}, bf16[2880,360]{0,1:T(8,128)(2,1)}, u32[]{:S(2)}) copy-start(bf16[2880,360]{0,1:T(8,128)(2,1)} %param.27) | copy-start | bytes 6220804
  426.1 2.0 copy-start.2
  492.6 28.4 %all-to-all-start.1 = ((bf16[16,112,360]{2,1,0:T(8,128)(2,1)}), bf16[16,112,360]{2,1,0:T(8,128)(2,1)}, u32[]{:S(2)}, u32[]{:S(2)}) async-start(bf16[16,112,360]{2,1,0:T(8,128)(2,1)} %broadcast_select_fusion), calls=%async_computation.2 | async-start | bytes 2752512 | tf_op jit(solution)/shard_map/all_to_all | solution.py:181
Sparse Core Ops, SparseCore 0:
  28.1 180.1 all-gather.1
  329.0 91.5 all-reduce.1
  442.9 37.4 reduce-scatter.1
where the time goes:
time: 540 us; the launch traced here: 531 us
  waiting for transfers between devices  326 us (60%)
  local copies, waits for them, and re-layouts  103 us (19%)
  matrix products  40.7 us (8%)
  other arithmetic  33.2 us (6%)
  starting transfers between devices  15 us (3%)
  between operations  13.8 us (3%)
    all_gather x1, waiting for transfers between devices, fetch_prefix(): shard_rows = lax.all_gather(prefix_cache, 'req', axis=0, tiled=True)  176 us
    psum x1, waiting for transfers between devices, local(): lax.psum(partial_value.astype(jnp.bfloat16), 'tp').astype(jnp.float32)  91 us
    reduce_scatter x1, waiting for transfers between devices, local(): lax.psum_scatter(jnp.dot(hidden, w_down, preferred_element_type=jnp.float...  36.8 us
    gather x3, local copies, waits for them, and re-layouts, to_slots(): return values[slot_source].reshape((peers, slot_length) + values.shape[1:])  27.8 us
    gather x2, local copies, waits for them, and re-layouts, local(): input_rows = landed.reshape(peers * slot_length, features)[flat_index]  21.2 us
    all_to_all x1, waiting for transfers between devices, local(): lax.all_to_all(out_slots, 'req', split_axis=0, concat_axis=0, tiled=True)  20.9 us
    dot_general x1, matrix products, local(): jnp.dot(hidden, w_down, preferred_element_type=jnp.float32)  11.4 us
  transfers between devices with their start and end apart: 5, of which 4 were waited for; matrix products, arithmetic and copies ran while one was open for 3% of the time, Pallas kernels for 0%

commit v1 on v0

--- a/solution.py
+++ b/solution.py
@@ -92,6 +92,23 @@
     inside = (tail_store >= 0) & (tail_store < held_blocks)
     picked = flat_rows[jnp.clip(tail_store, 0, held_blocks - 1) * block_len + tail_offset]
     return jnp.where(inside[..., None, None], picked, initial)
+
+
+def norm_groups(parts, gains):
+    widened = parts.astype(jnp.float32)
+    total = jnp.sum(widened * widened, axis=(0, 2), keepdims=True)
+    factor = lax.rsqrt(total / (parts.shape[0] * parts.shape[2]) + EPSILON)
+    return (widened * factor * gains.astype(jnp.float32)).astype(jnp.bfloat16)
+
+
+def group_dot(parts, weight):
+    groups, _, share = parts.shape
+    return jnp.einsum(
+        "gtf,gfo->to",
+        parts,
+        weight.reshape((groups, share) + weight.shape[1:]),
+        preferred_element_type=jnp.float32,
+    )
 
 
 def local(
@@ -144,31 +161,33 @@
         return values[slot_source].reshape((peers, slot_length) + values.shape[1:])
 
     tail_rows = fetch_prefix(arriving_attach, prefix_cache, block_of_slot, WINDOW)
+    my_features = lax.dynamic_slice_in_dim(
+        suffix_tokens, tensor_index * feature_share, feature_share, 2
+    )
     landed = lax.all_to_all(
-        suffix_tokens[send_order], "req", split_axis=0, concat_axis=0, tiled=True
-    )
-    input_rows = landed.reshape(peers * slot_length, features)[flat_index]
-    row_total = input_rows.shape[0]
-    normed_in = norm_rows(input_rows, attn_gain)
-    queries = jnp.dot(normed_in, w_query, preferred_element_type=jnp.float32).reshape(
-        row_total, -1, head_dim
-    )
+        my_features[send_order], "req", split_axis=0, concat_axis=0, tiled=True
+    )
+    input_part = landed.reshape(peers * slot_length, feature_share)[flat_index]
+    input_groups = lax.all_gather(input_part, "tp", axis=0, tiled=False)
+    row_total = input_part.shape[0]
+    normed_in = norm_groups(input_groups, attn_gain.reshape(splits, 1, feature_share))
+    queries = group_dot(normed_in, w_query).reshape(row_total, -1, head_dim)
     queries = rotate(queries, positions).astype(jnp.bfloat16)
-    paired = jnp.dot(
-        normed_in, w_keyval.reshape(features, -1), preferred_element_type=jnp.float32
-    ).reshape(row_total, value_heads, 2 * head_dim)
+    paired = group_dot(normed_in, w_keyval.reshape(features, -1)).reshape(
+        row_total, value_heads, 2 * head_dim
+    )
     rotated = rotate(paired[..., :head_dim], positions)
     paired = jnp.concatenate([rotated, paired[..., head_dim:]], axis=-1).astype(jnp.bfloat16)
     attended = attend(to_slots(queries), to_slots(paired), tail_rows, sink_logits)[flat_index]
     partial_value = jnp.dot(attended, w_out, preferred_element_type=jnp.float32)
-    summed = lax.psum(partial_value.astype(jnp.bfloat16), "tp").astype(jnp.float32)
-    residual = (input_rows.astype(jnp.float32) + summed).astype(jnp.bfloat16)
-    normed_mid = norm_rows(residual, mlp_gain)
-    residual_part = lax.dynamic_slice_in_dim(
-        residual, tensor_index * feature_share, feature_share, 1
-    )
-    gate_proj = jnp.dot(normed_mid, w_gate, preferred_element_type=jnp.float32)
-    up_proj = jnp.dot(normed_mid, w_up, preferred_element_type=jnp.float32)
+    summed = lax.psum_scatter(
+        partial_value.astype(jnp.bfloat16), "tp", scatter_dimension=1, tiled=True
+    ).astype(jnp.float32)
+    residual_part = (input_part.astype(jnp.float32) + summed).astype(jnp.bfloat16)
+    residual_groups = lax.all_gather(residual_part, "tp", axis=0, tiled=False)
+    normed_mid = norm_groups(residual_groups, mlp_gain.reshape(splits, 1, feature_share))
+    gate_proj = group_dot(normed_mid, w_gate)
+    up_proj = group_dot(normed_mid, w_up)
     hidden = (jax.nn.silu(gate_proj) * up_proj).astype(jnp.bfloat16)
     down_sum = lax.psum_scatter(
         jnp.dot(hidden, w_down, preferred_element_type=jnp.float32).astype(jnp.bfloat16),

time: 540 us -> 372 us (0.69)
  waiting for transfers between devices: 326 us -> 169 us
  local copies, waits for them, and re-layouts: 103 us -> 95 us
  matrix products: 40.7 us -> 46.8 us
  other arithmetic: 33.2 us -> 27.8 us
    all_gather x1, waiting for transfers between devices: 176 us -> 8.46 us  [fetch_prefix(): shard_rows = lax.all_gather(prefix_cache, 'req', axis=0, tiled=True)]
    psum x1 -> x0, waiting for transfers between devices: 91 us -> none  [local(): lax.psum(partial_value.astype(jnp.bfloat16), 'tp').astype(jnp.float32)]
    all_gather x0 -> x2, waiting for transfers between devices: none -> 45.4 us  [the longest x1 24.9 us: local(): input_groups = lax.all_gather(input_part, 'tp', axis=0, tiled=False)]
    reduce_scatter x0 -> x1, waiting for transfers between devices: none -> 36.5 us  [local(): lax.psum_scatter(partial_value.astype(jnp.bfloat16), 'tp', scatter_dimens...]
    gather x3, local copies, waits for them, and re-layouts: 30.9 us -> 8.84 us  [the longest x2 5.67 us: local(): input_part = landed.reshape(peers * slot_length, feature_share)[flat_index]]
    all_to_all x1, waiting for transfers between devices: 0.01 us -> 19.8 us  [local(): lax.all_to_all(my_features[send_order], 'req', split_axis=0, concat_axis=...]
    reshape x2 -> x4, local copies, waits for them, and re-layouts: 0.78 us -> 12.3 us  [the longest x2 11.5 us: group_dot(): weight.reshape((groups, share) + weight.shape[1:])]
    gather x3, local copies, waits for them, and re-layouts: 27.8 us -> 16.3 us  [to_slots(): return values[slot_source].reshape((peers, slot_length) + values.shape[1:])]
  transfers between devices with their start and end apart: 5 -> 7, of which waited for: 4 -> 7; matrix products, arithmetic and copies ran while one was open for 3% -> 13% of each run, Pallas kernels for 0% -> 0%
where the time goes in v1:
time: 372 us; the launch traced here: 368 us
  waiting for transfers between devices  169 us (45%)
  local copies, waits for them, and re-layouts  95 us (26%)
  matrix products  46.8 us (13%)
  other arithmetic  27.8 us (7%)
  starting transfers between devices  14.9 us (4%)
  between operations  13.7 us (4%)
    reduce_scatter x1, waiting for transfers between devices, local(): lax.psum_scatter(jnp.dot(hidden, w_down, preferred_element_type=jnp.float...  37.7 us
    reduce_scatter x1, waiting for transfers between devices, local(): lax.psum_scatter(partial_value.astype(jnp.bfloat16), 'tp', scatter_dimens...  36.5 us
    all_gather x1, waiting for transfers between devices, local(): input_groups = lax.all_gather(input_part, 'tp', axis=0, tiled=False)  24.9 us
    all_to_all x1, waiting for transfers between devices, local(): lax.all_to_all(out_slots, 'req', split_axis=0, concat_axis=0, tiled=True)  20.8 us
    all_gather x1, waiting for transfers between devices, local(): residual_groups = lax.all_gather(residual_part, 'tp', axis=0, tiled=False)  20.5 us
    all_to_all x1, waiting for transfers between devices, local(): lax.all_to_all(my_features[send_order], 'req', split_axis=0, concat_axis=...  19.8 us
    gather x3, local copies, waits for them, and re-layouts, to_slots(): return values[slot_source].reshape((peers, slot_length) + values.shape[1:])  16.3 us
    dot_general x3, matrix products, group_dot(): jnp.einsum('gtf,gfo->to', parts, weight.reshape((groups, share) + weight....  16.3 us
  transfers between devices with their start and end apart: 7, of which 7 were waited for; matrix products, arithmetic and copies ran while one was open for 13% of the time, Pallas kernels for 0%

profile of v1, /device:TPU:7, one launch (start us, length us, event | category | flops | bytes accessed | tf_op | source)
XLA Modules:
  0.0 367.6 jit_solution(10374005151619558409)
XLA Ops:
  6.5 0.7 all-gather.6.cloned.1.call-update
  7.3 0.8 fusion.73
  8.1 0.1 select_reduce_fusion.5
  8.3 3.2 constant_dynamic-slice_fusion.1
  11.4 3.2 gather_fusion
  14.6 7.8 %all-to-all-start = ((bf16[16,112,360]{2,1,0:T(8,128)(2,1)}), bf16[16,112,360]{2,1,0:T(8,128)(2,1)}, u32[]{:S(2)}, u32[]{:S(2)}) async-start(bf16[16,112,360]{2,1,0:T(8,128)(2,1)} %gather_fusion), calls=%async_computation | async-start | bytes 2752512 | tf_op jit(solution)/shard_map/all_to_all | solution.py:167
  22.5 0.7 fusion.84
  23.3 0.1 reduce.2
  23.5 0.1 select_reduce_fusion.4
  23.7 0.7 fusion.72
  24.6 19.8 %all-to-all-done = bf16[16,112,360]{2,1,0:T(8,128)(2,1)} async-done(((bf16[16,112,360]{2,1,0:T(8,128)(2,1)}), bf16[16,112,360]{2,1,0:T(8,128)(2,1)}, u32[]{:S(2)}, u32[]{:S(2)}) %all-to-all-start) | async-done | bytes 1290272 | tf_op jit(solution)/shard_map/all_to_all | solution.py:167
  44.4 4.6 %gather_fusion.1 = bf16[768,360]{1,0:T(8,128)(2,1)} fusion(bf16[1792,360]{1,0:T(8,128)(2,1)} %bitcast.8, s32[1024]{0:T(1024)S(1)} %pad_clamp_fusion.2), kind=kCustom, calls=%fused_computation.1 | custom fusion | bytes 1108992 | tf_op jit(solution)/shard_map/gather | solution.py:170
  49.0 0.2 reduce-scatter.3.cloned.1.call-start
  49.4 0.7 bitcast_subtract_fusion.1
  50.2 5.0 %copy.77 = bf16[512,360,8]{1,2,0:T(8,128)(2,1)} copy(bf16[512,360,8]{0,1,2:T(8,128)(2,1)} %bitcast.140) | data formatting | bytes 5898240 | tf_op jit(solution)/shard_map/gtf,gfo->to/dot_general | solution.py:106
  55.5 0.2 select_reduce_fusion
  55.8 1.1 multiply_cosine_fusion
  56.9 8.5 %all-gather.6.cloned.1.call-done = bf16[64,128,1,128]{3,1,2,0:T(8,128)(2,1)} async-done(((bf16[4,128,1,128]{3,1,2,0:T(8,128)(2,1)}), bf16[64,128,1,128]{3,1,2,0:T(8,128)(2,1)}) %all-gather.6.cloned.1.call-update) | async-done | bytes 2097168 | tf_op jit(solution)/shard_map/all_gather | solution.py:89
  65.4 7.5 %gather_fusion.2 = bf16[2048,128]{1,0:T(8,128)(2,1)S(1)} fusion(bf16[8192,128]{1,0:T(8,128)(2,1)} %bitcast.137, s32[2048]{0:T(1024)S(1)} %fusion.63), kind=kCustom, calls=%fused_computation.2 | custom fusion | bytes 1056768 | tf_op jit(solution)/shard_map/gather | solution.py:93
  72.9 1.0 copy.73
  73.9 1.9 broadcast_select_fusion.1
  75.8 24.9 %all-gather.8.cloned.1.call-done = bf16[6144,360]{1,0:T(8,128)(2,1)} async-done(((bf16[768,360]{1,0:T(8,128)(2,1)}), bf16[6144,360]{1,0:T(8,128)(2,1)}) %all-gather.8.cloned.1.call-update) | async-done | bytes 4423696 | tf_op jit(solution)/shard_map/all_gather | solution.py:171
  100.7 7.4 %copy.74 = f32[8,768,360]{1,2,0:T(8,128)} copy(bf16[8,768,360]{2,1,0:T(8,128)(2,1)} %bitcast.134) | data formatting | bytes 13271040 | tf_op jit(solution)/shard_map/convert_element_type | solution.py:98
  108.0 3.5 multiply_reduce_fusion
  111.5 5.0 %convolution_bitcast_fusion = f32[768,1,128]{0,2,1:T(8,128)S(1)} fusion(bf16[8,360,128]{2,1,0:T(8,128)(2,1)S(1)} %bitcast.143, f32[8,768,360]{1,2,0:T(8,128)} %copy.74, f32[8,360]{1,0:T(8,128)S(1)} %reshape.600, f32[768]{0:T(1024)S(1)} %add_rsqrt_fusion.1), kind=kOutput, calls=%fused_computation.41 | convolution fusion | flops 572866560 | bytes 9992448 | tf_op jit(solution)/shard_map/gtf,gfo->to/dot_general | solution.py:106
  116.5 0.4 fusion.54
  117.0 0.2 copy.75
  117.2 4.6 %gather_fusion.3 = bf16[1792,128]{1,0:T(8,128)(2,1)} fusion(bf16[768,128]{1,0:T(8,128)(2,1)S(1)} %copy.75, s32[2048]{0:T(1024)S(1)} %pad_clamp_fusion), kind=kCustom, calls=%fused_computation.3 | custom fusion | bytes 924672 | tf_op jit(solution)/shard_map/gather | solution.py:161
  121.8 2.1 copy.76
  123.9 7.6 %fusion.19 = f32[768,8,64]{0,2,1:T(8,128)S(1)} fusion(bf16[8,64,360,8]{2,3,1,0:T(8,128)(2,1)} %bitcast.139, f32[8,768,360]{1,2,0:T(8,128)} %copy.74, f32[8,360]{1,0:T(8,128)S(1)} %reshape.600, f32[768]{0:T(1024)S(1)} %add_rsqrt_fusion.1), kind=kOutput, calls=%fused_computation.35 | convolution fusion | flops 2271559680 | bytes 13383936 | tf_op jit(solution)/shard_map/gtf,gfo->to/dot_general | solution.py:106
  131.5 0.2 subtract_convert_fusion
  131.7 0.9 pad_maximum_fusion
  132.6 3.0 copy.79
  135.6 5.7 %gather_fusion.4 = bf16[1792,8,64]{2,1,0:T(8,128)(2,1)} fusion(bf16[768,8,64]{2,1,0:T(8,128)(2,1)} %copy.79, s32[2048]{0:T(1024)S(1)} %pad_clamp_fusion), kind=kCustom, calls=%fused_computation.4 | custom fusion | bytes 3677184 | tf_op jit(solution)/shard_map/gather | solution.py:161
  141.4 5.1 %fusion.1 = (f32[16,8,112]{2,1,0:T(8,128)S(1)}, f32[16,240,112,8]{1,2,3,0:T(8,128)S(1)}) fusion(pred[112,240]{1,0:T(8,128)(4,1)S(1)} %fusion.52, bf16[16,112,8,64]{3,2,1,0:T(8,128)(2,1)} %bitcast.136, bf16[16,112,1,128]{1,3,0,2:T(8,128)(2,1)} %copy.76, bf16[16,128,1,128]{1,3,0,2:T(8,128)(2,1)S(1)} %copy-done.5), kind=kOutput, calls=%fused_computation.12 | convolution fusion | flops 451692544 | bytes 16664832 | tf_op jit(solution)/shard_map/ntkgd,nskd->nkgts/dot_general | solution.py:44
  146.6 5.3 %fusion = f32[16,8,112]{2,1,0:T(8,128)S(1)} fusion(f32[16,240,112,8]{1,2,3,0:T(8,128)S(1)} %get-tuple-element.14, f32[16,8,112]{2,1,0:T(8,128)S(1)} %broadcast_maximum_fusion, pred[112,240]{1,0:T(8,128)(4,1)S(1)} %fusion.52), kind=kLoop, calls=%fused_computation.11 | loop fusion | flops 13748224 | bytes 13904128 | tf_op jit(solution)/shard_map/reduce_sum | solution.py:63
  152.0 6.6 %convert_bitcast_fusion = bf16[16,112,1,8,64]{1,4,3,0,2:T(8,128)(2,1)} fusion(f32[16,8,112]{2,1,0:T(8,128)S(1)} %exponential_add_fusion, f32[16,8,112]{2,1,0:T(8,128)S(1)} %broadcast_maximum_fusion, f32[16,240,112,8]{1,2,3,0:T(8,128)S(1)} %get-tuple-element.14, pred[112,240]{1,0:T(8,128)(4,1)S(1)} %fusion.52, bf16[16,128,1,128]{1,3,0,2:T(8,128)(2,1)S(1)} %copy-done.5, ...), kind=kOutput, calls=%fused_computation.34 | convolution fusion | flops 459505664 | bytes 16722176 | tf_op jit(solution)/shard_map/nkgts,nskd->ntkgd/dot_general | solution.py:65
  158.6 4.8 %copy.90 = bf16[16,112,1,8,64]{4,3,1,0,2:T(8,128)(2,1)} copy(bf16[16,112,1,8,64]{1,4,3,0,2:T(8,128)(2,1)} %convert_bitcast_fusion) | data formatting | bytes 3670016 | tf_op jit(solution)/shard_map/reshape | solution.py:71
  163.4 5.9 %reshape.685 = bf16[1792,512]{1,0:T(8,128)(2,1)} reshape(bf16[16,112,1,8,64]{4,3,1,0,2:T(8,128)(2,1)} %copy.90) | data formatting | bytes 3670016 | tf_op jit(solution)/shard_map/reshape | solution.py:71
  169.3 5.1 %gather_fusion.5 = bf16[768,512]{1,0:T(8,128)(2,1)} fusion(bf16[1792,512]{1,0:T(8,128)(2,1)} %reshape.685, s32[1024]{0:T(1024)S(1)} %pad_clamp_fusion.2), kind=kCustom, calls=%fused_computation.5 | custom fusion | bytes 1575936 | tf_op jit(solution)/shard_map/gather | solution.py:181
  174.4 5.6 %convolution_convert_fusion = bf16[768,2880]{0,1:T(8,128)(2,1)} fusion(bf16[768,512]{1,0:T(8,128)(2,1)} %gather_fusion.5, bf16[512,2880]{0,1:T(8,128)(2,1)S(1)} %copy-done), kind=kOutput, calls=%fused_computation.23 | convolution fusion | flops 2267136000 | bytes 8159232 | tf_op jit(solution)/shard_map/dot_general | solution.py:182
  180.1 1.0 copy-done.2
  181.1 1.1 copy.72
  182.2 36.5 %reduce-scatter.3.cloned.1.call-done = bf16[768,360]{0,1:T(8,128)(2,1)} async-done(((bf16[768,2880]{0,1:T(8,128)(2,1)}), bf16[768,360]{0,1:T(8,128)(2,1)}) %reduce-scatter.3.cloned.1.call-update) | async-done | bytes 552976 | tf_op jit(solution)/shard_map/reduce_scatter | solution.py:183
  218.6 2.2 add_convert_fusion.1
  221.0 5.6 %reshape.597 = bf16[8,360,360]{1,0,2:T(8,128)(2,1)} reshape(bf16[2880,360]{0,1:T(8,128)(2,1)} %param.27) | data formatting | bytes 4147200 | tf_op jit(solution)/shard_map/reshape | solution.py:109
  226.6 5.9 %reshape.598 = bf16[8,360,360]{1,0,2:T(8,128)(2,1)} reshape(bf16[2880,360]{0,1:T(8,128)(2,1)} %param.28) | data formatting | bytes 4147200 | tf_op jit(solution)/shard_map/reshape | solution.py:109
  232.5 20.5 %all-gather.10.cloned.1.call-done = bf16[6144,360]{0,1:T(8,128)(2,1)} async-done(((bf16[768,360]{0,1:T(8,128)(2,1)}), bf16[6144,360]{0,1:T(8,128)(2,1)}) %all-gather.10.cloned.1.call-update) | async-done | bytes 4423696 | tf_op jit(solution)/shard_map/all_gather | solution.py:187
  253.0 3.3 convert_element_type.133
  256.3 4.0 %copy.93 = f32[45,8,8,768]{3,2,1,0:T(8,128)S(1)} copy(f32[45,8,8,768]{3,1,2,0:T(8,128)S(1)} %bitcast.131) | data formatting | bytes 17694720
  260.4 0.6 fusion.2
  261.0 1.0 copy-done.4
  262.0 3.7 %fusion.24 = f32[768,360]{0,1:T(8,128)} fusion(bf16[8,360,360]{1,0,2:T(8,128)(2,1)S(1)} %copy-done.4, f32[45,8,8,768]{3,2,1,0:T(8,128)S(1)} %bitcast.132, f32[8,360]{1,0:T(8,128)S(1)} %reshape.601, f32[768]{0:T(1024)S(1)} %add_rsqrt_fusion), kind=kOutput, calls=%fused_computation.36 | convolution fusion | flops 1599160320 | bytes 12041472 | tf_op jit(solution)/shard_map/gtf,gfo->to/dot_general | solution.py:106
  265.7 13.1 %convolution_convert_fusion.1 = bf16[768,2880]{0,1:T(8,128)(2,1)} fusion(bf16[360,2880]{1,0:T(8,128)(2,1)} %param.29, bf16[8,360,360]{1,0,2:T(8,128)(2,1)} %reshape.598, f32[768,360]{0,1:T(8,128)} %fusion.24, f32[45,8,8,768]{3,2,1,0:T(8,128)} %bitcast.133, f32[8,360]{1,0:T(8,128)S(1)} %reshape.601, f32[768]{0:T(1024)S(1)} %add_rsqrt_fusion), kind=kOutput, calls=%fused_computation.24 | convolution fusion | flops 3195555840 | bytes 18538752 | tf_op jit(solution)/shard_map/dot_general | solution.py:193
  278.9 0.8 fusion.83
  279.7 37.7 %reduce-scatter.5.cloned.1.call-done = bf16[768,360]{0,1:T(8,128)(2,1)} async-done(((bf16[768,2880]{0,1:T(8,128)(2,1)}), bf16[768,360]{0,1:T(8,128)(2,1)}) %reduce-scatter.5.cloned.1.call-update) | async-done | bytes 552976 | tf_op jit(solution)/shard_map/reduce_scatter | solution.py:192
  317.4 2.0 add_convert_fusion
  319.4 1.4 copy.86
  320.8 6.0 %gather_fusion.6 = bf16[1792,360]{1,0:T(8,128)(2,1)} fusion(bf16[768,360]{1,0:T(8,128)(2,1)S(1)} %copy.86, s32[2048]{0:T(1024)S(1)} %pad_clamp_fusion), kind=kCustom, calls=%fused_computation.6 | custom fusion | bytes 2587648 | tf_op jit(solution)/shard_map/gather | solution.py:161
  326.8 2.7 broadcast_select_fusion
  329.5 6.7 %all-to-all-start.1 = ((bf16[16,112,360]{2,1,0:T(8,128)(2,1)}), bf16[16,112,360]{2,1,0:T(8,128)(2,1)}, u32[]{:S(2)}, u32[]{:S(2)}) async-start(bf16[16,112,360]{2,1,0:T(8,128)(2,1)} %broadcast_select_fusion), calls=%async_computation.3 | async-start | bytes 2752512 | tf_op jit(solution)/shard_map/all_to_all | solution.py:200
  336.2 0.7 fusion.71
  336.9 20.8 %all-to-all-done.1 = bf16[16,112,360]{2,1,0:T(8,128)(2,1)} async-done(((bf16[16,112,360]{2,1,0:T(8,128)(2,1)}), bf16[16,112,360]{2,1,0:T(8,128)(2,1)}, u32[]{:S(2)}, u32[]{:S(2)}) %all-to-all-start.1) | async-done | bytes 1290272 | tf_op jit(solution)/shard_map/all_to_all | solution.py:200
  357.8 3.2 gather_fusion.7
  (72 shorter events, 1.7 us)
Async XLA Ops:
  6.5 167.9 %copy-start = (bf16[512,2880]{0,1:T(8,128)(2,1)S(1)}, bf16[512,2880]{0,1:T(8,128)(2,1)}, u32[]{:S(2)}) copy-start(bf16[512,2880]{0,1:T(8,128)(2,1)} %param.25) | copy-start | bytes 8847364
  6.5 58.9 %all-gather.6.cloned.1.call-start = ((), (), s32[]{:S(2)}) async-start(), calls=%async_computation.4 | async-start | bytes 2228224 | tf_op jit(solution)/shard_map/all_gather | solution.py:89
  8.2 15.2 %copy-start.14 = (s32[256]{0:T(256)S(1)}, s32[256]{0:T(256)}, u32[]{:S(2)}) copy-start(s32[256]{0:T(256)} %param.18) | copy-start | bytes 3076
  8.3 15.3 %copy-start.10 = (s32[16,16]{1,0:T(8,128)S(1)}, s32[16,16]{1,0:T(8,128)}, u32[]{:S(2)}) copy-start(s32[16,16]{1,0:T(8,128)} %param.17) | copy-start | bytes 3076
  14.6 29.8 %all-to-all-start = ((bf16[16,112,360]{2,1,0:T(8,128)(2,1)}), bf16[16,112,360]{2,1,0:T(8,128)(2,1)}, u32[]{:S(2)}, u32[]{:S(2)}) async-start(bf16[16,112,360]{2,1,0:T(8,128)(2,1)} %gather_fusion), calls=%async_computation | async-start | bytes 2752512 | tf_op jit(solution)/shard_map/all_to_all | solution.py:167
  22.4 26.8 %copy-start.11 = (bf16[2880]{0:T(1024)(128)(2,1)S(1)}, bf16[2880]{0:T(1024)(128)(2,1)}, u32[]{:S(2)}) copy-start(bf16[2880]{0:T(1024)(128)(2,1)} %param.22) | copy-start | bytes 17284
  22.4 78.2 %all-gather.8.cloned.1.call-start = ((), (), s32[]{:S(2)}) async-start(), calls=%async_computation.7 | async-start | bytes 5308416 | tf_op jit(solution)/shard_map/all_gather | solution.py:171
  49.0 6.3 %copy-start.15 = (s32[64]{0:T(128)S(1)}, s32[64]{0:T(128)}, u32[]{:S(2)}) copy-start(s32[64]{0:T(128)} %param.20) | copy-start | bytes 772
  49.0 169.6 %reduce-scatter.3.cloned.1.call-start = ((), (), s32[]{:S(2)}) async-start(), calls=%async_computation.5 | async-start | bytes 4976640 | tf_op jit(solution)/shard_map/reduce_scatter | solution.py:183
  108.0 3.5 copy-start.7
  123.9 7.6 %copy-start.8 = (f32[768,32]{0,1:T(8,128)S(1)}, f32[768,32]{0,1:T(8,128)}, u32[]{:S(2)}) copy-start(f32[768,32]{0,1:T(8,128)} %get-tuple-element.11) | copy-start | bytes 294916
  123.9 7.6 %copy-start.9 = (f32[768,32]{0,1:T(8,128)S(1)}, f32[768,32]{0,1:T(8,128)}, u32[]{:S(2)}) copy-start(f32[768,32]{0,1:T(8,128)} %get-tuple-element.12) | copy-start | bytes 294916
  135.6 5.7 %copy-start.5 = (bf16[16,128,1,128]{1,3,0,2:T(8,128)(2,1)S(1)}, bf16[16,128,1,128]{1,3,0,2:T(8,128)(2,1)}, u32[]{:S(2)}) copy-start(bf16[16,128,1,128]{1,3,0,2:T(8,128)(2,1)} %broadcast_select_fusion.1) | copy-start | bytes 1572868
  141.4 5.1 %copy-start.13 = (f32[8]{0:T(128)S(1)}, f32[8]{0:T(128)}, u32[]{:S(2)}) copy-start(f32[8]{0:T(128)} %param.21) | copy-start | bytes 100
  146.6 5.4 %copy-start.6 = (bf16[16,112,1,128]{1,3,0,2:T(8,128)(2,1)S(1)}, bf16[16,112,1,128]{1,3,0,2:T(8,128)(2,1)}, u32[]{:S(2)}) copy-start(bf16[16,112,1,128]{1,3,0,2:T(8,128)(2,1)} %copy.76) | copy-start | bytes 1376260
  180.0 1.1 copy-start.2
  180.0 40.9 %copy-start.12 = (bf16[2880]{0:T(1024)(128)(2,1)S(1)}, bf16[2880]{0:T(1024)(128)(2,1)}, u32[]{:S(2)}) copy-start(bf16[2880]{0:T(1024)(128)(2,1)} %param.26) | copy-start | bytes 17284
  180.1 72.9 %all-gather.10.cloned.1.call-start = ((), (), s32[]{:S(2)}) async-start(), calls=%async_computation.8 | async-start | bytes 4976640 | tf_op jit(solution)/shard_map/all_gather | solution.py:187
  220.9 96.6 %reduce-scatter.5.cloned.1.call-start = ((), (), s32[]{:S(2)}) async-start(), calls=%async_computation.6 | async-start | bytes 4976640 | tf_op jit(solution)/shard_map/reduce_scatter | solution.py:192
  256.3 4.7 %copy-start.1 = (f32[6144,360]{0,1:T(8,128)}, f32[6144,360]{0,1:T(8,128)S(1)}, u32[]{:S(2)}) copy-start(f32[6144,360]{0,1:T(8,128)S(1)} %convert_element_type.133) | copy-start | bytes 26542084
  260.4 1.6 copy-start.4
  278.8 38.6 %copy-start.3 = (bf16[768,360]{0,1:T(8,128)(2,1)S(1)}, bf16[768,360]{0,1:T(8,128)(2,1)}, u32[]{:S(2)}) copy-start(bf16[768,360]{0,1:T(8,128)(2,1)} %add_convert_fusion.1) | copy-start | bytes 1658884
  329.5 28.3 %all-to-all-start.1 = ((bf16[16,112,360]{2,1,0:T(8,128)(2,1)}), bf16[16,112,360]{2,1,0:T(8,128)(2,1)}, u32[]{:S(2)}, u32[]{:S(2)}) async-start(bf16[16,112,360]{2,1,0:T(8,128)(2,1)} %broadcast_select_fusion), calls=%async_computation.3 | async-start | bytes 2752512 | tf_op jit(solution)/shard_map/all_to_all | solution.py:200
Sparse Core Ops, SparseCore 0:
  9.5 55.8 all-gather.5
  67.1 33.5 all-gather.7
  180.2 38.4 reduce-scatter.2
  221.0 31.9 all-gather.9
  279.0 38.4 reduce-scatter.4

commit v2 on v1

--- a/solution.py
+++ b/solution.py
@@ -2,6 +2,8 @@
 import jax.numpy as jnp
 from jax import lax
 from jax.sharding import PartitionSpec as P
+from jax.experimental import pallas as pl
+from jax.experimental.pallas import tpu as pltpu
 
 WINDOW = 128
 CAP = 768
@@ -71,6 +73,83 @@
     return mixed.astype(jnp.bfloat16).reshape(
         peers * slot_length, value_heads * group_size * head_dim
     )
+
+
+def attend_kernel(sink_ref, q_ref, kv_ref, tail_ref, o_ref):
+    slot_length = q_ref.shape[1]
+    window = tail_ref.shape[1]
+    head_dim = kv_ref.shape[2] // 2
+    heads = q_ref.shape[2] // head_dim
+    scale = head_dim ** (-0.5)
+    kv = kv_ref[0]
+    tail = tail_ref[0]
+    own_keys, own_values = kv[:, :head_dim], kv[:, head_dim:]
+    tail_keys, tail_values = tail[:, :head_dim], tail[:, head_dim:]
+    step = lax.broadcasted_iota(jnp.int32, (slot_length, window), 0)
+    column = lax.broadcasted_iota(jnp.int32, (slot_length, window), 1)
+    tail_allowed = column > step
+    own_step = lax.broadcasted_iota(jnp.int32, (slot_length, slot_length), 0)
+    own_column = lax.broadcasted_iota(jnp.int32, (slot_length, slot_length), 1)
+    own_allowed = own_column <= own_step
+    contract = (((1,), (1,)), ((), ()))
+    for head in range(heads):
+        query = q_ref[0, :, head * head_dim:(head + 1) * head_dim]
+        tail_scores = lax.dot_general(
+            query, tail_keys, contract, preferred_element_type=jnp.float32
+        ) * scale
+        own_scores = lax.dot_general(
+            query, own_keys, contract, preferred_element_type=jnp.float32
+        ) * scale
+        tail_scores = jnp.where(tail_allowed, tail_scores, -jnp.inf)
+        own_scores = jnp.where(own_allowed, own_scores, -jnp.inf)
+        sink = sink_ref[head]
+        largest = jnp.maximum(
+            jnp.maximum(
+                jnp.max(tail_scores, axis=1, keepdims=True),
+                jnp.max(own_scores, axis=1, keepdims=True),
+            ),
+            sink,
+        )
+        tail_weights = jnp.exp(tail_scores - largest)
+        own_weights = jnp.exp(own_scores - largest)
+        normalizer = (
+            jnp.sum(tail_weights, axis=1, keepdims=True)
+            + jnp.sum(own_weights, axis=1, keepdims=True)
+            + jnp.exp(sink - largest)
+        )
+        tail_weights = (tail_weights / normalizer).astype(jnp.bfloat16)
+        own_weights = (own_weights / normalizer).astype(jnp.bfloat16)
+        mixed = jnp.dot(
+            tail_weights, tail_values, preferred_element_type=jnp.float32
+        ) + jnp.dot(own_weights, own_values, preferred_element_type=jnp.float32)
+        o_ref[0, :, head * head_dim:(head + 1) * head_dim] = mixed.astype(o_ref.dtype)
+
+
+def attend_pallas(query_slots, paired_slots, tail_rows, sink_logits):
+    peers, slot_length, width = query_slots.shape
+    window = tail_rows.shape[1]
+    pair_width = paired_slots.shape[2]
+    head_dim = pair_width // 2
+    heads = width // head_dim
+    flops = peers * heads * 4 * slot_length * (window + slot_length) * head_dim
+    moved = 2 * (2 * query_slots.size + paired_slots.size + tail_rows.size)
+    return pl.pallas_call(
+        attend_kernel,
+        grid=(peers,),
+        in_specs=[
+            pl.BlockSpec(memory_space=pltpu.SMEM),
+            pl.BlockSpec((1, slot_length, width), lambda n: (n, 0, 0)),
+            pl.BlockSpec((1, slot_length, pair_width), lambda n: (n, 0, 0)),
+            pl.BlockSpec((1, window, pair_width), lambda n: (n, 0, 0)),
+        ],
+        out_specs=pl.BlockSpec((1, slot_length, width), lambda n: (n, 0, 0)),
+        out_shape=jax.ShapeDtypeStruct((peers, slot_length, width), jnp.bfloat16),
+        cost_estimate=pl.CostEstimate(
+            flops=flops,
+            transcendentals=peers * heads * slot_length * (window + slot_length),
+            bytes_accessed=moved,
+        ),
+    )(sink_logits.astype(jnp.float32), query_slots, paired_slots, tail_rows)
 
 
 def fetch_prefix(attach_slots, prefix_cache, block_of_slot, window):
@@ -178,7 +257,12 @@
     )
     rotated = rotate(paired[..., :head_dim], positions)
     paired = jnp.concatenate([rotated, paired[..., head_dim:]], axis=-1).astype(jnp.bfloat16)
-    attended = attend(to_slots(queries), to_slots(paired), tail_rows, sink_logits)[flat_index]
+    attended = attend_pallas(
+        to_slots(queries.reshape(row_total, -1)),
+        to_slots(paired.reshape(row_total, -1)),
+        tail_rows.reshape(peers, WINDOW, -1),
+        sink_logits,
+    ).reshape(peers * slot_length, -1)[flat_index]
     partial_value = jnp.dot(attended, w_out, preferred_element_type=jnp.float32)
     summed = lax.psum_scatter(
         partial_value.astype(jnp.bfloat16), "tp", scatter_dimension=1, tiled=True

time: 372 us -> 366 us (0.984)
  Pallas kernels: 0 us -> 28.7 us
  local copies, waits for them, and re-layouts: 95 us -> 79.3 us
  matrix products: 46.8 us -> 34.4 us
  other arithmetic: 27.8 us -> 20.1 us
  waiting for transfers between devices: 169 us -> 174 us
    pallas_call x0 -> x1, Pallas kernels: none -> 28.7 us  [attend_pallas(): pl.pallas_call(attend_kernel, grid=(peers,), in_specs=[pl.BlockSpec(memor...]
    reshape x5 -> x2, local copies, waits for them, and re-layouts: 13.6 us -> 0.79 us  [the longest x2 10.7 us: attend(): mixed.astype(jnp.bfloat16)]
    dot_general x2 -> x0, matrix products: 11.8 us -> none  [the longest x1 6.63 us: attend(): jnp.einsum('nkgts,nskd->ntkgd', near_weights, near_keys[..., head_dim:],...]
    reduce_sum x1 -> x0, other arithmetic: 5.26 us -> none  [attend(): jnp.sum(near_weights, axis=-1, keepdims=True)]
    gather x2 -> x1, local copies, waits for them, and re-layouts: 8.47 us -> 7.46 us  [fetch_prefix(): flat_rows[jnp.clip(tail_store, 0, held_blocks - 1) * block_len + tail_off...]
  transfers between devices with their start and end apart: 7 -> 7, of which waited for: 7 -> 7; matrix products, arithmetic and copies ran while one was open for 13% -> 11% of each run, Pallas kernels for 0% -> 0%
where the time goes in v2:
time: 366 us; the launch traced here: 365 us
  waiting for transfers between devices  174 us (48%)
  local copies, waits for them, and re-layouts  79.3 us (22%)
  matrix products  34.4 us (9%)
  Pallas kernels  28.7 us (8%)
  other arithmetic  20.1 us (5%)
  starting transfers between devices  14.9 us (4%)
  between operations  13.5 us (4%)
    reduce_scatter x1, waiting for transfers between devices, local(): lax.psum_scatter(jnp.dot(hidden, w_down, preferred_element_type=jnp.float...  37.8 us
    reduce_scatter x1, waiting for transfers between devices, local(): lax.psum_scatter(partial_value.astype(jnp.bfloat16), 'tp', scatter_dimens...  37.3 us
    pallas_call x1, Pallas kernels, attend_pallas(): pl.pallas_call(attend_kernel, grid=(peers,), in_specs=[pl.BlockSpec(memor...  28.7 us
    all_gather x1, waiting for transfers between devices, local(): input_groups = lax.all_gather(input_part, 'tp', axis=0, tiled=False)  26.6 us
    all_gather x1, waiting for transfers between devices, local(): residual_groups = lax.all_gather(residual_part, 'tp', axis=0, tiled=False)  21.7 us
    all_to_all x1, waiting for transfers between devices, local(): lax.all_to_all(out_slots, 'req', split_axis=0, concat_axis=0, tiled=True)  21.5 us
    all_to_all x1, waiting for transfers between devices, local(): lax.all_to_all(my_features[send_order], 'req', split_axis=0, concat_axis=...  19.8 us
    gather x3, local copies, waits for them, and re-layouts, to_slots(): return values[slot_source].reshape((peers, slot_length) + values.shape[1:])  18 us
  transfers between devices with their start and end apart: 7, of which 7 were waited for; matrix products, arithmetic and copies ran while one was open for 11% of the time, Pallas kernels for 0%

profile of v2, /device:TPU:7, one launch (start us, length us, event | category | flops | bytes accessed | tf_op | source)
XLA Modules:
  0.0 364.9 jit_solution(11816630610966928794)
XLA Ops:
  6.5 0.7 all-gather.6.cloned.1.call-update
  7.3 0.8 fusion.60
  8.1 0.1 select_reduce_fusion.5
  8.2 3.2 constant_dynamic-slice_fusion.1
  11.4 3.2 gather_fusion
  14.6 7.8 %all-to-all-start = ((bf16[16,112,360]{2,1,0:T(8,128)(2,1)}), bf16[16,112,360]{2,1,0:T(8,128)(2,1)}, u32[]{:S(2)}, u32[]{:S(2)}) async-start(bf16[16,112,360]{2,1,0:T(8,128)(2,1)} %gather_fusion), calls=%async_computation | async-start | bytes 2752512 | tf_op jit(solution)/shard_map/all_to_all | solution.py:246
  22.5 0.7 fusion.67
  23.3 0.1 reduce
  23.5 0.1 select_reduce_fusion.4
  23.6 0.1 convert_reduce_fusion
  23.7 0.7 fusion.59
  24.4 0.1 select_reduce_fusion.1
  24.6 19.8 %all-to-all-done = bf16[16,112,360]{2,1,0:T(8,128)(2,1)} async-done(((bf16[16,112,360]{2,1,0:T(8,128)(2,1)}), bf16[16,112,360]{2,1,0:T(8,128)(2,1)}, u32[]{:S(2)}, u32[]{:S(2)}) %all-to-all-start) | async-done | bytes 1290272 | tf_op jit(solution)/shard_map/all_to_all | solution.py:246
  44.4 4.6 %gather_fusion.1 = bf16[768,360]{1,0:T(8,128)(2,1)} fusion(bf16[1792,360]{1,0:T(8,128)(2,1)} %bitcast.8, s32[1024]{0:T(1024)S(1)} %pad_clamp_fusion.2), kind=kCustom, calls=%fused_computation.1 | custom fusion | bytes 1108992 | tf_op jit(solution)/shard_map/gather | solution.py:249
  49.0 0.2 reduce-scatter.3.cloned.1.call-start
  49.3 0.1 reshape.523
  49.4 0.7 bitcast_subtract_fusion.1
  50.1 0.1 min.20
  50.2 5.0 %copy.59 = bf16[512,360,8]{1,2,0:T(8,128)(2,1)} copy(bf16[512,360,8]{0,1,2:T(8,128)(2,1)} %bitcast.105) | data formatting | bytes 5898240 | tf_op jit(solution)/shard_map/gtf,gfo->to/dot_general | solution.py:185
  55.3 0.1 select_reduce_fusion.3
  55.5 0.2 select_reduce_fusion
  55.7 0.1 fusion.50
  55.8 1.1 multiply_cosine_fusion.1
  56.9 8.5 %all-gather.6.cloned.1.call-done = bf16[64,128,1,128]{3,1,2,0:T(8,128)(2,1)} async-done(((bf16[4,128,1,128]{3,1,2,0:T(8,128)(2,1)}), bf16[64,128,1,128]{3,1,2,0:T(8,128)(2,1)}) %all-gather.6.cloned.1.call-update) | async-done | bytes 2097168 | tf_op jit(solution)/shard_map/all_gather | solution.py:168
  65.4 7.5 %gather_fusion.4 = bf16[2048,128]{1,0:T(8,128)(2,1)S(1)} fusion(bf16[8192,128]{1,0:T(8,128)(2,1)} %bitcast.101, s32[2048]{0:T(1024)S(1)} %fusion.50), kind=kCustom, calls=%fused_computation.4 | custom fusion | bytes 1056768 | tf_op jit(solution)/shard_map/gather | solution.py:172
  72.9 1.2 broadcast_select_fusion.1.tail_ref
  74.0 26.6 %all-gather.8.cloned.1.call-done = bf16[6144,360]{1,0:T(8,128)(2,1)} async-done(((bf16[768,360]{1,0:T(8,128)(2,1)}), bf16[6144,360]{1,0:T(8,128)(2,1)}) %all-gather.8.cloned.1.call-update) | async-done | bytes 4423696 | tf_op jit(solution)/shard_map/all_gather | solution.py:250
  100.7 7.4 %copy.58 = f32[8,768,360]{1,2,0:T(8,128)} copy(bf16[8,768,360]{2,1,0:T(8,128)(2,1)} %bitcast.99) | data formatting | bytes 13271040 | tf_op jit(solution)/shard_map/convert_element_type | solution.py:177
  108.0 3.5 multiply_reduce_fusion
  111.5 4.9 %convolution_bitcast_fusion = f32[768,1,128]{0,2,1:T(8,128)S(1)} fusion(bf16[8,360,128]{2,1,0:T(8,128)(2,1)S(1)} %bitcast.108, f32[8,768,360]{1,2,0:T(8,128)} %copy.58, f32[8,360]{1,0:T(8,128)S(1)} %reshape.523, f32[768]{0:T(1024)S(1)} %add_rsqrt_fusion.1), kind=kOutput, calls=%fused_computation.30 | convolution fusion | flops 572866560 | bytes 9992448 | tf_op jit(solution)/shard_map/gtf,gfo->to/dot_general | solution.py:185
  116.5 0.4 fusion.43
  117.0 0.2 copy.62
  117.2 7.6 %fusion.10 = f32[768,8,64]{0,2,1:T(8,128)S(1)} fusion(bf16[8,64,360,8]{2,3,1,0:T(8,128)(2,1)} %bitcast.103, f32[8,768,360]{1,2,0:T(8,128)} %copy.58, f32[8,360]{1,0:T(8,128)S(1)} %reshape.523, f32[768]{0:T(1024)S(1)} %add_rsqrt_fusion.1), kind=kOutput, calls=%fused_computation.24 | convolution fusion | flops 2271559680 | bytes 13383936 | tf_op jit(solution)/shard_map/gtf,gfo->to/dot_general | solution.py:185
  124.7 0.2 subtract_convert_fusion
  125.0 0.9 pad_maximum_fusion
  125.9 2.3 copy.61
  128.2 4.6 %gather_fusion.3 = bf16[1792,128]{1,0:T(8,128)(2,1)} fusion(bf16[768,128]{1,0:T(8,128)(2,1)S(1)} %copy.62, s32[2048]{0:T(1024)S(1)} %pad_clamp_fusion), kind=kCustom, calls=%fused_computation.3 | custom fusion | bytes 924672 | tf_op jit(solution)/shard_map/gather | solution.py:240
  132.8 7.4 %gather_fusion.2 = bf16[1792,512]{1,0:T(8,128)(2,1)} fusion(bf16[768,512]{1,0:T(8,128)(2,1)} %copy.61, s32[2048]{0:T(1024)S(1)} %pad_clamp_fusion), kind=kCustom, calls=%fused_computation.2 | custom fusion | bytes 3677184 | tf_op jit(solution)/shard_map/gather | solution.py:240
  140.2 28.7 %shard_map.145 = bf16[16,112,512]{2,1,0:T(8,128)(2,1)} custom-call(f32[8]{0:T(128)} %sink_ref.1, bf16[16,112,512]{2,1,0:T(8,128)(2,1)} %bitcast.107, bf16[16,112,128]{2,1,0:T(8,128)(2,1)} %bitcast.109, bf16[16,128,128]{2,1,0:T(8,128)(2,1)} %broadcast_select_fusion.1.tail_ref), custom_call_target="tpu_custom_call" | custom-call | flops 880803840 | bytes 4653056 | tf_op jit(solution)/shard_map/pallas_call | solution.py:136
  168.9 5.3 %gather_fusion.5 = bf16[768,512]{1,0:T(8,128)(2,1)} fusion(bf16[1792,512]{1,0:T(8,128)(2,1)} %bitcast.98, s32[1024]{0:T(1024)S(1)} %pad_clamp_fusion.2), kind=kCustom, calls=%fused_computation.5 | custom fusion | bytes 1575936 | tf_op jit(solution)/shard_map/gather | solution.py:260
  174.2 5.6 %convolution_convert_fusion = bf16[768,2880]{0,1:T(8,128)(2,1)} fusion(bf16[768,512]{1,0:T(8,128)(2,1)} %gather_fusion.5, bf16[512,2880]{0,1:T(8,128)(2,1)S(1)} %copy-done), kind=kOutput, calls=%fused_computation.15 | convolution fusion | flops 2267136000 | bytes 8159232 | tf_op jit(solution)/shard_map/dot_general | solution.py:266
  180.0 1.0 copy-done.3
  180.9 0.2 copy.57
  181.2 37.3 %reduce-scatter.3.cloned.1.call-done = bf16[768,360]{0,1:T(8,128)(2,1)} async-done(((bf16[768,2880]{0,1:T(8,128)(2,1)}), bf16[768,360]{0,1:T(8,128)(2,1)}) %reduce-scatter.3.cloned.1.call-update) | async-done | bytes 552976 | tf_op jit(solution)/shard_map/reduce_scatter | solution.py:267
  218.5 2.0 add_convert_fusion.1
  220.6 0.1 reshape.524
  220.7 5.6 %reshape.520 = bf16[8,360,360]{1,0,2:T(8,128)(2,1)} reshape(bf16[2880,360]{0,1:T(8,128)(2,1)} %param.27) | data formatting | bytes 4147200 | tf_op jit(solution)/shard_map/reshape | solution.py:188
  226.3 4.7 %reshape.521 = bf16[8,360,360]{1,0,2:T(8,128)(2,1)S(1)} reshape(bf16[2880,360]{0,1:T(8,128)(2,1)} %param.28) | data formatting | bytes 4147200 | tf_op jit(solution)/shard_map/reshape | solution.py:188
  231.0 21.7 %all-gather.10.cloned.1.call-done = bf16[6144,360]{0,1:T(8,128)(2,1)} async-done(((bf16[768,360]{0,1:T(8,128)(2,1)}), bf16[6144,360]{0,1:T(8,128)(2,1)}) %all-gather.10.cloned.1.call-update) | async-done | bytes 4423696 | tf_op jit(solution)/shard_map/all_gather | solution.py:271
  252.7 3.3 convert_element_type.117
  256.0 4.0 %copy.69 = f32[45,8,8,768]{3,2,1,0:T(8,128)S(1)} copy(f32[45,8,8,768]{3,1,2,0:T(8,128)S(1)} %bitcast.95) | data formatting | bytes 17694720
  260.1 0.6 fusion
  260.7 1.0 copy-done.5
  261.7 3.7 %fusion.15 = f32[768,360]{0,1:T(8,128)} fusion(bf16[8,360,360]{1,0,2:T(8,128)(2,1)S(1)} %copy-done.5, f32[45,8,8,768]{3,2,1,0:T(8,128)S(1)} %bitcast.96, f32[8,360]{1,0:T(8,128)S(1)} %reshape.524, f32[768]{0:T(1024)S(1)} %add_rsqrt_fusion), kind=kOutput, calls=%fused_computation.25 | convolution fusion | flops 1599160320 | bytes 12041472 | tf_op jit(solution)/shard_map/gtf,gfo->to/dot_general | solution.py:185
  265.4 12.6 %convolution_convert_fusion.1 = bf16[768,2880]{0,1:T(8,128)(2,1)} fusion(bf16[360,2880]{1,0:T(8,128)(2,1)} %param.29, bf16[8,360,360]{1,0,2:T(8,128)(2,1)S(1)} %reshape.521, f32[768,360]{0,1:T(8,128)} %fusion.15, f32[45,8,8,768]{3,2,1,0:T(8,128)} %bitcast.97, f32[8,360]{1,0:T(8,128)S(1)} %reshape.524, f32[768]{0:T(1024)S(1)} %add_rsqrt_fusion), kind=kOutput, calls=%fused_computation.16 | convolution fusion | flops 3195555840 | bytes 18538752 | tf_op jit(solution)/shard_map/dot_general | solution.py:277
  278.0 0.8 fusion.66
  278.8 37.8 %reduce-scatter.5.cloned.1.call-done = bf16[768,360]{0,1:T(8,128)(2,1)} async-done(((bf16[768,2880]{0,1:T(8,128)(2,1)}), bf16[768,360]{0,1:T(8,128)(2,1)}) %reduce-scatter.5.cloned.1.call-update) | async-done | bytes 552976 | tf_op jit(solution)/shard_map/reduce_scatter | solution.py:276
  316.6 1.2 add_convert_fusion
  317.8 0.3 copy.66
  318.1 6.0 %gather_fusion.6 = bf16[1792,360]{1,0:T(8,128)(2,1)} fusion(bf16[768,360]{1,0:T(8,128)(2,1)S(1)} %copy.66, s32[2048]{0:T(1024)S(1)} %pad_clamp_fusion), kind=kCustom, calls=%fused_computation.6 | custom fusion | bytes 2587648 | tf_op jit(solution)/shard_map/gather | solution.py:240
  324.1 2.9 broadcast_select_fusion
  327.0 6.7 %all-to-all-start.1 = ((bf16[16,112,360]{2,1,0:T(8,128)(2,1)}), bf16[16,112,360]{2,1,0:T(8,128)(2,1)}, u32[]{:S(2)}, u32[]{:S(2)}) async-start(bf16[16,112,360]{2,1,0:T(8,128)(2,1)} %broadcast_select_fusion), calls=%async_computation.3 | async-start | bytes 2752512 | tf_op jit(solution)/shard_map/all_to_all | solution.py:284
  333.7 21.5 %all-to-all-done.1 = bf16[16,112,360]{2,1,0:T(8,128)(2,1)} async-done(((bf16[16,112,360]{2,1,0:T(8,128)(2,1)}), bf16[16,112,360]{2,1,0:T(8,128)(2,1)}, u32[]{:S(2)}, u32[]{:S(2)}) %all-to-all-start.1) | async-done | bytes 1290272 | tf_op jit(solution)/shard_map/all_to_all | solution.py:284
  355.2 3.2 gather_fusion.7
  (57 shorter events, 0.8 us)
Async XLA Ops:
  6.5 167.7 %copy-start = (bf16[512,2880]{0,1:T(8,128)(2,1)S(1)}, bf16[512,2880]{0,1:T(8,128)(2,1)}, u32[]{:S(2)}) copy-start(bf16[512,2880]{0,1:T(8,128)(2,1)} %param.25) | copy-start | bytes 8847364
  6.5 58.9 %all-gather.6.cloned.1.call-start = ((), (), s32[]{:S(2)}) async-start(), calls=%async_computation.4 | async-start | bytes 2228224 | tf_op jit(solution)/shard_map/all_gather | solution.py:168
  11.4 12.0 %copy-start.12 = (s32[256]{0:T(256)S(1)}, s32[256]{0:T(256)}, u32[]{:S(2)}) copy-start(s32[256]{0:T(256)} %param.18) | copy-start | bytes 3076
  11.4 12.1 %copy-start.9 = (s32[16,16]{1,0:T(8,128)S(1)}, s32[16,16]{1,0:T(8,128)}, u32[]{:S(2)}) copy-start(s32[16,16]{1,0:T(8,128)} %param.17) | copy-start | bytes 3076
  14.6 29.8 %all-to-all-start = ((bf16[16,112,360]{2,1,0:T(8,128)(2,1)}), bf16[16,112,360]{2,1,0:T(8,128)(2,1)}, u32[]{:S(2)}, u32[]{:S(2)}) async-start(bf16[16,112,360]{2,1,0:T(8,128)(2,1)} %gather_fusion), calls=%async_computation | async-start | bytes 2752512 | tf_op jit(solution)/shard_map/all_to_all | solution.py:246
  22.4 78.2 %all-gather.8.cloned.1.call-start = ((), (), s32[]{:S(2)}) async-start(), calls=%async_computation.7 | async-start | bytes 5308416 | tf_op jit(solution)/shard_map/all_gather | solution.py:250
  44.4 4.9 %copy-start.10 = (bf16[2880]{0:T(1024)(128)(2,1)S(1)}, bf16[2880]{0:T(1024)(128)(2,1)}, u32[]{:S(2)}) copy-start(bf16[2880]{0:T(1024)(128)(2,1)} %param.22) | copy-start | bytes 17284
  49.0 169.5 %reduce-scatter.3.cloned.1.call-start = ((), (), s32[]{:S(2)}) async-start(), calls=%async_computation.5 | async-start | bytes 4976640 | tf_op jit(solution)/shard_map/reduce_scatter | solution.py:267
  50.2 5.0 %copy-start.13 = (s32[64]{0:T(128)S(1)}, s32[64]{0:T(128)}, u32[]{:S(2)}) copy-start(s32[64]{0:T(128)} %param.20) | copy-start | bytes 772
  108.0 3.5 copy-start.6
  117.1 7.6 %copy-start.7 = (f32[768,32]{0,1:T(8,128)S(1)}, f32[768,32]{0,1:T(8,128)}, u32[]{:S(2)}) copy-start(f32[768,32]{0,1:T(8,128)} %get-tuple-element.11) | copy-start | bytes 294916
  117.2 7.6 %copy-start.8 = (f32[768,32]{0,1:T(8,128)S(1)}, f32[768,32]{0,1:T(8,128)}, u32[]{:S(2)}) copy-start(f32[768,32]{0,1:T(8,128)} %get-tuple-element.12) | copy-start | bytes 294916
  179.9 1.1 copy-start.3
  179.9 40.7 %copy-start.11 = (bf16[2880]{0:T(1024)(128)(2,1)S(1)}, bf16[2880]{0:T(1024)(128)(2,1)}, u32[]{:S(2)}) copy-start(bf16[2880]{0:T(1024)(128)(2,1)} %param.26) | copy-start | bytes 17284
  179.9 72.8 %all-gather.10.cloned.1.call-start = ((), (), s32[]{:S(2)}) async-start(), calls=%async_computation.8 | async-start | bytes 4976640 | tf_op jit(solution)/shard_map/all_gather | solution.py:271
  220.6 96.1 %reduce-scatter.5.cloned.1.call-start = ((), (), s32[]{:S(2)}) async-start(), calls=%async_computation.6 | async-start | bytes 4976640 | tf_op jit(solution)/shard_map/reduce_scatter | solution.py:276
  256.0 4.7 %copy-start.2 = (f32[6144,360]{0,1:T(8,128)}, f32[6144,360]{0,1:T(8,128)S(1)}, u32[]{:S(2)}) copy-start(f32[6144,360]{0,1:T(8,128)S(1)} %convert_element_type.117) | copy-start | bytes 26542084
  260.1 1.6 copy-start.5
  278.0 38.6 %copy-start.4 = (bf16[768,360]{0,1:T(8,128)(2,1)S(1)}, bf16[768,360]{0,1:T(8,128)(2,1)}, u32[]{:S(2)}) copy-start(bf16[768,360]{0,1:T(8,128)(2,1)} %add_convert_fusion.1) | copy-start | bytes 1658884
  324.1 34.3 %copy-start.1 = (bf16[512,2880]{0,1:T(8,128)(2,1)S(1)}, bf16[512,2880]{0,1:T(8,128)(2,1)}, u32[]{:S(2)}) copy-start(bf16[512,2880]{0,1:T(8,128)(2,1)} %param.25) | copy-start | bytes 8847364
  327.0 28.2 %all-to-all-start.1 = ((bf16[16,112,360]{2,1,0:T(8,128)(2,1)}), bf16[16,112,360]{2,1,0:T(8,128)(2,1)}, u32[]{:S(2)}, u32[]{:S(2)}) async-start(bf16[16,112,360]{2,1,0:T(8,128)(2,1)} %broadcast_select_fusion), calls=%async_computation.3 | async-start | bytes 2752512 | tf_op jit(solution)/shard_map/all_to_all | solution.py:284
Sparse Core Ops, SparseCore 0:
  9.5 55.8 all-gather.5
  67.1 33.5 all-gather.7
  180.0 38.4 reduce-scatter.2
  220.7 31.9 all-gather.9
  278.1 38.4 reduce-scatter.4

commit v3 on v2

--- a/solution.py
+++ b/solution.py
@@ -173,23 +173,6 @@
     return jnp.where(inside[..., None, None], picked, initial)
 
 
-def norm_groups(parts, gains):
-    widened = parts.astype(jnp.float32)
-    total = jnp.sum(widened * widened, axis=(0, 2), keepdims=True)
-    factor = lax.rsqrt(total / (parts.shape[0] * parts.shape[2]) + EPSILON)
-    return (widened * factor * gains.astype(jnp.float32)).astype(jnp.bfloat16)
-
-
-def group_dot(parts, weight):
-    groups, _, share = parts.shape
-    return jnp.einsum(
-        "gtf,gfo->to",
-        parts,
-        weight.reshape((groups, share) + weight.shape[1:]),
-        preferred_element_type=jnp.float32,
-    )
-
-
 def local(
     suffix_tokens,
     route_lengths,
@@ -247,14 +230,16 @@
         my_features[send_order], "req", split_axis=0, concat_axis=0, tiled=True
     )
     input_part = landed.reshape(peers * slot_length, feature_share)[flat_index]
-    input_groups = lax.all_gather(input_part, "tp", axis=0, tiled=False)
+    input_rows = lax.all_gather(input_part, "tp", axis=1, tiled=True)
     row_total = input_part.shape[0]
-    normed_in = norm_groups(input_groups, attn_gain.reshape(splits, 1, feature_share))
-    queries = group_dot(normed_in, w_query).reshape(row_total, -1, head_dim)
+    normed_in = norm_rows(input_rows, attn_gain)
+    queries = jnp.dot(normed_in, w_query, preferred_element_type=jnp.float32).reshape(
+        row_total, -1, head_dim
+    )
     queries = rotate(queries, positions).astype(jnp.bfloat16)
-    paired = group_dot(normed_in, w_keyval.reshape(features, -1)).reshape(
-        row_total, value_heads, 2 * head_dim
-    )
+    paired = jnp.dot(
+        normed_in, w_keyval.reshape(features, -1), preferred_element_type=jnp.float32
+    ).reshape(row_total, value_heads, 2 * head_dim)
     rotated = rotate(paired[..., :head_dim], positions)
     paired = jnp.concatenate([rotated, paired[..., head_dim:]], axis=-1).astype(jnp.bfloat16)
     attended = attend_pallas(
@@ -268,10 +253,10 @@
         partial_value.astype(jnp.bfloat16), "tp", scatter_dimension=1, tiled=True
     ).astype(jnp.float32)
     residual_part = (input_part.astype(jnp.float32) + summed).astype(jnp.bfloat16)
-    residual_groups = lax.all_gather(residual_part, "tp", axis=0, tiled=False)
-    normed_mid = norm_groups(residual_groups, mlp_gain.reshape(splits, 1, feature_share))
-    gate_proj = group_dot(normed_mid, w_gate)
-    up_proj = group_dot(normed_mid, w_up)
+    residual = lax.all_gather(residual_part, "tp", axis=1, tiled=True)
+    normed_mid = norm_rows(residual, mlp_gain)
+    gate_proj = jnp.dot(normed_mid, w_gate, preferred_element_type=jnp.float32)
+    up_proj = jnp.dot(normed_mid, w_up, preferred_element_type=jnp.float32)
     hidden = (jax.nn.silu(gate_proj) * up_proj).astype(jnp.bfloat16)
     down_sum = lax.psum_scatter(
         jnp.dot(hidden, w_down, preferred_element_type=jnp.float32).astype(jnp.bfloat16),

time: 366 us -> 346 us (0.945)
  local copies, waits for them, and re-layouts: 79.3 us -> 50.9 us
  waiting for transfers between devices: 174 us -> 187 us
  matrix products: 34.4 us -> 28.7 us
    reshape x4 -> x2, local copies, waits for them, and re-layouts: 11 us -> 0.79 us  [the longest x2 10.2 us: group_dot(): weight.reshape((groups, share) + weight.shape[1:])]
    all_gather x2, waiting for transfers between devices: 48.4 us -> 57.6 us  [the longest x1 32.1 us: local(): residual = lax.all_gather(residual_part, 'tp', axis=1, tiled=True)]
    convert_element_type x3 -> x0, local copies, waits for them, and re-layouts: 7.53 us -> none  [the longest x1 7.35 us: norm_groups(): widened = parts.astype(jnp.float32)]
    unnamed x29 -> x26, local copies, waits for them, and re-layouts: 6.04 us -> 0.49 us
    dot_general x1 -> x0, local copies, waits for them, and re-layouts: 4.97 us -> none  [group_dot(): jnp.einsum('gtf,gfo->to', parts, weight.reshape((groups, share) + weight....]
    dot_general x3, matrix products: 16.2 us -> 11.8 us  [the longest x1 6.06 us: local(): jnp.dot(normed_in, w_query, preferred_element_type=jnp.float32)]
  transfers between devices with their start and end apart: 7 -> 7, of which waited for: 7 -> 7; matrix products, arithmetic and copies ran while one was open for 11% -> 8% of each run, Pallas kernels for 0% -> 0%
where the time goes in v3:
time: 346 us; the launch traced here: 345 us
  waiting for transfers between devices  187 us (54%)
  local copies, waits for them, and re-layouts  50.9 us (15%)
  matrix products  28.7 us (8%)
  Pallas kernels  28.7 us (8%)
  other arithmetic  22.2 us (6%)
  starting transfers between devices  14.9 us (4%)
  between operations  13.4 us (4%)
    reduce_scatter x1, waiting for transfers between devices, local(): lax.psum_scatter(partial_value.astype(jnp.bfloat16), 'tp', scatter_dimens...  38.5 us
    reduce_scatter x1, waiting for transfers between devices, local(): lax.psum_scatter(jnp.dot(hidden, w_down, preferred_element_type=jnp.float...  37.8 us
    all_gather x1, waiting for transfers between devices, local(): residual = lax.all_gather(residual_part, 'tp', axis=1, tiled=True)  32.1 us
    pallas_call x1, Pallas kernels, attend_pallas(): pl.pallas_call(attend_kernel, grid=(peers,), in_specs=[pl.BlockSpec(memor...  28.7 us
    all_gather x1, waiting for transfers between devices, local(): input_rows = lax.all_gather(input_part, 'tp', axis=1, tiled=True)  25.5 us
    all_to_all x1, waiting for transfers between devices, local(): lax.all_to_all(out_slots, 'req', split_axis=0, concat_axis=0, tiled=True)  20.8 us
    all_to_all x1, waiting for transfers between devices, local(): lax.all_to_all(my_features[send_order], 'req', split_axis=0, concat_axis=...  19.5 us
    gather x3, local copies, waits for them, and re-layouts, to_slots(): return values[slot_source].reshape((peers, slot_length) + values.shape[1:])  18 us
  transfers between devices with their start and end apart: 7, of which 7 were waited for; matrix products, arithmetic and copies ran while one was open for 8% of the time, Pallas kernels for 0%

profile of v3, /device:TPU:7, one launch (start us, length us, event | category | flops | bytes accessed | tf_op | source)
XLA Modules:
  0.0 345.3 jit_solution(11670862037995091618)
XLA Ops:
  6.5 0.7 all-gather.5.cloned.1.call-update
  7.3 0.8 fusion.48
  8.1 0.1 select_reduce_fusion.5
  8.2 3.2 constant_dynamic-slice_fusion.1
  11.4 3.2 gather_fusion
  14.6 7.8 %all-to-all-start = ((bf16[16,112,360]{2,1,0:T(8,128)(2,1)}), bf16[16,112,360]{2,1,0:T(8,128)(2,1)}, u32[]{:S(2)}, u32[]{:S(2)}) async-start(bf16[16,112,360]{2,1,0:T(8,128)(2,1)} %gather_fusion), calls=%async_computation | async-start | bytes 2752512 | tf_op jit(solution)/shard_map/all_to_all | solution.py:229
  22.5 0.7 fusion.57
  23.2 0.1 copy.32
  23.3 0.1 reduce
  23.5 0.1 reshape.491
  23.5 0.1 select_reduce_fusion.4
  23.7 0.1 convert_reduce_fusion
  23.7 0.7 fusion.47
  24.4 0.1 select_reduce_fusion.1
  24.6 19.5 %all-to-all-done = bf16[16,112,360]{2,1,0:T(8,128)(2,1)} async-done(((bf16[16,112,360]{2,1,0:T(8,128)(2,1)}), bf16[16,112,360]{2,1,0:T(8,128)(2,1)}, u32[]{:S(2)}, u32[]{:S(2)}) %all-to-all-start) | async-done | bytes 1290272 | tf_op jit(solution)/shard_map/all_to_all | solution.py:229
  44.1 4.0 %gather_fusion.1 = bf16[768,360]{1,0:T(8,128)(2,1)S(1)} fusion(bf16[1792,360]{1,0:T(8,128)(2,1)} %bitcast.4, s32[1024]{0:T(1024)S(1)} %pad_clamp_fusion.2), kind=kCustom, calls=%fused_computation.1 | custom fusion | bytes 1108992 | tf_op jit(solution)/shard_map/gather | solution.py:232
  48.1 1.1 copy.33
  49.2 0.2 reduce-scatter.3.cloned.1.call-start
  49.4 0.7 convert_element_type.80
  50.1 0.7 bitcast_subtract_fusion.1
  50.8 0.1 add_clamp_fusion
  50.9 0.1 min.20
  51.0 0.8 select_reduce_fusion.3
  51.8 0.7 broadcast_add_fusion
  52.5 0.1 add_select_fusion.1
  52.6 0.2 select_reduce_fusion
  52.8 0.1 fusion.38
  52.9 1.1 multiply_cosine_fusion.1
  53.9 11.5 %all-gather.5.cloned.1.call-done = bf16[64,128,1,128]{3,1,2,0:T(8,128)(2,1)} async-done(((bf16[4,128,1,128]{3,1,2,0:T(8,128)(2,1)}), bf16[64,128,1,128]{3,1,2,0:T(8,128)(2,1)}) %all-gather.5.cloned.1.call-update) | async-done | bytes 2097168 | tf_op jit(solution)/shard_map/all_gather | solution.py:168
  65.5 7.4 %gather_fusion.4 = bf16[2048,128]{1,0:T(8,128)(2,1)S(1)} fusion(bf16[8192,128]{1,0:T(8,128)(2,1)} %bitcast.54, s32[2048]{0:T(1024)S(1)} %fusion.38), kind=kCustom, calls=%fused_computation.4 | custom fusion | bytes 1056768 | tf_op jit(solution)/shard_map/gather | solution.py:172
  72.9 1.1 broadcast_select_fusion.1.tail_ref
  74.0 25.5 %all-gather.9.cloned.1.call-done = bf16[768,2880]{0,1:T(8,128)(2,1)} async-done(((bf16[768,360]{0,1:T(8,128)(2,1)}), bf16[768,2880]{0,1:T(8,128)(2,1)}) %all-gather.9.cloned.1.call-update) | async-done | bytes 4423696 | tf_op jit(solution)/shard_map/all_gather | solution.py:233
  99.5 3.3 fusion
  102.9 0.2 copy-done.4
  103.1 2.6 fusion.14
  105.7 0.4 fusion.31
  106.2 0.2 copy.36
  106.4 6.1 %fusion.12 = f32[768,512]{0,1:T(8,128)S(1)} fusion(bf16[2880,512]{1,0:T(8,128)(2,1)} %param.23, bf16[768,2880]{0,1:T(8,128)(2,1)} %all-gather.9.cloned.1.call-done, f32[2880]{0:T(1024)S(1)} %convert_element_type.80, f32[768]{0:T(1024)S(1)} %add_rsqrt_fusion.1), kind=kOutput, calls=%fused_computation.25 | convolution fusion | flops 2273771520 | bytes 8960256 | tf_op jit(solution)/shard_map/dot_general | solution.py:236
  112.5 0.2 subtract_convert_fusion
  112.7 0.9 pad_maximum_fusion
  113.6 2.3 copy.35
  115.9 4.6 %gather_fusion.3 = bf16[1792,128]{1,0:T(8,128)(2,1)} fusion(bf16[768,128]{1,0:T(8,128)(2,1)S(1)} %copy.36, s32[2048]{0:T(1024)S(1)} %pad_clamp_fusion), kind=kCustom, calls=%fused_computation.3 | custom fusion | bytes 924672 | tf_op jit(solution)/shard_map/gather | solution.py:223
  120.5 7.4 %gather_fusion.2 = bf16[1792,512]{1,0:T(8,128)(2,1)} fusion(bf16[768,512]{1,0:T(8,128)(2,1)} %copy.35, s32[2048]{0:T(1024)S(1)} %pad_clamp_fusion), kind=kCustom, calls=%fused_computation.2 | custom fusion | bytes 3677184 | tf_op jit(solution)/shard_map/gather | solution.py:223
  127.9 28.7 %shard_map.145 = bf16[16,112,512]{2,1,0:T(8,128)(2,1)} custom-call(f32[8]{0:T(128)} %sink_ref.1, bf16[16,112,512]{2,1,0:T(8,128)(2,1)} %bitcast.58, bf16[16,112,128]{2,1,0:T(8,128)(2,1)} %bitcast.60, bf16[16,128,128]{2,1,0:T(8,128)(2,1)} %broadcast_select_fusion.1.tail_ref), custom_call_target="tpu_custom_call" | custom-call | flops 880803840 | bytes 4653056 | tf_op jit(solution)/shard_map/pallas_call | solution.py:136
  156.6 5.1 %gather_fusion.5 = bf16[768,512]{1,0:T(8,128)(2,1)} fusion(bf16[1792,512]{1,0:T(8,128)(2,1)} %bitcast.53, s32[1024]{0:T(1024)S(1)} %pad_clamp_fusion.2), kind=kCustom, calls=%fused_computation.5 | custom fusion | bytes 1575936 | tf_op jit(solution)/shard_map/gather | solution.py:245
  161.7 5.6 %convolution_convert_fusion = bf16[768,2880]{0,1:T(8,128)(2,1)} fusion(bf16[768,512]{1,0:T(8,128)(2,1)} %gather_fusion.5, bf16[512,2880]{0,1:T(8,128)(2,1)S(1)} %copy-done), kind=kOutput, calls=%fused_computation.18 | convolution fusion | flops 2267136000 | bytes 8159232 | tf_op jit(solution)/shard_map/dot_general | solution.py:251
  167.5 38.5 %reduce-scatter.3.cloned.1.call-done = bf16[768,360]{0,1:T(8,128)(2,1)} async-done(((bf16[768,2880]{0,1:T(8,128)(2,1)}), bf16[768,360]{0,1:T(8,128)(2,1)}) %reduce-scatter.3.cloned.1.call-update) | async-done | bytes 552976 | tf_op jit(solution)/shard_map/reduce_scatter | solution.py:252
  206.0 2.2 add_convert_fusion.1
  208.3 32.1 %all-gather.7.cloned.1.call-done = bf16[768,2880]{0,1:T(8,128)(2,1)} async-done(((bf16[768,360]{0,1:T(8,128)(2,1)}), bf16[768,2880]{0,1:T(8,128)(2,1)}) %all-gather.7.cloned.1.call-update) | async-done | bytes 4423696 | tf_op jit(solution)/shard_map/all_gather | solution.py:256
  240.4 3.3 fusion.3
  243.7 0.2 copy-done.5
  244.0 3.1 fusion.8
  247.1 11.3 %convolution_convert_fusion.1 = bf16[768,2880]{0,1:T(8,128)(2,1)} fusion(bf16[360,2880]{1,0:T(8,128)(2,1)} %param.29, bf16[2880,360]{0,1:T(8,128)(2,1)} %param.28, bf16[768,2880]{0,1:T(8,128)(2,1)} %all-gather.7.cloned.1.call-done, f32[2880]{0:T(1024)S(1)} %convert_element_type.90, f32[768]{0:T(1024)S(1)} %add_rsqrt_fusion, f32[768,360]{0,1:T(8,128)} %fusion.8), kind=kOutput, calls=%fused_computation.19 | convolution fusion | flops 3197767680 | bytes 14115072 | tf_op jit(solution)/shard_map/dot_general | solution.py:262
  258.4 0.8 fusion.56
  259.1 0.1 iota_compare_fusion.5
  259.2 37.8 %reduce-scatter.5.cloned.1.call-done = bf16[768,360]{0,1:T(8,128)(2,1)} async-done(((bf16[768,2880]{0,1:T(8,128)(2,1)}), bf16[768,360]{0,1:T(8,128)(2,1)}) %reduce-scatter.5.cloned.1.call-update) | async-done | bytes 552976 | tf_op jit(solution)/shard_map/reduce_scatter | solution.py:261
  297.0 1.2 add_convert_fusion
  298.2 0.3 copy.37
  298.5 6.0 %gather_fusion.6 = bf16[1792,360]{1,0:T(8,128)(2,1)} fusion(bf16[768,360]{1,0:T(8,128)(2,1)S(1)} %copy.37, s32[2048]{0:T(1024)S(1)} %pad_clamp_fusion), kind=kCustom, calls=%fused_computation.6 | custom fusion | bytes 2587648 | tf_op jit(solution)/shard_map/gather | solution.py:223
  304.4 2.9 broadcast_select_fusion
  307.3 6.7 %all-to-all-start.1 = ((bf16[16,112,360]{2,1,0:T(8,128)(2,1)}), bf16[16,112,360]{2,1,0:T(8,128)(2,1)}, u32[]{:S(2)}, u32[]{:S(2)}) async-start(bf16[16,112,360]{2,1,0:T(8,128)(2,1)} %broadcast_select_fusion), calls=%async_computation.3 | async-start | bytes 2752512 | tf_op jit(solution)/shard_map/all_to_all | solution.py:269
  314.1 0.7 fusion.46
  314.8 20.8 %all-to-all-done.1 = bf16[16,112,360]{2,1,0:T(8,128)(2,1)} async-done(((bf16[16,112,360]{2,1,0:T(8,128)(2,1)}), bf16[16,112,360]{2,1,0:T(8,128)(2,1)}, u32[]{:S(2)}, u32[]{:S(2)}) %all-to-all-start.1) | async-done | bytes 1290272 | tf_op jit(solution)/shard_map/all_to_all | solution.py:269
  335.6 3.2 gather_fusion.7
  (49 shorter events, 0.4 us)
Async XLA Ops:
  6.5 155.2 %copy-start = (bf16[512,2880]{0,1:T(8,128)(2,1)S(1)}, bf16[512,2880]{0,1:T(8,128)(2,1)}, u32[]{:S(2)}) copy-start(bf16[512,2880]{0,1:T(8,128)(2,1)} %param.25) | copy-start | bytes 8847364
  6.5 58.9 %all-gather.5.cloned.1.call-start = ((), (), s32[]{:S(2)}) async-start(), calls=%async_computation.4 | async-start | bytes 2228224 | tf_op jit(solution)/shard_map/all_gather | solution.py:168
  11.4 12.0 %copy-start.11 = (s32[256]{0:T(256)S(1)}, s32[256]{0:T(256)}, u32[]{:S(2)}) copy-start(s32[256]{0:T(256)} %param.18) | copy-start | bytes 3076
  11.4 12.1 %copy-start.8 = (s32[16,16]{1,0:T(8,128)S(1)}, s32[16,16]{1,0:T(8,128)}, u32[]{:S(2)}) copy-start(s32[16,16]{1,0:T(8,128)} %param.17) | copy-start | bytes 3076
  14.6 29.5 %all-to-all-start = ((bf16[16,112,360]{2,1,0:T(8,128)(2,1)}), bf16[16,112,360]{2,1,0:T(8,128)(2,1)}, u32[]{:S(2)}, u32[]{:S(2)}) async-start(bf16[16,112,360]{2,1,0:T(8,128)(2,1)} %gather_fusion), calls=%async_computation | async-start | bytes 2752512 | tf_op jit(solution)/shard_map/all_to_all | solution.py:229
  22.5 77.1 %all-gather.9.cloned.1.call-start = ((), (), s32[]{:S(2)}) async-start(), calls=%async_computation.8 | async-start | bytes 4976640 | tf_op jit(solution)/shard_map/all_gather | solution.py:233
  23.7 20.5 %copy-start.10 = (s32[16]{0:T(128)}, s32[16]{0:T(128)S(1)}, u32[]{:S(2)}) copy-start(s32[16]{0:T(128)S(1)} %select_reduce_fusion.4) | copy-start | bytes 196
  49.2 156.8 %reduce-scatter.3.cloned.1.call-start = ((), (), s32[]{:S(2)}) async-start(), calls=%async_computation.5 | async-start | bytes 4976640 | tf_op jit(solution)/shard_map/reduce_scatter | solution.py:252
  99.5 3.6 %copy-start.4 = (bf16[768,2880]{0,1:T(8,128)(2,1)S(1)}, bf16[768,2880]{0,1:T(8,128)(2,1)}, u32[]{:S(2)}) copy-start(bf16[768,2880]{0,1:T(8,128)(2,1)} %all-gather.9.cloned.1.call-done) | copy-start | bytes 13271044
  106.4 6.1 %copy-start.6 = (f32[768,32]{0,1:T(8,128)S(1)}, f32[768,32]{0,1:T(8,128)}, u32[]{:S(2)}) copy-start(f32[768,32]{0,1:T(8,128)} %get-tuple-element.11) | copy-start | bytes 294916
  106.4 6.1 %copy-start.7 = (f32[768,32]{0,1:T(8,128)S(1)}, f32[768,32]{0,1:T(8,128)}, u32[]{:S(2)}) copy-start(f32[768,32]{0,1:T(8,128)} %get-tuple-element.12) | copy-start | bytes 294916
  167.4 38.6 %copy-start.3 = (bf16[768,360]{0,1:T(8,128)(2,1)S(1)}, bf16[768,360]{0,1:T(8,128)(2,1)}, u32[]{:S(2)}) copy-start(bf16[768,360]{0,1:T(8,128)(2,1)} %copy.33) | copy-start | bytes 1658884
  167.4 40.9 %copy-start.9 = (bf16[2880]{0:T(1024)(128)(2,1)S(1)}, bf16[2880]{0:T(1024)(128)(2,1)}, u32[]{:S(2)}) copy-start(bf16[2880]{0:T(1024)(128)(2,1)} %param.26) | copy-start | bytes 17284
  167.4 72.9 %all-gather.7.cloned.1.call-start = ((), (), s32[]{:S(2)}) async-start(), calls=%async_computation.6 | async-start | bytes 4976640 | tf_op jit(solution)/shard_map/all_gather | solution.py:256
  206.0 37.7 %copy-start.12 = (bf16[2880,360]{0,1:T(8,128)(2,1)S(1)}, bf16[2880,360]{0,1:T(8,128)(2,1)}, u32[]{:S(2)}) copy-start(bf16[2880,360]{0,1:T(8,128)(2,1)} %param.27) | copy-start | bytes 6220804
  208.2 88.8 %reduce-scatter.5.cloned.1.call-start = ((), (), s32[]{:S(2)}) async-start(), calls=%async_computation.7 | async-start | bytes 4976640 | tf_op jit(solution)/shard_map/reduce_scatter | solution.py:261
  240.4 3.6 %copy-start.5 = (bf16[768,2880]{0,1:T(8,128)(2,1)S(1)}, bf16[768,2880]{0,1:T(8,128)(2,1)}, u32[]{:S(2)}) copy-start(bf16[768,2880]{0,1:T(8,128)(2,1)} %all-gather.7.cloned.1.call-done) | copy-start | bytes 13271044
  258.3 38.6 %copy-start.2 = (bf16[768,360]{0,1:T(8,128)(2,1)S(1)}, bf16[768,360]{0,1:T(8,128)(2,1)}, u32[]{:S(2)}) copy-start(bf16[768,360]{0,1:T(8,128)(2,1)} %add_convert_fusion.1) | copy-start | bytes 1658884
  304.4 34.3 %copy-start.1 = (bf16[512,2880]{0,1:T(8,128)(2,1)S(1)}, bf16[512,2880]{0,1:T(8,128)(2,1)}, u32[]{:S(2)}) copy-start(bf16[512,2880]{0,1:T(8,128)(2,1)} %param.25) | copy-start | bytes 8847364
  307.3 28.3 %all-to-all-start.1 = ((bf16[16,112,360]{2,1,0:T(8,128)(2,1)}), bf16[16,112,360]{2,1,0:T(8,128)(2,1)}, u32[]{:S(2)}, u32[]{:S(2)}) async-start(bf16[16,112,360]{2,1,0:T(8,128)(2,1)} %broadcast_select_fusion), calls=%async_computation.3 | async-start | bytes 2752512 | tf_op jit(solution)/shard_map/all_to_all | solution.py:269
Sparse Core Ops, SparseCore 0:
  9.5 55.9 all-gather.4
  67.1 32.3 all-gather.8
  167.5 38.4 reduce-scatter.2
  208.3 31.9 all-gather.6
  258.5 38.4 reduce-scatter.4

commit v4 on v3

--- a/solution.py
+++ b/solution.py
@@ -155,6 +155,9 @@
 def fetch_prefix(attach_slots, prefix_cache, block_of_slot, window):
     total_blocks = block_of_slot.shape[0]
     block_len = prefix_cache.shape[1]
+    peers = lax.axis_size("req")
+    me = lax.axis_index("req")
+    held_here = prefix_cache.shape[0]
     catalog = jnp.arange(total_blocks)
     home_row = jnp.sum(
         jnp.where(block_of_slot[None, :] == catalog[:, None], catalog[None, :], 0), axis=1
@@ -165,11 +168,21 @@
     tail_offset = wanted - block_id * block_len
     trailing = prefix_cache.shape[2:]
     initial = jnp.zeros((attach_slots.shape[0], window) + trailing, jnp.bfloat16)
-    shard_rows = lax.all_gather(prefix_cache, "req", axis=0, tiled=True)
+    pieces = [prefix_cache]
+    for shift in range(1, peers):
+        pieces.append(
+            lax.ppermute(
+                prefix_cache, "req", [(i, (i + shift) % peers) for i in range(peers)]
+            )
+        )
+    shard_rows = jnp.concatenate(pieces, axis=0)
     held_blocks = shard_rows.shape[0]
     flat_rows = shard_rows.reshape((held_blocks * block_len,) + trailing)
     inside = (tail_store >= 0) & (tail_store < held_blocks)
-    picked = flat_rows[jnp.clip(tail_store, 0, held_blocks - 1) * block_len + tail_offset]
+    store = jnp.clip(tail_store, 0, held_blocks - 1)
+    owner = store // held_here
+    arrival = (me - owner + peers) % peers
+    picked = flat_rows[(arrival * held_here + store % held_here) * block_len + tail_offset]
     return jnp.where(inside[..., None, None], picked, initial)
 
 

time: 346 us -> 350 us (1.012)
  waiting for transfers between devices: 187 us -> 152 us
  starting transfers between devices: 14.9 us -> 39.5 us
  local copies, waits for them, and re-layouts: 50.9 us -> 64.3 us
    all_gather x1, waiting for transfers between devices: 25.5 us -> 0.01 us  [local(): input_rows = lax.all_gather(input_part, 'tp', axis=1, tiled=True)]
    ppermute x0 -> x15, starting transfers between devices: none -> 24.9 us  [fetch_prefix(): lax.ppermute(prefix_cache, 'req', [(i, (i + shift) % peers) for i in rang...]
    unnamed x26 -> x43, local copies, waits for them, and re-layouts: 0.49 us -> 13.3 us
    all_gather x1 -> x0, waiting for transfers between devices: 11.5 us -> none  [fetch_prefix(): shard_rows = lax.all_gather(prefix_cache, 'req', axis=0, tiled=True)]
  transfers between devices with their start and end apart: 7 -> 21, of which waited for: 7 -> 7; matrix products, arithmetic and copies ran while one was open for 8% -> 9% of each run, Pallas kernels for 0% -> 0%
where the time goes in v4:
time: 350 us; the launch traced here: 349 us
  waiting for transfers between devices  152 us (43%)
  local copies, waits for them, and re-layouts  64.3 us (18%)
  starting transfers between devices  39.5 us (11%)
  matrix products  28.7 us (8%)
  Pallas kernels  28.7 us (8%)
  other arithmetic  22.2 us (6%)
  between operations  13.4 us (4%)
    reduce_scatter x1, waiting for transfers between devices, local(): lax.psum_scatter(partial_value.astype(jnp.bfloat16), 'tp', scatter_dimens...  41 us
    reduce_scatter x1, waiting for transfers between devices, local(): lax.psum_scatter(jnp.dot(hidden, w_down, preferred_element_type=jnp.float...  37.7 us
    all_gather x1, waiting for transfers between devices, local(): residual = lax.all_gather(residual_part, 'tp', axis=1, tiled=True)  32 us
    pallas_call x1, Pallas kernels, attend_pallas(): pl.pallas_call(attend_kernel, grid=(peers,), in_specs=[pl.BlockSpec(memor...  28.7 us
    ppermute x15, starting transfers between devices, fetch_prefix(): lax.ppermute(prefix_cache, 'req', [(i, (i + shift) % peers) for i in rang...  24.9 us
    all_to_all x1, waiting for transfers between devices, local(): lax.all_to_all(out_slots, 'req', split_axis=0, concat_axis=0, tiled=True)  20.8 us
    gather x3, local copies, waits for them, and re-layouts, to_slots(): return values[slot_source].reshape((peers, slot_length) + values.shape[1:])  18 us
    all_to_all x1, waiting for transfers between devices, local(): lax.all_to_all(my_features[send_order], 'req', split_axis=0, concat_axis=...  16.8 us
  transfers between devices with their start and end apart: 21, of which 7 were waited for; matrix products, arithmetic and copies ran while one was open for 9% of the time, Pallas kernels for 0%

profile of v4, /device:TPU:7, one launch (start us, length us, event | category | flops | bytes accessed | tf_op | source)
XLA Modules:
  0.0 348.6 jit_solution(13165630399640641074)
XLA Ops:
  6.5 0.8 fusion.56
  7.5 3.2 constant_dynamic-slice_fusion.1
  10.7 3.2 gather_fusion
  13.9 7.8 %all-to-all-start = ((bf16[16,112,360]{2,1,0:T(8,128)(2,1)}), bf16[16,112,360]{2,1,0:T(8,128)(2,1)}, u32[]{:S(2)}, u32[]{:S(2)}) async-start(bf16[16,112,360]{2,1,0:T(8,128)(2,1)} %gather_fusion), calls=%async_computation | async-start | bytes 2752512 | tf_op jit(solution)/shard_map/all_to_all | solution.py:242
  21.7 0.7 fusion.65
  23.0 0.7 fusion.55
  23.8 16.8 %all-to-all-done = bf16[16,112,360]{2,1,0:T(8,128)(2,1)} async-done(((bf16[16,112,360]{2,1,0:T(8,128)(2,1)}), bf16[16,112,360]{2,1,0:T(8,128)(2,1)}, u32[]{:S(2)}, u32[]{:S(2)}) %all-to-all-start) | async-done | bytes 1290272 | tf_op jit(solution)/shard_map/all_to_all | solution.py:242
  40.7 4.0 %gather_fusion.1 = bf16[768,360]{1,0:T(8,128)(2,1)S(1)} fusion(bf16[1792,360]{1,0:T(8,128)(2,1)} %bitcast.4, s32[1024]{0:T(1024)S(1)} %pad_clamp_fusion.2), kind=kCustom, calls=%fused_computation.1 | custom fusion | bytes 1108992 | tf_op jit(solution)/shard_map/gather | solution.py:245
  44.6 1.1 copy.33
  45.9 2.4 collective-permute-start.1
  48.3 2.2 collective-permute-start.2
  51.0 0.7 bitcast_subtract_fusion.1
  51.8 0.8 select_reduce_fusion.3
  52.6 1.6 constant_dynamic-update-slice_fusion.15
  55.2 1.1 multiply_cosine_fusion.1
  56.4 0.7 convert_element_type.80
  57.1 2.6 collective-permute-start.5
  59.7 1.6 constant_dynamic-update-slice_fusion.14
  61.2 3.6 %collective-permute-start.6 = (bf16[4,128,1,128]{3,1,2,0:T(8,128)(2,1)}, bf16[4,128,1,128]{3,1,2,0:T(8,128)(2,1)S(1)}, u32[]{:S(2)}, u32[]{:S(2)}) collective-permute-start(bf16[4,128,1,128]{3,1,2,0:T(8,128)(2,1)} %param.19), channel_id=1, source_target_pairs={{0,56},{8,64},{16,72},{24,80},{32,88},{40,96},{48,104},{56,112},{6... | collective-permute-start | bytes 393224 | tf_op jit(solution)/shard_map/ppermute | solution.py:174
  64.9 1.6 constant_dynamic-update-slice_fusion.13
  66.4 1.4 collective-permute-start.7
  68.5 0.9 collective-permute-start.8
  69.5 0.7 constant_dynamic-update-slice_fusion.11
  70.1 3.8 %collective-permute-start.9 = (bf16[4,128,1,128]{3,1,2,0:T(8,128)(2,1)S(1)}, bf16[4,128,1,128]{3,1,2,0:T(8,128)(2,1)S(1)}, u32[]{:S(2)}, u32[]{:S(2)}) collective-permute-start(bf16[4,128,1,128]{3,1,2,0:T(8,128)(2,1)S(1)} %copy-done.8), channel_id=1, source_target_pairs={{0,80},{8,88},{16,96},{24,104},{32,112},{40,120},{48,0},{56,8},{64... | collective-permute-start | bytes 393224 | tf_op jit(solution)/shard_map/ppermute | solution.py:174
  74.6 3.1 collective-permute-start.10
  79.4 0.7 constant_dynamic-update-slice_fusion.7
  80.0 1.2 collective-permute-start.13
  81.2 0.7 constant_dynamic-update-slice_fusion.6
  81.9 2.7 collective-permute-start.14
  84.5 0.7 constant_dynamic-update-slice_fusion.5
  85.2 0.7 constant_dynamic-update-slice_fusion.4
  85.9 0.7 constant_dynamic-update-slice_fusion.3
  86.6 0.7 constant_dynamic-update-slice_fusion.2
  87.3 1.0 collective-permute-done.13
  88.3 0.7 constant_dynamic-update-slice_fusion.1
  89.0 2.1 collective-permute-done.14
  91.1 0.7 constant_dynamic-update-slice_fusion
  91.8 7.5 %gather_fusion.4 = bf16[2048,128]{1,0:T(8,128)(2,1)S(1)} fusion(bf16[8192,128]{1,0:T(8,128)(2,1)} %bitcast.16, s32[2048]{0:T(1024)S(1)} %fusion.44), kind=kCustom, calls=%fused_computation.4 | custom fusion | bytes 1056768 | tf_op jit(solution)/shard_map/gather | solution.py:185
  99.2 1.1 broadcast_select_fusion.1.tail_ref
  100.4 3.3 fusion
  104.0 2.6 fusion.14
  107.2 6.1 %fusion.12 = f32[768,512]{0,1:T(8,128)S(1)} fusion(bf16[2880,512]{1,0:T(8,128)(2,1)} %param.23, bf16[768,2880]{0,1:T(8,128)(2,1)} %all-gather.6.cloned.1.call-done, f32[2880]{0:T(1024)S(1)} %convert_element_type.80, f32[768]{0:T(1024)S(1)} %add_rsqrt_fusion.1), kind=kOutput, calls=%fused_computation.25 | convolution fusion | flops 2273771520 | bytes 8960256 | tf_op jit(solution)/shard_map/dot_general | solution.py:249
  113.5 0.9 pad_maximum_fusion
  114.5 2.3 copy.35
  116.8 4.6 %gather_fusion.3 = bf16[1792,128]{1,0:T(8,128)(2,1)} fusion(bf16[768,128]{1,0:T(8,128)(2,1)S(1)} %copy.36, s32[2048]{0:T(1024)S(1)} %pad_clamp_fusion), kind=kCustom, calls=%fused_computation.3 | custom fusion | bytes 924672 | tf_op jit(solution)/shard_map/gather | solution.py:236
  121.4 7.4 %gather_fusion.2 = bf16[1792,512]{1,0:T(8,128)(2,1)} fusion(bf16[768,512]{1,0:T(8,128)(2,1)} %copy.35, s32[2048]{0:T(1024)S(1)} %pad_clamp_fusion), kind=kCustom, calls=%fused_computation.2 | custom fusion | bytes 3677184 | tf_op jit(solution)/shard_map/gather | solution.py:236
  128.8 28.7 %shard_map.145 = bf16[16,112,512]{2,1,0:T(8,128)(2,1)} custom-call(f32[8]{0:T(128)} %sink_ref.1, bf16[16,112,512]{2,1,0:T(8,128)(2,1)} %bitcast.73, bf16[16,112,128]{2,1,0:T(8,128)(2,1)} %bitcast.75, bf16[16,128,128]{2,1,0:T(8,128)(2,1)} %broadcast_select_fusion.1.tail_ref), custom_call_target="tpu_custom_call" | custom-call | flops 880803840 | bytes 4653056 | tf_op jit(solution)/shard_map/pallas_call | solution.py:136
  157.5 5.1 %gather_fusion.5 = bf16[768,512]{1,0:T(8,128)(2,1)} fusion(bf16[1792,512]{1,0:T(8,128)(2,1)} %bitcast.69, s32[1024]{0:T(1024)S(1)} %pad_clamp_fusion.2), kind=kCustom, calls=%fused_computation.5 | custom fusion | bytes 1575936 | tf_op jit(solution)/shard_map/gather | solution.py:258
  162.6 5.7 %convolution_convert_fusion = bf16[768,2880]{0,1:T(8,128)(2,1)} fusion(bf16[768,512]{1,0:T(8,128)(2,1)} %gather_fusion.5, bf16[512,2880]{0,1:T(8,128)(2,1)S(1)} %copy-done), kind=kOutput, calls=%fused_computation.18 | convolution fusion | flops 2267136000 | bytes 8159232 | tf_op jit(solution)/shard_map/dot_general | solution.py:264
  168.3 41.0 %reduce-scatter.3.cloned.1.call-done = bf16[768,360]{0,1:T(8,128)(2,1)} async-done(((bf16[768,2880]{0,1:T(8,128)(2,1)}), bf16[768,360]{0,1:T(8,128)(2,1)}) %reduce-scatter.3.cloned.1.call-update) | async-done | bytes 552976 | tf_op jit(solution)/shard_map/reduce_scatter | solution.py:265
  209.4 2.2 add_convert_fusion.1
  211.7 32.0 %all-gather.4.cloned.1.call-done = bf16[768,2880]{0,1:T(8,128)(2,1)} async-done(((bf16[768,360]{0,1:T(8,128)(2,1)}), bf16[768,2880]{0,1:T(8,128)(2,1)}) %all-gather.4.cloned.1.call-update) | async-done | bytes 4423696 | tf_op jit(solution)/shard_map/all_gather | solution.py:269
  243.7 3.3 fusion.3
  247.3 3.1 fusion.8
  250.4 11.3 %convolution_convert_fusion.1 = bf16[768,2880]{0,1:T(8,128)(2,1)} fusion(bf16[360,2880]{1,0:T(8,128)(2,1)} %param.29, bf16[2880,360]{0,1:T(8,128)(2,1)} %param.28, bf16[768,2880]{0,1:T(8,128)(2,1)} %all-gather.4.cloned.1.call-done, f32[2880]{0:T(1024)S(1)} %convert_element_type.90, f32[768]{0:T(1024)S(1)} %add_rsqrt_fusion, f32[768,360]{0,1:T(8,128)} %fusion.8), kind=kOutput, calls=%fused_computation.19 | convolution fusion | flops 3197767680 | bytes 14115072 | tf_op jit(solution)/shard_map/dot_general | solution.py:275
  261.7 0.8 fusion.64
  262.5 37.7 %reduce-scatter.5.cloned.1.call-done = bf16[768,360]{0,1:T(8,128)(2,1)} async-done(((bf16[768,2880]{0,1:T(8,128)(2,1)}), bf16[768,360]{0,1:T(8,128)(2,1)}) %reduce-scatter.5.cloned.1.call-update) | async-done | bytes 552976 | tf_op jit(solution)/shard_map/reduce_scatter | solution.py:274
  300.3 1.2 add_convert_fusion
  301.8 6.0 %gather_fusion.6 = bf16[1792,360]{1,0:T(8,128)(2,1)} fusion(bf16[768,360]{1,0:T(8,128)(2,1)S(1)} %copy.37, s32[2048]{0:T(1024)S(1)} %pad_clamp_fusion), kind=kCustom, calls=%fused_computation.6 | custom fusion | bytes 2587648 | tf_op jit(solution)/shard_map/gather | solution.py:236
  307.8 2.9 broadcast_select_fusion
  310.6 6.7 %all-to-all-start.1 = ((bf16[16,112,360]{2,1,0:T(8,128)(2,1)}), bf16[16,112,360]{2,1,0:T(8,128)(2,1)}, u32[]{:S(2)}, u32[]{:S(2)}) async-start(bf16[16,112,360]{2,1,0:T(8,128)(2,1)} %broadcast_select_fusion), calls=%async_computation.3 | async-start | bytes 2752512 | tf_op jit(solution)/shard_map/all_to_all | solution.py:282
  317.4 0.7 fusion.54
  318.1 20.8 %all-to-all-done.1 = bf16[16,112,360]{2,1,0:T(8,128)(2,1)} async-done(((bf16[16,112,360]{2,1,0:T(8,128)(2,1)}), bf16[16,112,360]{2,1,0:T(8,128)(2,1)}, u32[]{:S(2)}, u32[]{:S(2)}) %all-to-all-start.1) | async-done | bytes 1290272 | tf_op jit(solution)/shard_map/all_to_all | solution.py:282
  338.9 3.2 gather_fusion.7
  (94 shorter events, 7.5 us)
Async XLA Ops:
  6.5 156.0 %copy-start = (bf16[512,2880]{0,1:T(8,128)(2,1)S(1)}, bf16[512,2880]{0,1:T(8,128)(2,1)}, u32[]{:S(2)}) copy-start(bf16[512,2880]{0,1:T(8,128)(2,1)} %param.25) | copy-start | bytes 8847364
  10.7 12.0 %copy-start.12 = (s32[256]{0:T(256)S(1)}, s32[256]{0:T(256)}, u32[]{:S(2)}) copy-start(s32[256]{0:T(256)} %param.18) | copy-start | bytes 3076
  10.7 12.1 %copy-start.9 = (s32[16,16]{1,0:T(8,128)S(1)}, s32[16,16]{1,0:T(8,128)}, u32[]{:S(2)}) copy-start(s32[16,16]{1,0:T(8,128)} %param.17) | copy-start | bytes 3076
  13.9 26.8 %all-to-all-start = ((bf16[16,112,360]{2,1,0:T(8,128)(2,1)}), bf16[16,112,360]{2,1,0:T(8,128)(2,1)}, u32[]{:S(2)}, u32[]{:S(2)}) async-start(bf16[16,112,360]{2,1,0:T(8,128)(2,1)} %gather_fusion), calls=%async_computation | async-start | bytes 2752512 | tf_op jit(solution)/shard_map/all_to_all | solution.py:242
  21.7 78.7 %all-gather.6.cloned.1.call-start = ((), (), s32[]{:S(2)}) async-start(), calls=%async_computation.7 | async-start | bytes 4976640 | tf_op jit(solution)/shard_map/all_gather | solution.py:246
  22.9 17.8 %copy-start.11 = (s32[16]{0:T(128)}, s32[16]{0:T(128)S(1)}, u32[]{:S(2)}) copy-start(s32[16]{0:T(128)S(1)} %select_reduce_fusion.4) | copy-start | bytes 196
  45.7 24.5 %copy-start.8 = (bf16[4,128,1,128]{3,1,2,0:T(8,128)(2,1)S(1)}, bf16[4,128,1,128]{3,1,2,0:T(8,128)(2,1)}, u32[]{:S(2)}) copy-start(bf16[4,128,1,128]{3,1,2,0:T(8,128)(2,1)} %param.19) | copy-start | bytes 393220
  45.7 163.7 %reduce-scatter.3.cloned.1.call-start = ((), (), s32[]{:S(2)}) async-start(), calls=%async_computation.4 | async-start | bytes 4976640 | tf_op jit(solution)/shard_map/reduce_scatter | solution.py:265
  45.8 11.3 %collective-permute-start = (bf16[4,128,1,128]{3,1,2,0:T(8,128)(2,1)}, bf16[4,128,1,128]{3,1,2,0:T(8,128)(2,1)}, u32[]{:S(2)}, u32[]{:S(2)}) collective-permute-start(bf16[4,128,1,128]{3,1,2,0:T(8,128)(2,1)} %param.19), channel_id=1, source_target_pairs={{0,8},{8,16},{16,24},{24,32},{32,40},{40,48},{48,56},{56,64},{64,7... | collective-permute-start | bytes 393224 | tf_op jit(solution)/shard_map/ppermute | solution.py:174
  45.9 15.3 %collective-permute-start.1 = (bf16[4,128,1,128]{3,1,2,0:T(8,128)(2,1)}, bf16[4,128,1,128]{3,1,2,0:T(8,128)(2,1)}, u32[]{:S(2)}, u32[]{:S(2)}) collective-permute-start(bf16[4,128,1,128]{3,1,2,0:T(8,128)(2,1)} %param.19), channel_id=1, source_target_pairs={{0,16},{8,24},{16,32},{24,40},{32,48},{40,56},{48,64},{56,72},{64,... | collective-permute-start | bytes 393224 | tf_op jit(solution)/shard_map/ppermute | solution.py:174
  48.3 18.1 %collective-permute-start.2 = (bf16[4,128,1,128]{3,1,2,0:T(8,128)(2,1)}, bf16[4,128,1,128]{3,1,2,0:T(8,128)(2,1)S(1)}, u32[]{:S(2)}, u32[]{:S(2)}) collective-permute-start(bf16[4,128,1,128]{3,1,2,0:T(8,128)(2,1)} %param.19), channel_id=1, source_target_pairs={{0,24},{8,32},{16,40},{24,48},{32,56},{40,64},{48,72},{56,80},{64,... | collective-permute-start | bytes 393224 | tf_op jit(solution)/shard_map/ppermute | solution.py:174
  50.5 18.0 %collective-permute-start.3 = (bf16[4,128,1,128]{3,1,2,0:T(8,128)(2,1)}, bf16[4,128,1,128]{3,1,2,0:T(8,128)(2,1)S(1)}, u32[]{:S(2)}, u32[]{:S(2)}) collective-permute-start(bf16[4,128,1,128]{3,1,2,0:T(8,128)(2,1)} %param.19), channel_id=1, source_target_pairs={{0,32},{8,40},{16,48},{24,56},{32,64},{40,72},{48,80},{56,88},{64,... | collective-permute-start | bytes 393224 | tf_op jit(solution)/shard_map/ppermute | solution.py:174
  50.9 19.3 %collective-permute-start.4 = (bf16[4,128,1,128]{3,1,2,0:T(8,128)(2,1)}, bf16[4,128,1,128]{3,1,2,0:T(8,128)(2,1)S(1)}, u32[]{:S(2)}, u32[]{:S(2)}) collective-permute-start(bf16[4,128,1,128]{3,1,2,0:T(8,128)(2,1)} %param.19), channel_id=1, source_target_pairs={{0,40},{8,48},{16,56},{24,64},{32,72},{40,80},{48,88},{56,96},{64,... | collective-permute-start | bytes 393224 | tf_op jit(solution)/shard_map/ppermute | solution.py:174
  57.1 17.5 %collective-permute-start.5 = (bf16[4,128,1,128]{3,1,2,0:T(8,128)(2,1)}, bf16[4,128,1,128]{3,1,2,0:T(8,128)(2,1)S(1)}, u32[]{:S(2)}, u32[]{:S(2)}) collective-permute-start(bf16[4,128,1,128]{3,1,2,0:T(8,128)(2,1)} %param.19), channel_id=1, source_target_pairs={{0,48},{8,56},{16,64},{24,72},{32,80},{40,88},{48,96},{56,104},{64... | collective-permute-start | bytes 393224 | tf_op jit(solution)/shard_map/ppermute | solution.py:174
  61.2 17.2 %collective-permute-start.6 = (bf16[4,128,1,128]{3,1,2,0:T(8,128)(2,1)}, bf16[4,128,1,128]{3,1,2,0:T(8,128)(2,1)S(1)}, u32[]{:S(2)}, u32[]{:S(2)}) collective-permute-start(bf16[4,128,1,128]{3,1,2,0:T(8,128)(2,1)} %param.19), channel_id=1, source_target_pairs={{0,56},{8,64},{16,72},{24,80},{32,88},{40,96},{48,104},{56,112},{6... | collective-permute-start | bytes 393224 | tf_op jit(solution)/shard_map/ppermute | solution.py:174
  66.4 12.9 %collective-permute-start.7 = (bf16[4,128,1,128]{3,1,2,0:T(8,128)(2,1)}, bf16[4,128,1,128]{3,1,2,0:T(8,128)(2,1)S(1)}, u32[]{:S(2)}, u32[]{:S(2)}) collective-permute-start(bf16[4,128,1,128]{3,1,2,0:T(8,128)(2,1)} %param.19), channel_id=1, source_target_pairs={{0,64},{8,72},{16,80},{24,88},{32,96},{40,104},{48,112},{56,120},{... | collective-permute-start | bytes 393224 | tf_op jit(solution)/shard_map/ppermute | solution.py:174
  68.5 11.5 %collective-permute-start.8 = (bf16[4,128,1,128]{3,1,2,0:T(8,128)(2,1)}, bf16[4,128,1,128]{3,1,2,0:T(8,128)(2,1)S(1)}, u32[]{:S(2)}, u32[]{:S(2)}) collective-permute-start(bf16[4,128,1,128]{3,1,2,0:T(8,128)(2,1)} %param.19), channel_id=1, source_target_pairs={{0,72},{8,80},{16,88},{24,96},{32,104},{40,112},{48,120},{56,0},{6... | collective-permute-start | bytes 393224 | tf_op jit(solution)/shard_map/ppermute | solution.py:174
  70.1 11.8 %collective-permute-start.9 = (bf16[4,128,1,128]{3,1,2,0:T(8,128)(2,1)S(1)}, bf16[4,128,1,128]{3,1,2,0:T(8,128)(2,1)S(1)}, u32[]{:S(2)}, u32[]{:S(2)}) collective-permute-start(bf16[4,128,1,128]{3,1,2,0:T(8,128)(2,1)S(1)} %copy-done.8), channel_id=1, source_target_pairs={{0,80},{8,88},{16,96},{24,104},{32,112},{40,120},{48,0},{56,8},{64... | collective-permute-start | bytes 393224 | tf_op jit(solution)/shard_map/ppermute | solution.py:174
  74.6 10.6 %collective-permute-start.10 = (bf16[4,128,1,128]{3,1,2,0:T(8,128)(2,1)S(1)}, bf16[4,128,1,128]{3,1,2,0:T(8,128)(2,1)S(1)}, u32[]{:S(2)}, u32[]{:S(2)}) collective-permute-start(bf16[4,128,1,128]{3,1,2,0:T(8,128)(2,1)S(1)} %copy-done.8), channel_id=1, source_target_pairs={{0,88},{8,96},{16,104},{24,112},{32,120},{40,0},{48,8},{56,16},{64... | collective-permute-start | bytes 393224 | tf_op jit(solution)/shard_map/ppermute | solution.py:174
  78.4 7.5 %collective-permute-start.11 = (bf16[4,128,1,128]{3,1,2,0:T(8,128)(2,1)S(1)}, bf16[4,128,1,128]{3,1,2,0:T(8,128)(2,1)S(1)}, u32[]{:S(2)}, u32[]{:S(2)}) collective-permute-start(bf16[4,128,1,128]{3,1,2,0:T(8,128)(2,1)S(1)} %copy-done.8), channel_id=1, source_target_pairs={{0,96},{8,104},{16,112},{24,120},{32,0},{40,8},{48,16},{56,24},{64... | collective-permute-start | bytes 393224 | tf_op jit(solution)/shard_map/ppermute | solution.py:174
  79.4 7.2 %collective-permute-start.12 = (bf16[4,128,1,128]{3,1,2,0:T(8,128)(2,1)S(1)}, bf16[4,128,1,128]{3,1,2,0:T(8,128)(2,1)S(1)}, u32[]{:S(2)}, u32[]{:S(2)}) collective-permute-start(bf16[4,128,1,128]{3,1,2,0:T(8,128)(2,1)S(1)} %copy-done.8), channel_id=1, source_target_pairs={{0,104},{8,112},{16,120},{24,0},{32,8},{40,16},{48,24},{56,32},{64... | collective-permute-start | bytes 393224 | tf_op jit(solution)/shard_map/ppermute | solution.py:174
  80.0 8.2 %collective-permute-start.13 = (bf16[4,128,1,128]{3,1,2,0:T(8,128)(2,1)S(1)}, bf16[4,128,1,128]{3,1,2,0:T(8,128)(2,1)S(1)}, u32[]{:S(2)}, u32[]{:S(2)}) collective-permute-start(bf16[4,128,1,128]{3,1,2,0:T(8,128)(2,1)S(1)} %copy-done.8), channel_id=1, source_target_pairs={{0,112},{8,120},{16,0},{24,8},{32,16},{40,24},{48,32},{56,40},{64,... | collective-permute-start | bytes 393224 | tf_op jit(solution)/shard_map/ppermute | solution.py:174
  81.9 9.2 %collective-permute-start.14 = (bf16[4,128,1,128]{3,1,2,0:T(8,128)(2,1)S(1)}, bf16[4,128,1,128]{3,1,2,0:T(8,128)(2,1)S(1)}, u32[]{:S(2)}, u32[]{:S(2)}) collective-permute-start(bf16[4,128,1,128]{3,1,2,0:T(8,128)(2,1)S(1)} %copy-done.8), channel_id=1, source_target_pairs={{0,120},{8,0},{16,8},{24,16},{32,24},{40,32},{48,40},{56,48},{64,5... | collective-permute-start | bytes 393224 | tf_op jit(solution)/shard_map/ppermute | solution.py:174
  100.4 3.6 %copy-start.4 = (bf16[768,2880]{0,1:T(8,128)(2,1)S(1)}, bf16[768,2880]{0,1:T(8,128)(2,1)}, u32[]{:S(2)}) copy-start(bf16[768,2880]{0,1:T(8,128)(2,1)} %all-gather.6.cloned.1.call-done) | copy-start | bytes 13271044
  107.2 6.1 %copy-start.6 = (f32[768,32]{0,1:T(8,128)S(1)}, f32[768,32]{0,1:T(8,128)}, u32[]{:S(2)}) copy-start(f32[768,32]{0,1:T(8,128)} %get-tuple-element.11) | copy-start | bytes 294916
  107.2 6.1 %copy-start.7 = (f32[768,32]{0,1:T(8,128)S(1)}, f32[768,32]{0,1:T(8,128)}, u32[]{:S(2)}) copy-start(f32[768,32]{0,1:T(8,128)} %get-tuple-element.12) | copy-start | bytes 294916
  168.2 41.1 %copy-start.3 = (bf16[768,360]{0,1:T(8,128)(2,1)S(1)}, bf16[768,360]{0,1:T(8,128)(2,1)}, u32[]{:S(2)}) copy-start(bf16[768,360]{0,1:T(8,128)(2,1)} %copy.33) | copy-start | bytes 1658884
  168.3 43.4 %copy-start.10 = (bf16[2880]{0:T(1024)(128)(2,1)S(1)}, bf16[2880]{0:T(1024)(128)(2,1)}, u32[]{:S(2)}) copy-start(bf16[2880]{0:T(1024)(128)(2,1)} %param.26) | copy-start | bytes 17284
  168.3 75.4 %all-gather.4.cloned.1.call-start = ((), (), s32[]{:S(2)}) async-start(), calls=%async_computation.5 | async-start | bytes 4976640 | tf_op jit(solution)/shard_map/all_gather | solution.py:269
  209.4 37.7 %copy-start.13 = (bf16[2880,360]{0,1:T(8,128)(2,1)S(1)}, bf16[2880,360]{0,1:T(8,128)(2,1)}, u32[]{:S(2)}) copy-start(bf16[2880,360]{0,1:T(8,128)(2,1)} %param.27) | copy-start | bytes 6220804
  211.6 88.7 %reduce-scatter.5.cloned.1.call-start = ((), (), s32[]{:S(2)}) async-start(), calls=%async_computation.6 | async-start | bytes 4976640 | tf_op jit(solution)/shard_map/reduce_scatter | solution.py:274
  243.7 3.6 %copy-start.5 = (bf16[768,2880]{0,1:T(8,128)(2,1)S(1)}, bf16[768,2880]{0,1:T(8,128)(2,1)}, u32[]{:S(2)}) copy-start(bf16[768,2880]{0,1:T(8,128)(2,1)} %all-gather.4.cloned.1.call-done) | copy-start | bytes 13271044
  261.7 38.6 %copy-start.2 = (bf16[768,360]{0,1:T(8,128)(2,1)S(1)}, bf16[768,360]{0,1:T(8,128)(2,1)}, u32[]{:S(2)}) copy-start(bf16[768,360]{0,1:T(8,128)(2,1)} %add_convert_fusion.1) | copy-start | bytes 1658884
  307.8 34.3 %copy-start.1 = (bf16[512,2880]{0,1:T(8,128)(2,1)S(1)}, bf16[512,2880]{0,1:T(8,128)(2,1)}, u32[]{:S(2)}) copy-start(bf16[512,2880]{0,1:T(8,128)(2,1)} %param.25) | copy-start | bytes 8847364
  310.6 28.3 %all-to-all-start.1 = ((bf16[16,112,360]{2,1,0:T(8,128)(2,1)}), bf16[16,112,360]{2,1,0:T(8,128)(2,1)}, u32[]{:S(2)}, u32[]{:S(2)}) async-start(bf16[16,112,360]{2,1,0:T(8,128)(2,1)} %broadcast_select_fusion), calls=%async_computation.3 | async-start | bytes 2752512 | tf_op jit(solution)/shard_map/all_to_all | solution.py:282
Sparse Core Ops, SparseCore 0:
  45.8 32.3 all-gather.5
  168.4 40.9 reduce-scatter.2
  211.7 31.9 all-gather.3
  261.8 38.4 reduce-scatter.4

commit v5 on v3

--- a/solution.py
+++ b/solution.py
@@ -159,18 +159,20 @@
     home_row = jnp.sum(
         jnp.where(block_of_slot[None, :] == catalog[:, None], catalog[None, :], 0), axis=1
     )
-    wanted = attach_slots[:, None] - window + jnp.arange(window)[None, :]
-    block_id = wanted // block_len
-    tail_store = jnp.sum(jnp.where(block_id[..., None] == catalog, home_row, 0), axis=-1)
-    tail_offset = wanted - block_id * block_len
-    trailing = prefix_cache.shape[2:]
-    initial = jnp.zeros((attach_slots.shape[0], window) + trailing, jnp.bfloat16)
+    first_block = jnp.clip((attach_slots - window) // block_len, 0, total_blocks - 1)
+    second_block = jnp.clip(first_block + 1, 0, total_blocks - 1)
+    offset = attach_slots - window - first_block * block_len
     shard_rows = lax.all_gather(prefix_cache, "req", axis=0, tiled=True)
-    held_blocks = shard_rows.shape[0]
-    flat_rows = shard_rows.reshape((held_blocks * block_len,) + trailing)
-    inside = (tail_store >= 0) & (tail_store < held_blocks)
-    picked = flat_rows[jnp.clip(tail_store, 0, held_blocks - 1) * block_len + tail_offset]
-    return jnp.where(inside[..., None, None], picked, initial)
+    shard_rows = shard_rows.reshape(total_blocks, block_len, -1)
+    pair = jnp.stack([home_row[first_block], home_row[second_block]], axis=1)
+    both = shard_rows[pair].reshape(attach_slots.shape[0], 2 * block_len, -1)
+    picks = (
+        jnp.arange(2 * block_len)[None, None, :]
+        == offset[:, None, None] + jnp.arange(window)[None, :, None]
+    ).astype(jnp.bfloat16)
+    return jnp.einsum(
+        "ruk,rkd->rud", picks, both, preferred_element_type=jnp.float32
+    ).astype(jnp.bfloat16)
 
 
 def local(
@@ -219,8 +221,19 @@
     slot_source = jnp.clip(starts[:, None] + slot_steps[None, :], 0, CAP - 1).reshape(-1)
     live_mask = slot_steps[None, :] < arriving_lengths[:, None]
 
+    slot_pick = (
+        (jnp.arange(CAP)[None, :] == slot_source[:, None]) & live_mask.reshape(-1)[:, None]
+    ).astype(jnp.bfloat16)
+    pack_pick = (
+        jnp.arange(peers * slot_length)[None, :] == flat_index[:, None]
+    ).astype(jnp.bfloat16)
+
     def to_slots(values):
-        return values[slot_source].reshape((peers, slot_length) + values.shape[1:])
+        moved = jnp.dot(slot_pick, values, preferred_element_type=jnp.float32)
+        return moved.astype(values.dtype).reshape((peers, slot_length) + values.shape[1:])
+
+    def to_packed(values):
+        return jnp.dot(pack_pick, values, preferred_element_type=jnp.float32).astype(values.dtype)
 
     tail_rows = fetch_prefix(arriving_attach, prefix_cache, block_of_slot, WINDOW)
     my_features = lax.dynamic_slice_in_dim(
@@ -229,7 +242,7 @@
     landed = lax.all_to_all(
         my_features[send_order], "req", split_axis=0, concat_axis=0, tiled=True
     )
-    input_part = landed.reshape(peers * slot_length, feature_share)[flat_index]
+    input_part = to_packed(landed.reshape(peers * slot_length, feature_share))
     input_rows = lax.all_gather(input_part, "tp", axis=1, tiled=True)
     row_total = input_part.shape[0]
     normed_in = norm_rows(input_rows, attn_gain)
@@ -245,9 +258,10 @@
     attended = attend_pallas(
         to_slots(queries.reshape(row_total, -1)),
         to_slots(paired.reshape(row_total, -1)),
-        tail_rows.reshape(peers, WINDOW, -1),
+        tail_rows,
         sink_logits,
-    ).reshape(peers * slot_length, -1)[flat_index]
+    ).reshape(peers * slot_length, -1)
+    attended = to_packed(attended)
     partial_value = jnp.dot(attended, w_out, preferred_element_type=jnp.float32)
     summed = lax.psum_scatter(
         partial_value.astype(jnp.bfloat16), "tp", scatter_dimension=1, tiled=True
@@ -265,7 +279,7 @@
         tiled=True,
     ).astype(jnp.float32)
     out_rows = (residual_part.astype(jnp.float32) + down_sum).astype(jnp.bfloat16)
-    out_slots = jnp.where(live_mask[..., None], to_slots(out_rows), jnp.zeros((), jnp.bfloat16))
+    out_slots = to_slots(out_rows)
     returned = lax.all_to_all(out_slots, "req", split_axis=0, concat_axis=0, tiled=True)
     return returned[my_row]
 

time: 346 us -> 329 us (0.951)
  local copies, waits for them, and re-layouts: 50.9 us -> 20.5 us
  matrix products: 28.7 us -> 45.8 us
  other arithmetic: 22.2 us -> 13.7 us
  waiting for transfers between devices: 187 us -> 191 us
    gather x7 -> x3, local copies, waits for them, and re-layouts: 35.6 us -> 4.57 us  [the longest x1 3.24 us: fetch_prefix(): both = shard_rows[pair].reshape(attach_slots.shape[0], 2 * block_len, -1)]
    dot_general x0 -> x5, matrix products: none -> 16.5 us  [the longest x3 10.3 us: to_slots(): moved = jnp.dot(slot_pick, values, preferred_element_type=jnp.float32)]
    select_n x6 -> x2, other arithmetic: 4.15 us -> 0.03 us  [the longest x1 0.02 us: fetch_prefix(): pair = jnp.stack([home_row[first_block], home_row[second_block]], axis=1)]
where the time goes in v5:
time: 329 us; the launch traced here: 328 us
  waiting for transfers between devices  191 us (58%)
  matrix products  45.8 us (14%)
  Pallas kernels  28.7 us (9%)
  local copies, waits for them, and re-layouts  20.5 us (6%)
  starting transfers between devices  14.9 us (5%)
  other arithmetic  13.7 us (4%)
  between operations  13.4 us (4%)
    reduce_scatter x1, waiting for transfers between devices, local(): lax.psum_scatter(jnp.dot(hidden, w_down, preferred_element_type=jnp.float...  38.6 us
    reduce_scatter x1, waiting for transfers between devices, local(): lax.psum_scatter(partial_value.astype(jnp.bfloat16), 'tp', scatter_dimens...  38.5 us
    all_gather x1, waiting for transfers between devices, local(): residual = lax.all_gather(residual_part, 'tp', axis=1, tiled=True)  31.9 us
    pallas_call x1, Pallas kernels, attend_pallas(): pl.pallas_call(attend_kernel, grid=(peers,), in_specs=[pl.BlockSpec(memor...  28.7 us
    all_gather x1, waiting for transfers between devices, local(): input_rows = lax.all_gather(input_part, 'tp', axis=1, tiled=True)  28.3 us
    all_to_all x1, waiting for transfers between devices, local(): lax.all_to_all(out_slots, 'req', split_axis=0, concat_axis=0, tiled=True)  20.8 us
    all_to_all x1, waiting for transfers between devices, local(): lax.all_to_all(my_features[send_order], 'req', split_axis=0, concat_axis=...  19.8 us
    all_gather x1, waiting for transfers between devices, fetch_prefix(): shard_rows = lax.all_gather(prefix_cache, 'req', axis=0, tiled=True)  12.3 us
  transfers between devices with their start and end apart: 7, of which 7 were waited for; matrix products, arithmetic and copies ran while one was open for 8% of the time, Pallas kernels for 0%

profile of v5, /device:TPU:7, one launch (start us, length us, event | category | flops | bytes accessed | tf_op | source)
XLA Modules:
  0.0 327.9 jit_solution(6854022663121294813)
XLA Ops:
  6.5 0.7 all-gather.6.cloned.1.call-update
  7.3 0.9 reshape.525
  8.2 0.7 fusion.74
  8.9 0.1 select_reduce_fusion.4
  9.0 0.8 select_reduce_fusion.3
  9.8 3.2 constant_dynamic-slice_fusion.1
  13.0 3.2 gather_fusion
  16.2 7.8 %all-to-all-start = ((bf16[16,112,360]{2,1,0:T(8,128)(2,1)}), bf16[16,112,360]{2,1,0:T(8,128)(2,1)}, u32[]{:S(2)}, u32[]{:S(2)}) async-start(bf16[16,112,360]{2,1,0:T(8,128)(2,1)} %gather_fusion), calls=%async_computation | async-start | bytes 2752512 | tf_op jit(solution)/shard_map/all_to_all | solution.py:242
  24.0 0.0 all-gather.4.cloned.1.call-start
  24.1 0.7 fusion.87
  24.8 0.1 copy.24
  24.9 0.1 reduce
  25.0 0.1 convert_reduce_fusion
  25.1 0.7 fusion.72
  25.8 0.1 select_reduce_fusion
  25.9 19.8 %all-to-all-done = bf16[16,112,360]{2,1,0:T(8,128)(2,1)} async-done(((bf16[16,112,360]{2,1,0:T(8,128)(2,1)}), bf16[16,112,360]{2,1,0:T(8,128)(2,1)}, u32[]{:S(2)}, u32[]{:S(2)}) %all-to-all-start) | async-done | bytes 1290272 | tf_op jit(solution)/shard_map/all_to_all | solution.py:242
  45.7 3.7 %fusion.35 = bf16[768,360]{0,1:T(8,128)(2,1)} fusion(bf16[1792,360]{1,0:T(8,128)(2,1)} %bitcast.6, s32[768]{0:T(1024)S(1)} %get-tuple-element.14), kind=kOutput, calls=%fused_computation.41 | convolution fusion | flops 992557056 | bytes 1846272 | tf_op jit(solution)/shard_map/dot_general | solution.py:236
  49.4 0.0 all-gather.4.cloned.1.call-update
  49.4 0.0 reduce-scatter.3.cloned.1.call-start
  49.5 0.7 bitcast_subtract_fusion.1
  50.2 0.1 add_clamp_fusion
  50.2 0.1 min.28
  50.3 0.7 fusion.86
  51.0 0.1 iota_compare_fusion.18
  51.1 0.1 lt.82
  51.2 0.1 select_reduce_fusion.2
  51.3 0.7 gather_fusion.1
  52.0 0.7 gather_fusion.2
  52.7 0.1 copy.25
  52.8 0.1 reshape.560
  52.9 0.1 iota_add_fusion
  53.0 0.4 multiply_cosine_fusion.1
  53.4 12.3 %all-gather.6.cloned.1.call-done = bf16[64,128,1,128]{3,1,2,0:T(8,128)(2,1)} async-done(((bf16[4,128,1,128]{3,1,2,0:T(8,128)(2,1)}), bf16[64,128,1,128]{3,1,2,0:T(8,128)(2,1)}) %all-gather.6.cloned.1.call-update) | async-done | bytes 2097168 | tf_op jit(solution)/shard_map/all_gather | solution.py:165
  65.7 3.2 gather_fusion.3
  68.9 2.6 fusion.36.tail_ref
  71.5 28.3 %all-gather.4.cloned.1.call-done = bf16[768,2880]{0,1:T(8,128)(2,1)} async-done(((bf16[768,360]{0,1:T(8,128)(2,1)}), bf16[768,2880]{0,1:T(8,128)(2,1)}) %all-gather.4.cloned.1.call-update) | async-done | bytes 4423696 | tf_op jit(solution)/shard_map/all_gather | solution.py:246
  99.8 3.3 %fusion = f32[768]{0:T(1024)S(1)} fusion(bf16[768,2880]{0,1:T(8,128)(2,1)} %all-gather.4.cloned.1.call-done), kind=kLoop, calls=%fused_computation.9 | loop fusion | flops 6634752 | bytes 4426752 | tf_op jit(solution)/shard_map/reduce_sum | solution.py:18
  103.2 0.2 copy-done.1
  103.4 2.8 fusion.44
  106.2 0.4 fusion.67
  106.7 3.1 fusion.42
  109.8 0.2 subtract_convert_fusion
  110.0 0.1 pad_maximum_fusion
  110.1 3.5 %fusion.15 = bf16[1792,512]{1,0:T(8,128)(2,1)} fusion(bf16[768,512]{0,1:T(8,128)(2,1)S(1)} %bitcast.75, s32[1792]{0:T(1024)S(1)} %min.28, pred[1792]{0:T(1024)(128)(4,1)S(1)} %lt.82), kind=kOutput, calls=%fused_computation.25 | convolution fusion | flops 1412956160 | bytes 2630400 | tf_op jit(solution)/shard_map/dot_general | solution.py:232
  113.6 2.4 fusion.29
  116.0 28.7 %shard_map.145 = bf16[16,112,512]{2,1,0:T(8,128)(2,1)} custom-call(f32[8]{0:T(128)} %sink_ref.1, bf16[16,112,512]{2,1,0:T(8,128)(2,1)} %bitcast.79, bf16[16,112,128]{2,1,0:T(8,128)(2,1)} %bitcast.81, bf16[16,128,128]{2,1,0:T(8,128)(2,1)} %fusion.36.tail_ref), custom_call_target="tpu_custom_call" | custom-call | flops 880803840 | bytes 4653056 | tf_op jit(solution)/shard_map/pallas_call | solution.py:136
  144.7 7.4 %convolution_convert_fusion = bf16[768,2880]{0,1:T(8,128)(2,1)} fusion(bf16[512,2880]{0,1:T(8,128)(2,1)S(1)} %copy-done, bf16[1792,512]{1,0:T(8,128)(2,1)} %bitcast.80, s32[768]{0:T(1024)S(1)} %get-tuple-element.14), kind=kOutput, calls=%fused_computation.23 | convolution fusion | flops 3678191616 | bytes 9210880 | tf_op jit(solution)/shard_map/dot_general | solution.py:265
  152.2 0.0 all-gather.8.cloned.1.call-start
  152.3 38.5 %reduce-scatter.3.cloned.1.call-done = bf16[768,360]{0,1:T(8,128)(2,1)} async-done(((bf16[768,2880]{0,1:T(8,128)(2,1)}), bf16[768,360]{0,1:T(8,128)(2,1)}) %reduce-scatter.3.cloned.1.call-update) | async-done | bytes 552976 | tf_op jit(solution)/shard_map/reduce_scatter | solution.py:266
  190.8 2.0 add_convert_fusion.1
  192.8 0.0 all-gather.8.cloned.1.call-update
  192.9 0.3 reduce-scatter.5.cloned.1.call-start
  193.2 31.9 %all-gather.8.cloned.1.call-done = bf16[768,2880]{0,1:T(8,128)(2,1)} async-done(((bf16[768,360]{0,1:T(8,128)(2,1)}), bf16[768,2880]{0,1:T(8,128)(2,1)}) %all-gather.8.cloned.1.call-update) | async-done | bytes 4423696 | tf_op jit(solution)/shard_map/all_gather | solution.py:270
  225.0 3.3 %fusion.3 = f32[768]{0:T(1024)S(1)} fusion(bf16[768,2880]{0,1:T(8,128)(2,1)} %all-gather.8.cloned.1.call-done), kind=kLoop, calls=%fused_computation.12 | loop fusion | flops 6634752 | bytes 4426752 | tf_op jit(solution)/shard_map/reduce_sum | solution.py:18
  228.4 0.2 copy-done.2
  228.6 4.6 %fusion.38 = f32[768,360]{0,1:T(8,128)} fusion(bf16[2880,360]{0,1:T(8,128)(2,1)} %param.27, bf16[768,2880]{0,1:T(8,128)(2,1)S(1)} %copy-done.2, f32[2880]{0:T(1024)S(1)} %convert_element_type.116, f32[768]{0:T(1024)S(1)} %add_rsqrt_fusion), kind=kOutput, calls=%fused_computation.43 | convolution fusion | flops 1601372160 | bytes 7617792 | tf_op jit(solution)/shard_map/dot_general | solution.py:272
  233.2 11.3 %convolution_convert_fusion.1 = bf16[768,2880]{0,1:T(8,128)(2,1)} fusion(bf16[360,2880]{1,0:T(8,128)(2,1)} %param.29, bf16[2880,360]{0,1:T(8,128)(2,1)} %param.28, bf16[768,2880]{0,1:T(8,128)(2,1)} %all-gather.8.cloned.1.call-done, f32[2880]{0:T(1024)S(1)} %convert_element_type.116, f32[768]{0:T(1024)S(1)} %add_rsqrt_fusion, f32[768,360]{0,1:T(8,128)} %fusion.38), kind=kOutput, calls=%fused_computation.24 | convolution fusion | flops 3197767680 | bytes 14115072 | tf_op jit(solution)/shard_map/dot_general | solution.py:276
  244.6 38.6 %reduce-scatter.5.cloned.1.call-done = bf16[768,360]{0,1:T(8,128)(2,1)} async-done(((bf16[768,2880]{0,1:T(8,128)(2,1)}), bf16[768,360]{0,1:T(8,128)(2,1)}) %reduce-scatter.5.cloned.1.call-update) | async-done | bytes 552976 | tf_op jit(solution)/shard_map/reduce_scatter | solution.py:275
  283.1 4.3 %fusion.18 = bf16[1792,360]{0,1:T(8,128)(2,1)} fusion(s32[1792]{0:T(1024)S(1)} %min.28, pred[1792]{0:T(1024)(128)(4,1)S(1)} %lt.82, bf16[768,360]{0,1:T(8,128)(2,1)} %reduce-scatter.5.cloned.1.call-done, bf16[768,360]{0,1:T(8,128)(2,1)S(1)} %copy-done.4), kind=kOutput, calls=%fused_computation.26 | convolution fusion | flops 995407872 | bytes 2405120 | tf_op jit(solution)/shard_map/dot_general | solution.py:232
  287.5 2.5 copy.26
  289.9 6.7 %all-to-all-start.1 = ((bf16[16,112,360]{2,1,0:T(8,128)(2,1)}), bf16[16,112,360]{2,1,0:T(8,128)(2,1)}, u32[]{:S(2)}, u32[]{:S(2)}) async-start(bf16[16,112,360]{2,1,0:T(8,128)(2,1)} %bitcast.72), calls=%async_computation.3 | async-start | bytes 2752512 | tf_op jit(solution)/shard_map/all_to_all | solution.py:283
  296.7 0.7 fusion.71
  297.4 20.8 %all-to-all-done.1 = bf16[16,112,360]{2,1,0:T(8,128)(2,1)} async-done(((bf16[16,112,360]{2,1,0:T(8,128)(2,1)}), bf16[16,112,360]{2,1,0:T(8,128)(2,1)}, u32[]{:S(2)}, u32[]{:S(2)}) %all-to-all-start.1) | async-done | bytes 1290272 | tf_op jit(solution)/shard_map/all_to_all | solution.py:283
  318.2 3.2 gather_fusion.4
  (35 shorter events, 0.2 us)
Async XLA Ops:
  6.5 138.2 %copy-start = (bf16[512,2880]{0,1:T(8,128)(2,1)S(1)}, bf16[512,2880]{0,1:T(8,128)(2,1)}, u32[]{:S(2)}) copy-start(bf16[512,2880]{0,1:T(8,128)(2,1)} %param.25) | copy-start | bytes 8847364
  6.5 59.2 %all-gather.6.cloned.1.call-start = ((), (), s32[]{:S(2)}) async-start(), calls=%async_computation.5 | async-start | bytes 2228224 | tf_op jit(solution)/shard_map/all_gather | solution.py:165
  16.2 29.5 %all-to-all-start = ((bf16[16,112,360]{2,1,0:T(8,128)(2,1)}), bf16[16,112,360]{2,1,0:T(8,128)(2,1)}, u32[]{:S(2)}, u32[]{:S(2)}) async-start(bf16[16,112,360]{2,1,0:T(8,128)(2,1)} %gather_fusion), calls=%async_computation | async-start | bytes 2752512 | tf_op jit(solution)/shard_map/all_to_all | solution.py:242
  24.0 75.8 %all-gather.4.cloned.1.call-start = ((), (), s32[]{:S(2)}) async-start(), calls=%async_computation.4 | async-start | bytes 4976640 | tf_op jit(solution)/shard_map/all_gather | solution.py:246
  45.7 3.8 %copy-start.5 = (bf16[2880]{0:T(1024)(128)(2,1)S(1)}, bf16[2880]{0:T(1024)(128)(2,1)}, u32[]{:S(2)}) copy-start(bf16[2880]{0:T(1024)(128)(2,1)} %param.22) | copy-start | bytes 17284
  45.7 5.5 %copy-start.8 = (s32[64]{0:T(128)S(1)}, s32[64]{0:T(128)}, u32[]{:S(2)}) copy-start(s32[64]{0:T(128)} %param.20) | copy-start | bytes 772
  49.4 141.4 %reduce-scatter.3.cloned.1.call-start = ((), (), s32[]{:S(2)}) async-start(), calls=%async_computation.6 | async-start | bytes 4976640 | tf_op jit(solution)/shard_map/reduce_scatter | solution.py:266
  99.8 3.6 %copy-start.1 = (bf16[768,2880]{0,1:T(8,128)(2,1)S(1)}, bf16[768,2880]{0,1:T(8,128)(2,1)}, u32[]{:S(2)}) copy-start(bf16[768,2880]{0,1:T(8,128)(2,1)} %all-gather.4.cloned.1.call-done) | copy-start | bytes 13271044
  103.4 3.3 %copy-start.7 = (bf16[2880,512]{1,0:T(8,128)(2,1)S(1)}, bf16[2880,512]{1,0:T(8,128)(2,1)}, u32[]{:S(2)}) copy-start(bf16[2880,512]{1,0:T(8,128)(2,1)} %param.23) | copy-start | bytes 8847364
  152.2 38.6 %copy-start.3 = (bf16[768,360]{0,1:T(8,128)(2,1)S(1)}, bf16[768,360]{0,1:T(8,128)(2,1)}, u32[]{:S(2)}) copy-start(bf16[768,360]{0,1:T(8,128)(2,1)} %fusion.35) | copy-start | bytes 1658884
  152.2 40.9 %copy-start.6 = (bf16[2880]{0:T(1024)(128)(2,1)S(1)}, bf16[2880]{0:T(1024)(128)(2,1)}, u32[]{:S(2)}) copy-start(bf16[2880]{0:T(1024)(128)(2,1)} %param.26) | copy-start | bytes 17284
  152.2 72.8 %all-gather.8.cloned.1.call-start = ((), (), s32[]{:S(2)}) async-start(), calls=%async_computation.7 | async-start | bytes 4976640 | tf_op jit(solution)/shard_map/all_gather | solution.py:270
  192.9 90.3 %reduce-scatter.5.cloned.1.call-start = ((), (), s32[]{:S(2)}) async-start(), calls=%async_computation.8 | async-start | bytes 4976640 | tf_op jit(solution)/shard_map/reduce_scatter | solution.py:275
  225.0 3.6 %copy-start.2 = (bf16[768,2880]{0,1:T(8,128)(2,1)S(1)}, bf16[768,2880]{0,1:T(8,128)(2,1)}, u32[]{:S(2)}) copy-start(bf16[768,2880]{0,1:T(8,128)(2,1)} %all-gather.8.cloned.1.call-done) | copy-start | bytes 13271044
  244.5 38.6 %copy-start.4 = (bf16[768,360]{0,1:T(8,128)(2,1)S(1)}, bf16[768,360]{0,1:T(8,128)(2,1)}, u32[]{:S(2)}) copy-start(bf16[768,360]{0,1:T(8,128)(2,1)} %add_convert_fusion.1) | copy-start | bytes 1658884
  289.9 28.3 %all-to-all-start.1 = ((bf16[16,112,360]{2,1,0:T(8,128)(2,1)}), bf16[16,112,360]{2,1,0:T(8,128)(2,1)}, u32[]{:S(2)}, u32[]{:S(2)}) async-start(bf16[16,112,360]{2,1,0:T(8,128)(2,1)} %bitcast.72), calls=%async_computation.3 | async-start | bytes 2752512 | tf_op jit(solution)/shard_map/all_to_all | solution.py:283
Sparse Core Ops, SparseCore 0:
  9.5 56.1 all-gather.5
  67.4 32.3 all-gather.3
  152.3 38.4 reduce-scatter.2
  193.0 31.9 all-gather.7
  244.7 38.4 reduce-scatter.4

commit v6 on v5

--- a/solution.py
+++ b/solution.py
@@ -6,6 +6,7 @@
 from jax.experimental.pallas import tpu as pltpu
 
 WINDOW = 128
+TP = ("x", "core")
 CAP = 768
 
 
@@ -175,6 +176,25 @@
     ).astype(jnp.bfloat16)
 
 
+def gather_features(part):
+    chips = lax.axis_size("x")
+    cores = lax.axis_size("core")
+    rows, share = part.shape
+    across = lax.all_gather(part, "x", axis=1, tiled=True)
+    both = lax.all_gather(across, "core", axis=1, tiled=True)
+    return both.reshape(rows, cores, chips, share).transpose(0, 2, 1, 3).reshape(rows, -1)
+
+
+def scatter_features(whole):
+    chips = lax.axis_size("x")
+    cores = lax.axis_size("core")
+    rows, width = whole.shape
+    share = width // (chips * cores)
+    ordered = whole.reshape(rows, chips, cores, share).transpose(0, 2, 1, 3).reshape(rows, -1)
+    inside = lax.psum_scatter(ordered, "core", scatter_dimension=1, tiled=True)
+    return lax.psum_scatter(inside, "x", scatter_dimension=1, tiled=True)
+
+
 def local(
     suffix_tokens,
     route_lengths,
@@ -193,9 +213,9 @@
     w_down,
 ):
     peers = lax.axis_size("req")
-    splits = lax.axis_size("tp")
+    splits = lax.axis_size(("x", "core"))
     request_index = lax.axis_index("req")
-    tensor_index = lax.axis_index("tp")
+    tensor_index = lax.axis_index(("x", "core"))
     slot_count, slot_length, features = suffix_tokens.shape
     feature_share = features // splits
     value_heads = w_keyval.shape[1]
@@ -243,7 +263,7 @@
         my_features[send_order], "req", split_axis=0, concat_axis=0, tiled=True
     )
     input_part = to_packed(landed.reshape(peers * slot_length, feature_share))
-    input_rows = lax.all_gather(input_part, "tp", axis=1, tiled=True)
+    input_rows = gather_features(input_part)
     row_total = input_part.shape[0]
     normed_in = norm_rows(input_rows, attn_gain)
     queries = jnp.dot(normed_in, w_query, preferred_element_type=jnp.float32).reshape(
@@ -263,20 +283,15 @@
     ).reshape(peers * slot_length, -1)
     attended = to_packed(attended)
     partial_value = jnp.dot(attended, w_out, preferred_element_type=jnp.float32)
-    summed = lax.psum_scatter(
-        partial_value.astype(jnp.bfloat16), "tp", scatter_dimension=1, tiled=True
-    ).astype(jnp.float32)
+    summed = scatter_features(partial_value.astype(jnp.bfloat16)).astype(jnp.float32)
     residual_part = (input_part.astype(jnp.float32) + summed).astype(jnp.bfloat16)
-    residual = lax.all_gather(residual_part, "tp", axis=1, tiled=True)
+    residual = gather_features(residual_part)
     normed_mid = norm_rows(residual, mlp_gain)
     gate_proj = jnp.dot(normed_mid, w_gate, preferred_element_type=jnp.float32)
     up_proj = jnp.dot(normed_mid, w_up, preferred_element_type=jnp.float32)
     hidden = (jax.nn.silu(gate_proj) * up_proj).astype(jnp.bfloat16)
-    down_sum = lax.psum_scatter(
-        jnp.dot(hidden, w_down, preferred_element_type=jnp.float32).astype(jnp.bfloat16),
-        "tp",
-        scatter_dimension=1,
-        tiled=True,
+    down_sum = scatter_features(
+        jnp.dot(hidden, w_down, preferred_element_type=jnp.float32).astype(jnp.bfloat16)
     ).astype(jnp.float32)
     out_rows = (residual_part.astype(jnp.float32) + down_sum).astype(jnp.bfloat16)
     out_slots = to_slots(out_rows)
@@ -285,22 +300,26 @@
 
 
 def solution(mesh):
+    chips = mesh.shape["tp"] // 2
+    split_mesh = jax.sharding.Mesh(
+        mesh.devices.reshape(mesh.shape["req"], chips, 2), ("req", "x", "core")
+    )
     in_specs = (
         P("req", None, None),
         P(),
         P(),
         P(),
-        P("req", None, "tp", None),
-        P(),
-        P("tp"),
-        P(),
-        P(None, "tp"),
-        P(None, "tp", None),
-        P("tp", None),
-        P(),
-        P(None, "tp"),
-        P(None, "tp"),
-        P("tp", None),
-    )
-    out_specs = P("req", None, "tp")
-    return jax.shard_map(local, mesh=mesh, in_specs=in_specs, out_specs=out_specs, check_vma=False)
+        P("req", None, TP, None),
+        P(),
+        P(TP),
+        P(),
+        P(None, TP),
+        P(None, TP, None),
+        P(TP, None),
+        P(),
+        P(None, TP),
+        P(None, TP),
+        P(TP, None),
+    )
+    out_specs = P("req", None, TP)
+    return jax.shard_map(local, mesh=split_mesh, in_specs=in_specs, out_specs=out_specs, check_vma=False)

time: 329 us -> 426 us (1.29); the launches traced: 328 us -> 420 us
  waiting for transfers between devices: 191 us -> 268 us
  local copies, waits for them, and re-layouts: 20.5 us -> 40.6 us
  matrix products: 45.8 us -> 40.4 us
    all_gather x2 -> x4, waiting for transfers between devices: 60.2 us -> 96.1 us  [the longest x2 61.3 us: gather_features(): across = lax.all_gather(part, 'x', axis=1, tiled=True)]
    all_gather x1, waiting for transfers between devices: 12.3 us -> 38.9 us  [fetch_prefix(): shard_rows = lax.all_gather(prefix_cache, 'req', axis=0, tiled=True)]
    reduce_scatter x2 -> x4, waiting for transfers between devices: 77.1 us -> 96.8 us  [the longest x2 64.1 us: scatter_features(): return lax.psum_scatter(inside, 'x', scatter_dimension=1, tiled=True)]
    reshape x2 -> x4, local copies, waits for them, and re-layouts: 0.78 us -> 10.1 us  [the longest x2 9.27 us: scatter_features(): whole.reshape(rows, chips, cores, share).transpose(0, 2, 1, 3)]
    unnamed x18 -> x27, local copies, waits for them, and re-layouts: 0.48 us -> 8.65 us
  transfers between devices with their start and end apart: 7 -> 11, of which waited for: 7 -> 11; matrix products, arithmetic and copies ran while one was open for 8% -> 4% of each run, Pallas kernels for 0% -> 0%
where the time goes in v6:
time: 426 us; the launch traced here: 420 us
  waiting for transfers between devices  268 us (63%)
  local copies, waits for them, and re-layouts  40.6 us (10%)
  matrix products  40.4 us (9%)
  Pallas kernels  28.7 us (7%)
  starting transfers between devices  15.4 us (4%)
  other arithmetic  13.7 us (3%)
  between operations  13.5 us (3%)
    reduce_scatter x2, waiting for transfers between devices, scatter_features(): return lax.psum_scatter(inside, 'x', scatter_dimension=1, tiled=True)  64.1 us
    all_gather x2, waiting for transfers between devices, gather_features(): across = lax.all_gather(part, 'x', axis=1, tiled=True)  61.3 us
    all_gather x1, waiting for transfers between devices, fetch_prefix(): shard_rows = lax.all_gather(prefix_cache, 'req', axis=0, tiled=True)  38.9 us
    all_gather x2, waiting for transfers between devices, gather_features(): both = lax.all_gather(across, 'core', axis=1, tiled=True)  34.8 us
    reduce_scatter x2, waiting for transfers between devices, scatter_features(): inside = lax.psum_scatter(ordered, 'core', scatter_dimension=1, tiled=True)  32.7 us
    pallas_call x1, Pallas kernels, attend_pallas(): pl.pallas_call(attend_kernel, grid=(peers,), in_specs=[pl.BlockSpec(memor...  28.7 us
    all_to_all x1, waiting for transfers between devices, local(): lax.all_to_all(out_slots, 'req', split_axis=0, concat_axis=0, tiled=True)  18.2 us
    all_to_all x1, waiting for transfers between devices, local(): lax.all_to_all(my_features[send_order], 'req', split_axis=0, concat_axis=...  17.1 us
  transfers between devices with their start and end apart: 11, of which 11 were waited for; matrix products, arithmetic and copies ran while one was open for 4% of the time, Pallas kernels for 0%

profile of v6, /device:TPU:7, one launch (start us, length us, event | category | flops | bytes accessed | tf_op | source)
XLA Modules:
  0.0 420.2 jit_solution(3428056236279177331)
XLA Ops:
  6.5 0.9 reshape.569
  7.4 0.8 select_reduce_fusion.3
  8.3 0.7 fusion.62
  9.0 0.1 select_reduce_fusion.4
  9.1 3.2 constant_dynamic-slice_fusion.1
  12.3 3.2 gather_fusion
  15.5 7.8 %all-to-all-start = ((bf16[16,112,360]{2,1,0:T(8,128)(2,1)}), bf16[16,112,360]{2,1,0:T(8,128)(2,1)}, u32[]{:S(2)}, u32[]{:S(2)}) async-start(bf16[16,112,360]{2,1,0:T(8,128)(2,1)} %gather_fusion), calls=%async_computation | async-start | bytes 2752512 | tf_op jit(solution)/shard_map/all_to_all | solution.py:262
  23.3 0.7 fusion.81
  24.2 0.1 reduce.5
  24.4 0.7 fusion.60
  25.2 17.1 %all-to-all-done = bf16[16,112,360]{2,1,0:T(8,128)(2,1)} async-done(((bf16[16,112,360]{2,1,0:T(8,128)(2,1)}), bf16[16,112,360]{2,1,0:T(8,128)(2,1)}, u32[]{:S(2)}, u32[]{:S(2)}) %all-to-all-start) | async-done | bytes 1290272 | tf_op jit(solution)/shard_map/all_to_all | solution.py:262
  42.2 3.6 fusion.35
  45.9 0.7 all-gather.10.cloned.1.call-update
  46.7 29.9 %all-gather.6.cloned.1.call-done = bf16[768,1440]{0,1:T(8,128)(2,1)} async-done(((bf16[768,360]{0,1:T(8,128)(2,1)}), bf16[768,1440]{0,1:T(8,128)(2,1)}) %all-gather.6.cloned.1.call-update) | async-done | bytes 2211856 | tf_op jit(solution)/shard_map/all_gather | solution.py:183
  76.6 0.2 reduce-scatter.5.cloned.1.call-start
  76.8 0.1 reshape.583
  76.9 0.7 bitcast_subtract_fusion.1
  77.8 0.7 fusion.80
  78.7 4.6 %copy.43 = bf16[2880,512]{0,1:T(8,128)(2,1)} copy(bf16[2880,512]{1,0:T(8,128)(2,1)} %param.23) | data formatting | bytes 5898240 | tf_op args[8]
  83.3 0.1 select_reduce_fusion.2
  83.4 0.7 gather_fusion.1
  84.1 0.7 gather_fusion.2
  84.8 0.1 reshape.612
  85.0 0.4 multiply_cosine_fusion.1
  85.5 38.9 %all-gather.10.cloned.1.call-done = bf16[64,128,1,128]{3,1,2,0:T(8,128)(2,1)} async-done(((bf16[4,128,1,128]{3,1,2,0:T(8,128)(2,1)}), bf16[64,128,1,128]{3,1,2,0:T(8,128)(2,1)}) %all-gather.10.cloned.1.call-update) | async-done | bytes 2097168 | tf_op jit(solution)/shard_map/all_gather | solution.py:166
  124.3 3.2 gather_fusion.3
  127.6 2.6 fusion.36.tail_ref
  130.1 13.9 %all-gather.8.cloned.1.call-done = bf16[768,2880]{0,1:T(8,128)(2,1)} async-done(((bf16[768,1440]{0,1:T(8,128)(2,1)}), bf16[768,2880]{0,1:T(8,128)(2,1)}) %all-gather.8.cloned.1.call-update) | async-done | bytes 4423696 | tf_op jit(solution)/shard_map/all_gather | solution.py:184
  144.0 3.3 fusion
  147.4 0.2 copy-done.3
  147.6 1.1 fusion.3
  148.8 0.3 copy.42
  149.0 0.8 copy-done.11
  149.9 0.9 convolution_bitcast_fusion
  150.7 0.4 fusion.55
  151.2 0.5 copy-done.5
  151.7 2.7 fusion.65
  154.4 0.2 subtract_convert_fusion
  154.6 3.3 fusion.15
  158.0 2.4 fusion.29
  160.4 28.7 %shard_map.145 = bf16[16,112,512]{2,1,0:T(8,128)(2,1)} custom-call(f32[8]{0:T(128)} %sink_ref.1, bf16[16,112,512]{2,1,0:T(8,128)(2,1)} %bitcast.123, bf16[16,112,128]{2,1,0:T(8,128)(2,1)} %bitcast.125, bf16[16,128,128]{2,1,0:T(8,128)(2,1)} %fusion.36.tail_ref), custom_call_target="tpu_custom_call" | custom-call | flops 880803840 | bytes 4653056 | tf_op jit(solution)/shard_map/pallas_call | solution.py:137
  189.1 7.4 %convolution_convert_fusion = bf16[768,2880]{0,1:T(8,128)(2,1)} fusion(bf16[512,2880]{0,1:T(8,128)(2,1)S(1)} %copy-done, bf16[1792,512]{1,0:T(8,128)(2,1)} %bitcast.124, s32[768]{0:T(1024)S(1)} %get-tuple-element.14), kind=kOutput, calls=%fused_computation.23 | convolution fusion | flops 3678191616 | bytes 9210880 | tf_op jit(solution)/shard_map/dot_general | solution.py:285
  196.5 4.6 %copy.45 = bf16[768,4,2,360]{0,3,1,2:T(8,128)(2,1)} copy(bf16[768,4,2,360]{0,3,2,1:T(8,128)(2,1)} %bitcast.115) | data formatting | bytes 8847360 | tf_op jit(solution)/shard_map/reshape | solution.py:193
  201.2 16.4 %reduce-scatter.5.cloned.1.call-done = bf16[768,1440]{0,1:T(8,128)(2,1)} async-done(((bf16[768,2880]{0,1:T(8,128)(2,1)}), bf16[768,1440]{0,1:T(8,128)(2,1)}) %reduce-scatter.5.cloned.1.call-update) | async-done | bytes 2211856 | tf_op jit(solution)/shard_map/reduce_scatter | solution.py:194
  217.7 32.0 %reduce-scatter.7.cloned.1.call-done = bf16[768,360]{0,1:T(8,128)(2,1)} async-done(((bf16[768,1440]{0,1:T(8,128)(2,1)}), bf16[768,360]{0,1:T(8,128)(2,1)}) %reduce-scatter.7.cloned.1.call-update) | async-done | bytes 552976 | tf_op jit(solution)/shard_map/reduce_scatter | solution.py:195
  249.6 2.0 add_convert_fusion.1
  251.7 31.4 %all-gather.12.cloned.1.call-done = bf16[768,1440]{0,1:T(8,128)(2,1)} async-done(((bf16[768,360]{0,1:T(8,128)(2,1)}), bf16[768,1440]{0,1:T(8,128)(2,1)}) %all-gather.12.cloned.1.call-update) | async-done | bytes 2211856 | tf_op jit(solution)/shard_map/all_gather | solution.py:183
  283.3 20.9 %all-gather.14.cloned.1.call-done = bf16[768,2880]{0,1:T(8,128)(2,1)} async-done(((bf16[768,1440]{0,1:T(8,128)(2,1)}), bf16[768,2880]{0,1:T(8,128)(2,1)}) %all-gather.14.cloned.1.call-update) | async-done | bytes 4423696 | tf_op jit(solution)/shard_map/all_gather | solution.py:184
  304.2 3.2 copy.46
  307.4 0.4 copy-done.2
  307.7 1.0 multiply_reduce_fusion
  308.7 1.3 fusion.5
  310.1 2.1 copy-done.4
  312.2 2.9 fusion.66
  315.0 11.1 %convolution_convert_fusion.1 = bf16[768,2880]{0,1:T(8,128)(2,1)} fusion(bf16[360,2880]{1,0:T(8,128)(2,1)} %param.29, bf16[768,2880]{0,1:T(8,128)(2,1)} %copy-done.4, bf16[2880,360]{0,1:T(8,128)(2,1)} %param.28, f32[768,360]{0,1:T(8,128)} %fusion.66), kind=kOutput, calls=%fused_computation.24 | convolution fusion | flops 3188920320 | bytes 14100480 | tf_op jit(solution)/shard_map/dot_general | solution.py:294
  326.2 4.6 %copy.47 = bf16[768,4,2,360]{0,3,1,2:T(8,128)(2,1)} copy(bf16[768,4,2,360]{0,3,2,1:T(8,128)(2,1)} %bitcast.116) | data formatting | bytes 8847360 | tf_op jit(solution)/shard_map/reshape | solution.py:193
  330.9 16.4 %reduce-scatter.9.cloned.1.call-done = bf16[768,1440]{0,1:T(8,128)(2,1)} async-done(((bf16[768,2880]{0,1:T(8,128)(2,1)}), bf16[768,1440]{0,1:T(8,128)(2,1)}) %reduce-scatter.9.cloned.1.call-update) | async-done | bytes 2211856 | tf_op jit(solution)/shard_map/reduce_scatter | solution.py:194
  347.3 32.2 %reduce-scatter.11.cloned.1.call-done = bf16[768,360]{0,1:T(8,128)(2,1)} async-done(((bf16[768,1440]{0,1:T(8,128)(2,1)}), bf16[768,360]{0,1:T(8,128)(2,1)}) %reduce-scatter.11.cloned.1.call-update) | async-done | bytes 552976 | tf_op jit(solution)/shard_map/reduce_scatter | solution.py:195
  379.4 3.5 fusion.18
  382.9 1.5 copy.48
  384.5 7.0 %all-to-all-start.1 = ((bf16[16,112,360]{2,1,0:T(8,128)(2,1)}), bf16[16,112,360]{2,1,0:T(8,128)(2,1)}, u32[]{:S(2)}, u32[]{:S(2)}) async-start(bf16[16,112,360]{2,1,0:T(8,128)(2,1)} %bitcast.112), calls=%async_computation.5 | async-start | bytes 2752512 | tf_op jit(solution)/shard_map/all_to_all | solution.py:298
  391.5 0.7 fusion.59
  392.2 18.2 %all-to-all-done.1 = bf16[16,112,360]{2,1,0:T(8,128)(2,1)} async-done(((bf16[16,112,360]{2,1,0:T(8,128)(2,1)}), bf16[16,112,360]{2,1,0:T(8,128)(2,1)}, u32[]{:S(2)}, u32[]{:S(2)}) %all-to-all-start.1) | async-done | bytes 1290272 | tf_op jit(solution)/shard_map/all_to_all | solution.py:298
  410.5 3.2 gather_fusion.4
  (63 shorter events, 1.5 us)
Async XLA Ops:
  6.5 182.5 %copy-start = (bf16[512,2880]{0,1:T(8,128)(2,1)S(1)}, bf16[512,2880]{0,1:T(8,128)(2,1)}, u32[]{:S(2)}) copy-start(bf16[512,2880]{0,1:T(8,128)(2,1)} %param.25) | copy-start | bytes 8847364
  15.5 26.8 %all-to-all-start = ((bf16[16,112,360]{2,1,0:T(8,128)(2,1)}), bf16[16,112,360]{2,1,0:T(8,128)(2,1)}, u32[]{:S(2)}, u32[]{:S(2)}) async-start(bf16[16,112,360]{2,1,0:T(8,128)(2,1)} %gather_fusion), calls=%async_computation | async-start | bytes 2752512 | tf_op jit(solution)/shard_map/all_to_all | solution.py:262
  23.3 53.3 %all-gather.6.cloned.1.call-start = ((), (), s32[]{:S(2)}) async-start(), calls=%async_computation.6 | async-start | bytes 2764800 | tf_op jit(solution)/shard_map/all_gather | solution.py:183
  45.9 31.0 %copy-start.8 = (bf16[2880]{0:T(1024)(128)(2,1)S(1)}, bf16[2880]{0:T(1024)(128)(2,1)}, u32[]{:S(2)}) copy-start(bf16[2880]{0:T(1024)(128)(2,1)} %param.22) | copy-start | bytes 17284
  45.9 78.4 %all-gather.10.cloned.1.call-start = ((), (), s32[]{:S(2)}) async-start(), calls=%async_computation.8 | async-start | bytes 2228224 | tf_op jit(solution)/shard_map/all_gather | solution.py:166
  46.6 97.4 %all-gather.8.cloned.1.call-start = ((), (), s32[]{:S(2)}) async-start(), calls=%async_computation.7 | async-start | bytes 6635520 | tf_op jit(solution)/shard_map/all_gather | solution.py:184
  76.6 141.0 %reduce-scatter.5.cloned.1.call-start = ((), (), s32[]{:S(2)}) async-start(), calls=%async_computation.9 | async-start | bytes 6635520 | tf_op jit(solution)/shard_map/reduce_scatter | solution.py:194
  78.7 4.6 %copy-start.12 = (s32[64]{0:T(128)S(1)}, s32[64]{0:T(128)}, u32[]{:S(2)}) copy-start(s32[64]{0:T(128)} %param.20) | copy-start | bytes 772
  144.0 3.6 copy-start.3
  148.7 1.1 copy-start.11
  149.9 1.9 copy-start.5
  201.2 48.5 %copy-start.6 = (bf16[768,360]{0,1:T(8,128)(2,1)S(1)}, bf16[768,360]{0,1:T(8,128)(2,1)}, u32[]{:S(2)}) copy-start(bf16[768,360]{0,1:T(8,128)(2,1)} %fusion.35) | copy-start | bytes 1658884
  201.2 48.4 %reduce-scatter.7.cloned.1.call-start = ((), (), s32[]{:S(2)}) async-start(), calls=%async_computation.10 | async-start | bytes 2764800 | tf_op jit(solution)/shard_map/reduce_scatter | solution.py:195
  217.6 65.6 %copy-start.9 = (bf16[2880]{0:T(1024)(128)(2,1)S(1)}, bf16[2880]{0:T(1024)(128)(2,1)}, u32[]{:S(2)}) copy-start(bf16[2880]{0:T(1024)(128)(2,1)} %param.26) | copy-start | bytes 17284
  217.6 65.5 %all-gather.12.cloned.1.call-start = ((), (), s32[]{:S(2)}) async-start(), calls=%async_computation.11 | async-start | bytes 2764800 | tf_op jit(solution)/shard_map/all_gather | solution.py:183
  251.7 52.5 %all-gather.14.cloned.1.call-start = ((), (), s32[]{:S(2)}) async-start(), calls=%async_computation.12 | async-start | bytes 6635520 | tf_op jit(solution)/shard_map/all_gather | solution.py:184
  283.2 64.0 %reduce-scatter.9.cloned.1.call-start = ((), (), s32[]{:S(2)}) async-start(), calls=%async_computation.13 | async-start | bytes 6635520 | tf_op jit(solution)/shard_map/reduce_scatter | solution.py:194
  304.2 3.6 copy-start.2
  308.7 3.5 copy-start.10
  310.1 2.1 copy-start.4
  330.8 48.6 %copy-start.7 = (bf16[768,360]{0,1:T(8,128)(2,1)S(1)}, bf16[768,360]{0,1:T(8,128)(2,1)}, u32[]{:S(2)}) copy-start(bf16[768,360]{0,1:T(8,128)(2,1)} %add_convert_fusion.1) | copy-start | bytes 1658884
  330.8 48.6 %reduce-scatter.11.cloned.1.call-start = ((), (), s32[]{:S(2)}) async-start(), calls=%async_computation.14 | async-start | bytes 2764800 | tf_op jit(solution)/shard_map/reduce_scatter | solution.py:195
  384.5 29.2 %copy-start.1 = (bf16[512,2880]{0,1:T(8,128)(2,1)S(1)}, bf16[512,2880]{0,1:T(8,128)(2,1)}, u32[]{:S(2)}) copy-start(bf16[512,2880]{0,1:T(8,128)(2,1)} %param.25) | copy-start | bytes 8847364
  384.5 26.0 %all-to-all-start.1 = ((bf16[16,112,360]{2,1,0:T(8,128)(2,1)}), bf16[16,112,360]{2,1,0:T(8,128)(2,1)}, u32[]{:S(2)}, u32[]{:S(2)}) async-start(bf16[16,112,360]{2,1,0:T(8,128)(2,1)} %bitcast.112), calls=%async_computation.5 | async-start | bytes 2752512 | tf_op jit(solution)/shard_map/all_to_all | solution.py:298
Sparse Core Ops, SparseCore 0:
  46.0 30.5 all-gather.5
  78.7 45.5 all-gather.9
  126.0 17.9 all-gather.7
  201.3 16.2 reduce-scatter.4
  219.9 29.7 reduce-scatter.6
  251.8 31.3 all-gather.11
  284.8 19.2 all-gather.13
  331.0 16.2 reduce-scatter.8
  349.7 29.7 reduce-scatter.10

commit v7 on v5

--- a/solution.py
+++ b/solution.py
@@ -76,33 +76,37 @@
 
 
 def attend_kernel(sink_ref, q_ref, kv_ref, tail_ref, o_ref):
-    slot_length = q_ref.shape[1]
+    batch, slot_length = q_ref.shape[0], q_ref.shape[1]
     window = tail_ref.shape[1]
     head_dim = kv_ref.shape[2] // 2
     heads = q_ref.shape[2] // head_dim
     scale = head_dim ** (-0.5)
-    kv = kv_ref[0]
-    tail = tail_ref[0]
-    own_keys, own_values = kv[:, :head_dim], kv[:, head_dim:]
-    tail_keys, tail_values = tail[:, :head_dim], tail[:, head_dim:]
     step = lax.broadcasted_iota(jnp.int32, (slot_length, window), 0)
     column = lax.broadcasted_iota(jnp.int32, (slot_length, window), 1)
-    tail_allowed = column > step
+    tail_allowed = jnp.concatenate([column > step] * heads, axis=0)
     own_step = lax.broadcasted_iota(jnp.int32, (slot_length, slot_length), 0)
     own_column = lax.broadcasted_iota(jnp.int32, (slot_length, slot_length), 1)
-    own_allowed = own_column <= own_step
+    own_allowed = jnp.concatenate([own_column <= own_step] * heads, axis=0)
+    sink = jnp.concatenate(
+        [jnp.full((slot_length, 1), sink_ref[head], jnp.float32) for head in range(heads)],
+        axis=0,
+    )
     contract = (((1,), (1,)), ((), ()))
-    for head in range(heads):
-        query = q_ref[0, :, head * head_dim:(head + 1) * head_dim]
+    for item in range(batch):
+        kv = kv_ref[item]
+        tail = tail_ref[item]
+        query = q_ref[item]
+        stacked = jnp.concatenate(
+            [query[:, head * head_dim:(head + 1) * head_dim] for head in range(heads)], axis=0
+        )
         tail_scores = lax.dot_general(
-            query, tail_keys, contract, preferred_element_type=jnp.float32
+            stacked, tail[:, :head_dim], contract, preferred_element_type=jnp.float32
         ) * scale
         own_scores = lax.dot_general(
-            query, own_keys, contract, preferred_element_type=jnp.float32
+            stacked, kv[:, :head_dim], contract, preferred_element_type=jnp.float32
         ) * scale
         tail_scores = jnp.where(tail_allowed, tail_scores, -jnp.inf)
         own_scores = jnp.where(own_allowed, own_scores, -jnp.inf)
-        sink = sink_ref[head]
         largest = jnp.maximum(
             jnp.maximum(
                 jnp.max(tail_scores, axis=1, keepdims=True),
@@ -120,12 +124,16 @@
         tail_weights = (tail_weights / normalizer).astype(jnp.bfloat16)
         own_weights = (own_weights / normalizer).astype(jnp.bfloat16)
         mixed = jnp.dot(
-            tail_weights, tail_values, preferred_element_type=jnp.float32
-        ) + jnp.dot(own_weights, own_values, preferred_element_type=jnp.float32)
-        o_ref[0, :, head * head_dim:(head + 1) * head_dim] = mixed.astype(o_ref.dtype)
-
-
-def attend_pallas(query_slots, paired_slots, tail_rows, sink_logits):
+            tail_weights, tail[:, head_dim:], preferred_element_type=jnp.float32
+        ) + jnp.dot(own_weights, kv[:, head_dim:], preferred_element_type=jnp.float32)
+        mixed = mixed.astype(o_ref.dtype)
+        for head in range(heads):
+            o_ref[item, :, head * head_dim:(head + 1) * head_dim] = mixed[
+                head * slot_length:(head + 1) * slot_length
+            ]
+
+
+def attend_pallas(query_slots, paired_slots, tail_rows, sink_logits, batch=2):
     peers, slot_length, width = query_slots.shape
     window = tail_rows.shape[1]
     pair_width = paired_slots.shape[2]
@@ -135,14 +143,14 @@
     moved = 2 * (2 * query_slots.size + paired_slots.size + tail_rows.size)
     return pl.pallas_call(
         attend_kernel,
-        grid=(peers,),
+        grid=(peers // batch,),
         in_specs=[
             pl.BlockSpec(memory_space=pltpu.SMEM),
-            pl.BlockSpec((1, slot_length, width), lambda n: (n, 0, 0)),
-            pl.BlockSpec((1, slot_length, pair_width), lambda n: (n, 0, 0)),
-            pl.BlockSpec((1, window, pair_width), lambda n: (n, 0, 0)),
+            pl.BlockSpec((batch, slot_length, width), lambda n: (n, 0, 0)),
+            pl.BlockSpec((batch, slot_length, pair_width), lambda n: (n, 0, 0)),
+            pl.BlockSpec((batch, window, pair_width), lambda n: (n, 0, 0)),
         ],
-        out_specs=pl.BlockSpec((1, slot_length, width), lambda n: (n, 0, 0)),
+        out_specs=pl.BlockSpec((batch, slot_length, width), lambda n: (n, 0, 0)),
         out_shape=jax.ShapeDtypeStruct((peers, slot_length, width), jnp.bfloat16),
         cost_estimate=pl.CostEstimate(
             flops=flops,

time: 329 us -> 330 us (level)
  no operation moved by 1% of the time
where the time goes in v7:
time: 330 us; the launch traced here: 329 us
  waiting for transfers between devices  191 us (58%)
  matrix products  45.8 us (14%)
  Pallas kernels  29.5 us (9%)
  local copies, waits for them, and re-layouts  20.5 us (6%)
  starting transfers between devices  15 us (5%)
  other arithmetic  13.7 us (4%)
  between operations  13.4 us (4%)
    reduce_scatter x1, waiting for transfers between devices, local(): lax.psum_scatter(jnp.dot(hidden, w_down, preferred_element_type=jnp.float...  38.5 us
    reduce_scatter x1, waiting for transfers between devices, local(): lax.psum_scatter(partial_value.astype(jnp.bfloat16), 'tp', scatter_dimens...  38.5 us
    all_gather x1, waiting for transfers between devices, local(): residual = lax.all_gather(residual_part, 'tp', axis=1, tiled=True)  31.9 us
    pallas_call x1, Pallas kernels, attend_pallas(): pl.pallas_call(attend_kernel, grid=(peers // batch,), in_specs=[pl.BlockS...  29.5 us
    all_gather x1, waiting for transfers between devices, local(): input_rows = lax.all_gather(input_part, 'tp', axis=1, tiled=True)  28.2 us
    all_to_all x1, waiting for transfers between devices, local(): lax.all_to_all(out_slots, 'req', split_axis=0, concat_axis=0, tiled=True)  20.8 us
    all_to_all x1, waiting for transfers between devices, local(): lax.all_to_all(my_features[send_order], 'req', split_axis=0, concat_axis=...  19.8 us
    all_gather x1, waiting for transfers between devices, fetch_prefix(): shard_rows = lax.all_gather(prefix_cache, 'req', axis=0, tiled=True)  12.3 us
  transfers between devices with their start and end apart: 7, of which 7 were waited for; matrix products, arithmetic and copies ran while one was open for 8% of the time, Pallas kernels for 0%

profile of v7, /device:TPU:7, one launch (start us, length us, event | category | flops | bytes accessed | tf_op | source)
XLA Modules:
  0.0 328.6 jit_solution(2690363154774716973)
XLA Ops:
  6.5 0.7 all-gather.6.cloned.1.call-update
  7.3 0.9 reshape.525
  8.2 0.7 fusion.74
  8.9 0.1 select_reduce_fusion.4
  9.0 0.8 select_reduce_fusion.3
  9.8 3.2 constant_dynamic-slice_fusion.1
  13.0 3.2 gather_fusion
  16.2 7.8 %all-to-all-start = ((bf16[16,112,360]{2,1,0:T(8,128)(2,1)}), bf16[16,112,360]{2,1,0:T(8,128)(2,1)}, u32[]{:S(2)}, u32[]{:S(2)}) async-start(bf16[16,112,360]{2,1,0:T(8,128)(2,1)} %gather_fusion), calls=%async_computation | async-start | bytes 2752512 | tf_op jit(solution)/shard_map/all_to_all | solution.py:250
  24.0 0.0 all-gather.4.cloned.1.call-start
  24.1 0.7 fusion.87
  24.8 0.1 copy.24
  24.9 0.1 reduce
  25.0 0.1 convert_reduce_fusion
  25.1 0.7 fusion.72
  25.8 0.1 select_reduce_fusion
  25.9 19.8 %all-to-all-done = bf16[16,112,360]{2,1,0:T(8,128)(2,1)} async-done(((bf16[16,112,360]{2,1,0:T(8,128)(2,1)}), bf16[16,112,360]{2,1,0:T(8,128)(2,1)}, u32[]{:S(2)}, u32[]{:S(2)}) %all-to-all-start) | async-done | bytes 1290272 | tf_op jit(solution)/shard_map/all_to_all | solution.py:250
  45.7 3.7 %fusion.35 = bf16[768,360]{0,1:T(8,128)(2,1)} fusion(bf16[1792,360]{1,0:T(8,128)(2,1)} %bitcast.6, s32[768]{0:T(1024)S(1)} %get-tuple-element.14), kind=kOutput, calls=%fused_computation.41 | convolution fusion | flops 992557056 | bytes 1846272 | tf_op jit(solution)/shard_map/dot_general | solution.py:244
  49.4 0.0 reduce-scatter.3.cloned.1.call-start
  49.5 0.7 bitcast_subtract_fusion.1
  50.2 0.1 add_clamp_fusion
  50.2 0.1 min.28
  50.3 0.7 fusion.86
  51.0 0.1 iota_compare_fusion.18
  51.1 0.1 lt.82
  51.2 0.1 select_reduce_fusion.2
  51.3 0.7 gather_fusion.1
  52.0 0.7 gather_fusion.2
  52.7 0.1 copy.25
  52.8 0.1 reshape.560
  52.9 0.1 iota_add_fusion
  53.0 0.4 multiply_cosine_fusion.1
  53.4 12.3 %all-gather.6.cloned.1.call-done = bf16[64,128,1,128]{3,1,2,0:T(8,128)(2,1)} async-done(((bf16[4,128,1,128]{3,1,2,0:T(8,128)(2,1)}), bf16[64,128,1,128]{3,1,2,0:T(8,128)(2,1)}) %all-gather.6.cloned.1.call-update) | async-done | bytes 2097168 | tf_op jit(solution)/shard_map/all_gather | solution.py:173
  65.7 3.2 gather_fusion.3
  68.9 2.6 fusion.36.tail_ref
  71.5 28.2 %all-gather.4.cloned.1.call-done = bf16[768,2880]{0,1:T(8,128)(2,1)} async-done(((bf16[768,360]{0,1:T(8,128)(2,1)}), bf16[768,2880]{0,1:T(8,128)(2,1)}) %all-gather.4.cloned.1.call-update) | async-done | bytes 4423696 | tf_op jit(solution)/shard_map/all_gather | solution.py:254
  99.7 3.3 %fusion = f32[768]{0:T(1024)S(1)} fusion(bf16[768,2880]{0,1:T(8,128)(2,1)} %all-gather.4.cloned.1.call-done), kind=kLoop, calls=%fused_computation.9 | loop fusion | flops 6634752 | bytes 4426752 | tf_op jit(solution)/shard_map/reduce_sum | solution.py:18
  103.1 0.2 copy-done.1
  103.3 2.8 fusion.44
  106.1 0.4 fusion.67
  106.6 3.1 fusion.42
  109.7 0.2 subtract_convert_fusion
  110.0 0.1 pad_maximum_fusion
  110.0 3.5 %fusion.15 = bf16[1792,512]{1,0:T(8,128)(2,1)} fusion(bf16[768,512]{0,1:T(8,128)(2,1)S(1)} %bitcast.75, s32[1792]{0:T(1024)S(1)} %min.28, pred[1792]{0:T(1024)(128)(4,1)S(1)} %lt.82), kind=kOutput, calls=%fused_computation.25 | convolution fusion | flops 1412956160 | bytes 2630400 | tf_op jit(solution)/shard_map/dot_general | solution.py:240
  113.5 2.4 fusion.29
  116.0 29.5 %shard_map.145 = bf16[16,112,512]{2,1,0:T(8,128)(2,1)} custom-call(f32[8]{0:T(128)} %sink_ref.1, bf16[16,112,512]{2,1,0:T(8,128)(2,1)} %bitcast.79, bf16[16,112,128]{2,1,0:T(8,128)(2,1)} %bitcast.81, bf16[16,128,128]{2,1,0:T(8,128)(2,1)} %fusion.36.tail_ref), custom_call_target="tpu_custom_call" | custom-call | flops 880803840 | bytes 4653056 | tf_op jit(solution)/shard_map/pallas_call | solution.py:144
  145.5 7.4 %convolution_convert_fusion = bf16[768,2880]{0,1:T(8,128)(2,1)} fusion(bf16[512,2880]{0,1:T(8,128)(2,1)S(1)} %copy-done, bf16[1792,512]{1,0:T(8,128)(2,1)} %bitcast.80, s32[768]{0:T(1024)S(1)} %get-tuple-element.14), kind=kOutput, calls=%fused_computation.23 | convolution fusion | flops 3678191616 | bytes 9210880 | tf_op jit(solution)/shard_map/dot_general | solution.py:273
  153.0 0.0 reduce-scatter.3.cloned.1.call-update
  153.0 0.0 all-gather.8.cloned.1.call-start
  153.0 38.5 %reduce-scatter.3.cloned.1.call-done = bf16[768,360]{0,1:T(8,128)(2,1)} async-done(((bf16[768,2880]{0,1:T(8,128)(2,1)}), bf16[768,360]{0,1:T(8,128)(2,1)}) %reduce-scatter.3.cloned.1.call-update) | async-done | bytes 552976 | tf_op jit(solution)/shard_map/reduce_scatter | solution.py:274
  191.6 2.0 add_convert_fusion.1
  193.6 0.0 all-gather.8.cloned.1.call-update
  193.6 0.3 reduce-scatter.5.cloned.1.call-start
  193.9 31.9 %all-gather.8.cloned.1.call-done = bf16[768,2880]{0,1:T(8,128)(2,1)} async-done(((bf16[768,360]{0,1:T(8,128)(2,1)}), bf16[768,2880]{0,1:T(8,128)(2,1)}) %all-gather.8.cloned.1.call-update) | async-done | bytes 4423696 | tf_op jit(solution)/shard_map/all_gather | solution.py:278
  225.8 3.3 %fusion.3 = f32[768]{0:T(1024)S(1)} fusion(bf16[768,2880]{0,1:T(8,128)(2,1)} %all-gather.8.cloned.1.call-done), kind=kLoop, calls=%fused_computation.12 | loop fusion | flops 6634752 | bytes 4426752 | tf_op jit(solution)/shard_map/reduce_sum | solution.py:18
  229.1 0.2 copy-done.2
  229.4 4.6 %fusion.38 = f32[768,360]{0,1:T(8,128)} fusion(bf16[2880,360]{0,1:T(8,128)(2,1)} %param.27, bf16[768,2880]{0,1:T(8,128)(2,1)S(1)} %copy-done.2, f32[2880]{0:T(1024)S(1)} %convert_element_type.116, f32[768]{0:T(1024)S(1)} %add_rsqrt_fusion), kind=kOutput, calls=%fused_computation.43 | convolution fusion | flops 1601372160 | bytes 7617792 | tf_op jit(solution)/shard_map/dot_general | solution.py:280
  234.0 11.3 %convolution_convert_fusion.1 = bf16[768,2880]{0,1:T(8,128)(2,1)} fusion(bf16[360,2880]{1,0:T(8,128)(2,1)} %param.29, bf16[2880,360]{0,1:T(8,128)(2,1)} %param.28, bf16[768,2880]{0,1:T(8,128)(2,1)} %all-gather.8.cloned.1.call-done, f32[2880]{0:T(1024)S(1)} %convert_element_type.116, f32[768]{0:T(1024)S(1)} %add_rsqrt_fusion, f32[768,360]{0,1:T(8,128)} %fusion.38), kind=kOutput, calls=%fused_computation.24 | convolution fusion | flops 3197767680 | bytes 14115072 | tf_op jit(solution)/shard_map/dot_general | solution.py:284
  245.3 38.5 %reduce-scatter.5.cloned.1.call-done = bf16[768,360]{0,1:T(8,128)(2,1)} async-done(((bf16[768,2880]{0,1:T(8,128)(2,1)}), bf16[768,360]{0,1:T(8,128)(2,1)}) %reduce-scatter.5.cloned.1.call-update) | async-done | bytes 552976 | tf_op jit(solution)/shard_map/reduce_scatter | solution.py:283
  283.9 4.3 %fusion.18 = bf16[1792,360]{0,1:T(8,128)(2,1)} fusion(s32[1792]{0:T(1024)S(1)} %min.28, pred[1792]{0:T(1024)(128)(4,1)S(1)} %lt.82, bf16[768,360]{0,1:T(8,128)(2,1)} %reduce-scatter.5.cloned.1.call-done, bf16[768,360]{0,1:T(8,128)(2,1)S(1)} %copy-done.4), kind=kOutput, calls=%fused_computation.26 | convolution fusion | flops 995407872 | bytes 2405120 | tf_op jit(solution)/shard_map/dot_general | solution.py:240
  288.2 2.5 copy.26
  290.7 6.7 %all-to-all-start.1 = ((bf16[16,112,360]{2,1,0:T(8,128)(2,1)}), bf16[16,112,360]{2,1,0:T(8,128)(2,1)}, u32[]{:S(2)}, u32[]{:S(2)}) async-start(bf16[16,112,360]{2,1,0:T(8,128)(2,1)} %bitcast.72), calls=%async_computation.3 | async-start | bytes 2752512 | tf_op jit(solution)/shard_map/all_to_all | solution.py:291
  297.4 0.7 fusion.71
  298.1 20.8 %all-to-all-done.1 = bf16[16,112,360]{2,1,0:T(8,128)(2,1)} async-done(((bf16[16,112,360]{2,1,0:T(8,128)(2,1)}), bf16[16,112,360]{2,1,0:T(8,128)(2,1)}, u32[]{:S(2)}, u32[]{:S(2)}) %all-to-all-start.1) | async-done | bytes 1290272 | tf_op jit(solution)/shard_map/all_to_all | solution.py:291
  319.0 3.2 gather_fusion.4
  (35 shorter events, 0.2 us)
Async XLA Ops:
  6.5 139.0 %copy-start = (bf16[512,2880]{0,1:T(8,128)(2,1)S(1)}, bf16[512,2880]{0,1:T(8,128)(2,1)}, u32[]{:S(2)}) copy-start(bf16[512,2880]{0,1:T(8,128)(2,1)} %param.25) | copy-start | bytes 8847364
  6.5 59.2 %all-gather.6.cloned.1.call-start = ((), (), s32[]{:S(2)}) async-start(), calls=%async_computation.5 | async-start | bytes 2228224 | tf_op jit(solution)/shard_map/all_gather | solution.py:173
  16.2 29.5 %all-to-all-start = ((bf16[16,112,360]{2,1,0:T(8,128)(2,1)}), bf16[16,112,360]{2,1,0:T(8,128)(2,1)}, u32[]{:S(2)}, u32[]{:S(2)}) async-start(bf16[16,112,360]{2,1,0:T(8,128)(2,1)} %gather_fusion), calls=%async_computation | async-start | bytes 2752512 | tf_op jit(solution)/shard_map/all_to_all | solution.py:250
  24.0 75.7 %all-gather.4.cloned.1.call-start = ((), (), s32[]{:S(2)}) async-start(), calls=%async_computation.4 | async-start | bytes 4976640 | tf_op jit(solution)/shard_map/all_gather | solution.py:254
  45.7 3.8 %copy-start.5 = (bf16[2880]{0:T(1024)(128)(2,1)S(1)}, bf16[2880]{0:T(1024)(128)(2,1)}, u32[]{:S(2)}) copy-start(bf16[2880]{0:T(1024)(128)(2,1)} %param.22) | copy-start | bytes 17284
  45.7 5.5 %copy-start.8 = (s32[64]{0:T(128)S(1)}, s32[64]{0:T(128)}, u32[]{:S(2)}) copy-start(s32[64]{0:T(128)} %param.20) | copy-start | bytes 772
  49.4 142.1 %reduce-scatter.3.cloned.1.call-start = ((), (), s32[]{:S(2)}) async-start(), calls=%async_computation.6 | async-start | bytes 4976640 | tf_op jit(solution)/shard_map/reduce_scatter | solution.py:274
  99.7 3.6 %copy-start.1 = (bf16[768,2880]{0,1:T(8,128)(2,1)S(1)}, bf16[768,2880]{0,1:T(8,128)(2,1)}, u32[]{:S(2)}) copy-start(bf16[768,2880]{0,1:T(8,128)(2,1)} %all-gather.4.cloned.1.call-done) | copy-start | bytes 13271044
  103.3 3.3 %copy-start.7 = (bf16[2880,512]{1,0:T(8,128)(2,1)S(1)}, bf16[2880,512]{1,0:T(8,128)(2,1)}, u32[]{:S(2)}) copy-start(bf16[2880,512]{1,0:T(8,128)(2,1)} %param.23) | copy-start | bytes 8847364
  152.9 38.6 %copy-start.3 = (bf16[768,360]{0,1:T(8,128)(2,1)S(1)}, bf16[768,360]{0,1:T(8,128)(2,1)}, u32[]{:S(2)}) copy-start(bf16[768,360]{0,1:T(8,128)(2,1)} %fusion.35) | copy-start | bytes 1658884
  153.0 40.9 %copy-start.6 = (bf16[2880]{0:T(1024)(128)(2,1)S(1)}, bf16[2880]{0:T(1024)(128)(2,1)}, u32[]{:S(2)}) copy-start(bf16[2880]{0:T(1024)(128)(2,1)} %param.26) | copy-start | bytes 17284
  153.0 72.8 %all-gather.8.cloned.1.call-start = ((), (), s32[]{:S(2)}) async-start(), calls=%async_computation.7 | async-start | bytes 4976640 | tf_op jit(solution)/shard_map/all_gather | solution.py:278
  193.6 90.2 %reduce-scatter.5.cloned.1.call-start = ((), (), s32[]{:S(2)}) async-start(), calls=%async_computation.8 | async-start | bytes 4976640 | tf_op jit(solution)/shard_map/reduce_scatter | solution.py:283
  225.8 3.6 %copy-start.2 = (bf16[768,2880]{0,1:T(8,128)(2,1)S(1)}, bf16[768,2880]{0,1:T(8,128)(2,1)}, u32[]{:S(2)}) copy-start(bf16[768,2880]{0,1:T(8,128)(2,1)} %all-gather.8.cloned.1.call-done) | copy-start | bytes 13271044
  245.3 38.6 %copy-start.4 = (bf16[768,360]{0,1:T(8,128)(2,1)S(1)}, bf16[768,360]{0,1:T(8,128)(2,1)}, u32[]{:S(2)}) copy-start(bf16[768,360]{0,1:T(8,128)(2,1)} %add_convert_fusion.1) | copy-start | bytes 1658884
  290.7 28.3 %all-to-all-start.1 = ((bf16[16,112,360]{2,1,0:T(8,128)(2,1)}), bf16[16,112,360]{2,1,0:T(8,128)(2,1)}, u32[]{:S(2)}, u32[]{:S(2)}) async-start(bf16[16,112,360]{2,1,0:T(8,128)(2,1)} %bitcast.72), calls=%async_computation.3 | async-start | bytes 2752512 | tf_op jit(solution)/shard_map/all_to_all | solution.py:291
Sparse Core Ops, SparseCore 0:
  9.5 56.1 all-gather.5
  67.4 32.2 all-gather.3
  153.1 38.4 reduce-scatter.2
  193.7 31.9 all-gather.7
  245.4 38.3 reduce-scatter.4

commit v8 on v7

--- a/solution.py
+++ b/solution.py
@@ -121,8 +121,9 @@
             + jnp.sum(own_weights, axis=1, keepdims=True)
             + jnp.exp(sink - largest)
         )
-        tail_weights = (tail_weights / normalizer).astype(jnp.bfloat16)
-        own_weights = (own_weights / normalizer).astype(jnp.bfloat16)
+        inverse = 1.0 / normalizer
+        tail_weights = (tail_weights * inverse).astype(jnp.bfloat16)
+        own_weights = (own_weights * inverse).astype(jnp.bfloat16)
         mixed = jnp.dot(
             tail_weights, tail[:, head_dim:], preferred_element_type=jnp.float32
         ) + jnp.dot(own_weights, kv[:, head_dim:], preferred_element_type=jnp.float32)

time: 330 us -> 329 us (level)
  no operation moved by 1% of the time
where the time goes in v8:
time: 329 us; the launch traced here: 328 us
  waiting for transfers between devices  191 us (58%)
  matrix products  45.8 us (14%)
  Pallas kernels  28.6 us (9%)
  local copies, waits for them, and re-layouts  20.5 us (6%)
  starting transfers between devices  14.9 us (5%)
  other arithmetic  13.7 us (4%)
  between operations  13.4 us (4%)
    reduce_scatter x1, waiting for transfers between devices, local(): lax.psum_scatter(jnp.dot(hidden, w_down, preferred_element_type=jnp.float...  38.6 us
    reduce_scatter x1, waiting for transfers between devices, local(): lax.psum_scatter(partial_value.astype(jnp.bfloat16), 'tp', scatter_dimens...  38.5 us
    all_gather x1, waiting for transfers between devices, local(): residual = lax.all_gather(residual_part, 'tp', axis=1, tiled=True)  31.8 us
    pallas_call x1, Pallas kernels, attend_pallas(): pl.pallas_call(attend_kernel, grid=(peers // batch,), in_specs=[pl.BlockS...  28.6 us
    all_gather x1, waiting for transfers between devices, local(): input_rows = lax.all_gather(input_part, 'tp', axis=1, tiled=True)  28.2 us
    all_to_all x1, waiting for transfers between devices, local(): lax.all_to_all(out_slots, 'req', split_axis=0, concat_axis=0, tiled=True)  20.8 us
    all_to_all x1, waiting for transfers between devices, local(): lax.all_to_all(my_features[send_order], 'req', split_axis=0, concat_axis=...  19.8 us
    all_gather x1, waiting for transfers between devices, fetch_prefix(): shard_rows = lax.all_gather(prefix_cache, 'req', axis=0, tiled=True)  12.3 us
  transfers between devices with their start and end apart: 7, of which 7 were waited for; matrix products, arithmetic and copies ran while one was open for 8% of the time, Pallas kernels for 0%

profile of v8, /device:TPU:7, one launch (start us, length us, event | category | flops | bytes accessed | tf_op | source)
XLA Modules:
  0.0 327.7 jit_solution(2530118793672747257)
XLA Ops:
  6.5 0.7 all-gather.6.cloned.1.call-update
  7.3 0.9 reshape.525
  8.2 0.7 fusion.74
  8.9 0.1 select_reduce_fusion.4
  9.0 0.8 select_reduce_fusion.3
  9.8 3.2 constant_dynamic-slice_fusion.1
  13.0 3.2 gather_fusion
  16.2 7.8 %all-to-all-start = ((bf16[16,112,360]{2,1,0:T(8,128)(2,1)}), bf16[16,112,360]{2,1,0:T(8,128)(2,1)}, u32[]{:S(2)}, u32[]{:S(2)}) async-start(bf16[16,112,360]{2,1,0:T(8,128)(2,1)} %gather_fusion), calls=%async_computation | async-start | bytes 2752512 | tf_op jit(solution)/shard_map/all_to_all | solution.py:251
  24.0 0.0 all-gather.4.cloned.1.call-start
  24.1 0.7 fusion.87
  24.8 0.1 copy.24
  24.9 0.1 reduce
  25.0 0.1 convert_reduce_fusion
  25.1 0.7 fusion.72
  25.8 0.1 select_reduce_fusion
  25.9 19.8 %all-to-all-done = bf16[16,112,360]{2,1,0:T(8,128)(2,1)} async-done(((bf16[16,112,360]{2,1,0:T(8,128)(2,1)}), bf16[16,112,360]{2,1,0:T(8,128)(2,1)}, u32[]{:S(2)}, u32[]{:S(2)}) %all-to-all-start) | async-done | bytes 1290272 | tf_op jit(solution)/shard_map/all_to_all | solution.py:251
  45.7 3.7 %fusion.35 = bf16[768,360]{0,1:T(8,128)(2,1)} fusion(bf16[1792,360]{1,0:T(8,128)(2,1)} %bitcast.6, s32[768]{0:T(1024)S(1)} %get-tuple-element.14), kind=kOutput, calls=%fused_computation.41 | convolution fusion | flops 992557056 | bytes 1846272 | tf_op jit(solution)/shard_map/dot_general | solution.py:245
  49.4 0.0 all-gather.4.cloned.1.call-update
  49.4 0.0 reduce-scatter.3.cloned.1.call-start
  49.5 0.7 bitcast_subtract_fusion.1
  50.2 0.1 add_clamp_fusion
  50.3 0.1 min.28
  50.3 0.7 fusion.86
  51.0 0.1 iota_compare_fusion.18
  51.1 0.1 lt.82
  51.2 0.1 select_reduce_fusion.2
  51.3 0.7 gather_fusion.1
  52.0 0.7 gather_fusion.2
  52.7 0.1 copy.25
  52.8 0.1 reshape.560
  52.9 0.1 iota_add_fusion
  53.0 0.4 multiply_cosine_fusion.1
  53.4 12.3 %all-gather.6.cloned.1.call-done = bf16[64,128,1,128]{3,1,2,0:T(8,128)(2,1)} async-done(((bf16[4,128,1,128]{3,1,2,0:T(8,128)(2,1)}), bf16[64,128,1,128]{3,1,2,0:T(8,128)(2,1)}) %all-gather.6.cloned.1.call-update) | async-done | bytes 2097168 | tf_op jit(solution)/shard_map/all_gather | solution.py:174
  65.7 3.2 gather_fusion.3
  68.9 2.6 fusion.36.tail_ref
  71.5 28.2 %all-gather.4.cloned.1.call-done = bf16[768,2880]{0,1:T(8,128)(2,1)} async-done(((bf16[768,360]{0,1:T(8,128)(2,1)}), bf16[768,2880]{0,1:T(8,128)(2,1)}) %all-gather.4.cloned.1.call-update) | async-done | bytes 4423696 | tf_op jit(solution)/shard_map/all_gather | solution.py:255
  99.7 3.3 %fusion = f32[768]{0:T(1024)S(1)} fusion(bf16[768,2880]{0,1:T(8,128)(2,1)} %all-gather.4.cloned.1.call-done), kind=kLoop, calls=%fused_computation.9 | loop fusion | flops 6634752 | bytes 4426752 | tf_op jit(solution)/shard_map/reduce_sum | solution.py:18
  103.1 0.2 copy-done.1
  103.3 2.8 fusion.44
  106.1 0.4 fusion.67
  106.6 3.1 fusion.42
  109.7 0.2 subtract_convert_fusion
  110.0 0.1 pad_maximum_fusion
  110.0 3.5 %fusion.15 = bf16[1792,512]{1,0:T(8,128)(2,1)} fusion(bf16[768,512]{0,1:T(8,128)(2,1)S(1)} %bitcast.75, s32[1792]{0:T(1024)S(1)} %min.28, pred[1792]{0:T(1024)(128)(4,1)S(1)} %lt.82), kind=kOutput, calls=%fused_computation.25 | convolution fusion | flops 1412956160 | bytes 2630400 | tf_op jit(solution)/shard_map/dot_general | solution.py:241
  113.5 2.4 fusion.29
  116.0 28.6 %shard_map.145 = bf16[16,112,512]{2,1,0:T(8,128)(2,1)} custom-call(f32[8]{0:T(128)} %sink_ref.1, bf16[16,112,512]{2,1,0:T(8,128)(2,1)} %bitcast.79, bf16[16,112,128]{2,1,0:T(8,128)(2,1)} %bitcast.81, bf16[16,128,128]{2,1,0:T(8,128)(2,1)} %fusion.36.tail_ref), custom_call_target="tpu_custom_call" | custom-call | flops 880803840 | bytes 4653056 | tf_op jit(solution)/shard_map/pallas_call | solution.py:145
  144.5 7.4 %convolution_convert_fusion = bf16[768,2880]{0,1:T(8,128)(2,1)} fusion(bf16[512,2880]{0,1:T(8,128)(2,1)S(1)} %copy-done, bf16[1792,512]{1,0:T(8,128)(2,1)} %bitcast.80, s32[768]{0:T(1024)S(1)} %get-tuple-element.14), kind=kOutput, calls=%fused_computation.23 | convolution fusion | flops 3678191616 | bytes 9210880 | tf_op jit(solution)/shard_map/dot_general | solution.py:274
  152.0 0.0 reduce-scatter.3.cloned.1.call-update
  152.0 0.0 all-gather.8.cloned.1.call-start
  152.1 38.5 %reduce-scatter.3.cloned.1.call-done = bf16[768,360]{0,1:T(8,128)(2,1)} async-done(((bf16[768,2880]{0,1:T(8,128)(2,1)}), bf16[768,360]{0,1:T(8,128)(2,1)}) %reduce-scatter.3.cloned.1.call-update) | async-done | bytes 552976 | tf_op jit(solution)/shard_map/reduce_scatter | solution.py:275
  190.6 2.0 add_convert_fusion.1
  192.6 0.3 reduce-scatter.5.cloned.1.call-start
  192.9 31.8 %all-gather.8.cloned.1.call-done = bf16[768,2880]{0,1:T(8,128)(2,1)} async-done(((bf16[768,360]{0,1:T(8,128)(2,1)}), bf16[768,2880]{0,1:T(8,128)(2,1)}) %all-gather.8.cloned.1.call-update) | async-done | bytes 4423696 | tf_op jit(solution)/shard_map/all_gather | solution.py:279
  224.8 3.3 %fusion.3 = f32[768]{0:T(1024)S(1)} fusion(bf16[768,2880]{0,1:T(8,128)(2,1)} %all-gather.8.cloned.1.call-done), kind=kLoop, calls=%fused_computation.12 | loop fusion | flops 6634752 | bytes 4426752 | tf_op jit(solution)/shard_map/reduce_sum | solution.py:18
  228.1 0.2 copy-done.2
  228.3 4.6 %fusion.38 = f32[768,360]{0,1:T(8,128)} fusion(bf16[2880,360]{0,1:T(8,128)(2,1)} %param.27, bf16[768,2880]{0,1:T(8,128)(2,1)S(1)} %copy-done.2, f32[2880]{0:T(1024)S(1)} %convert_element_type.116, f32[768]{0:T(1024)S(1)} %add_rsqrt_fusion), kind=kOutput, calls=%fused_computation.43 | convolution fusion | flops 1601372160 | bytes 7617792 | tf_op jit(solution)/shard_map/dot_general | solution.py:281
  233.0 11.3 %convolution_convert_fusion.1 = bf16[768,2880]{0,1:T(8,128)(2,1)} fusion(bf16[360,2880]{1,0:T(8,128)(2,1)} %param.29, bf16[2880,360]{0,1:T(8,128)(2,1)} %param.28, bf16[768,2880]{0,1:T(8,128)(2,1)} %all-gather.8.cloned.1.call-done, f32[2880]{0:T(1024)S(1)} %convert_element_type.116, f32[768]{0:T(1024)S(1)} %add_rsqrt_fusion, f32[768,360]{0,1:T(8,128)} %fusion.38), kind=kOutput, calls=%fused_computation.24 | convolution fusion | flops 3197767680 | bytes 14115072 | tf_op jit(solution)/shard_map/dot_general | solution.py:285
  244.3 38.6 %reduce-scatter.5.cloned.1.call-done = bf16[768,360]{0,1:T(8,128)(2,1)} async-done(((bf16[768,2880]{0,1:T(8,128)(2,1)}), bf16[768,360]{0,1:T(8,128)(2,1)}) %reduce-scatter.5.cloned.1.call-update) | async-done | bytes 552976 | tf_op jit(solution)/shard_map/reduce_scatter | solution.py:284
  282.9 4.3 %fusion.18 = bf16[1792,360]{0,1:T(8,128)(2,1)} fusion(s32[1792]{0:T(1024)S(1)} %min.28, pred[1792]{0:T(1024)(128)(4,1)S(1)} %lt.82, bf16[768,360]{0,1:T(8,128)(2,1)} %reduce-scatter.5.cloned.1.call-done, bf16[768,360]{0,1:T(8,128)(2,1)S(1)} %copy-done.4), kind=kOutput, calls=%fused_computation.26 | convolution fusion | flops 995407872 | bytes 2405120 | tf_op jit(solution)/shard_map/dot_general | solution.py:241
  287.2 2.5 copy.26
  289.7 6.7 %all-to-all-start.1 = ((bf16[16,112,360]{2,1,0:T(8,128)(2,1)}), bf16[16,112,360]{2,1,0:T(8,128)(2,1)}, u32[]{:S(2)}, u32[]{:S(2)}) async-start(bf16[16,112,360]{2,1,0:T(8,128)(2,1)} %bitcast.72), calls=%async_computation.3 | async-start | bytes 2752512 | tf_op jit(solution)/shard_map/all_to_all | solution.py:292
  296.4 0.7 fusion.71
  297.1 20.8 %all-to-all-done.1 = bf16[16,112,360]{2,1,0:T(8,128)(2,1)} async-done(((bf16[16,112,360]{2,1,0:T(8,128)(2,1)}), bf16[16,112,360]{2,1,0:T(8,128)(2,1)}, u32[]{:S(2)}, u32[]{:S(2)}) %all-to-all-start.1) | async-done | bytes 1290272 | tf_op jit(solution)/shard_map/all_to_all | solution.py:292
  318.0 3.2 gather_fusion.4
  (35 shorter events, 0.2 us)
Async XLA Ops:
  6.5 138.0 %copy-start = (bf16[512,2880]{0,1:T(8,128)(2,1)S(1)}, bf16[512,2880]{0,1:T(8,128)(2,1)}, u32[]{:S(2)}) copy-start(bf16[512,2880]{0,1:T(8,128)(2,1)} %param.25) | copy-start | bytes 8847364
  6.5 59.2 %all-gather.6.cloned.1.call-start = ((), (), s32[]{:S(2)}) async-start(), calls=%async_computation.5 | async-start | bytes 2228224 | tf_op jit(solution)/shard_map/all_gather | solution.py:174
  16.2 29.5 %all-to-all-start = ((bf16[16,112,360]{2,1,0:T(8,128)(2,1)}), bf16[16,112,360]{2,1,0:T(8,128)(2,1)}, u32[]{:S(2)}, u32[]{:S(2)}) async-start(bf16[16,112,360]{2,1,0:T(8,128)(2,1)} %gather_fusion), calls=%async_computation | async-start | bytes 2752512 | tf_op jit(solution)/shard_map/all_to_all | solution.py:251
  24.0 75.7 %all-gather.4.cloned.1.call-start = ((), (), s32[]{:S(2)}) async-start(), calls=%async_computation.4 | async-start | bytes 4976640 | tf_op jit(solution)/shard_map/all_gather | solution.py:255
  45.7 3.8 %copy-start.5 = (bf16[2880]{0:T(1024)(128)(2,1)S(1)}, bf16[2880]{0:T(1024)(128)(2,1)}, u32[]{:S(2)}) copy-start(bf16[2880]{0:T(1024)(128)(2,1)} %param.22) | copy-start | bytes 17284
  45.7 5.5 %copy-start.8 = (s32[64]{0:T(128)S(1)}, s32[64]{0:T(128)}, u32[]{:S(2)}) copy-start(s32[64]{0:T(128)} %param.20) | copy-start | bytes 772
  49.4 141.2 %reduce-scatter.3.cloned.1.call-start = ((), (), s32[]{:S(2)}) async-start(), calls=%async_computation.6 | async-start | bytes 4976640 | tf_op jit(solution)/shard_map/reduce_scatter | solution.py:275
  99.7 3.6 %copy-start.1 = (bf16[768,2880]{0,1:T(8,128)(2,1)S(1)}, bf16[768,2880]{0,1:T(8,128)(2,1)}, u32[]{:S(2)}) copy-start(bf16[768,2880]{0,1:T(8,128)(2,1)} %all-gather.4.cloned.1.call-done) | copy-start | bytes 13271044
  103.3 3.3 %copy-start.7 = (bf16[2880,512]{1,0:T(8,128)(2,1)S(1)}, bf16[2880,512]{1,0:T(8,128)(2,1)}, u32[]{:S(2)}) copy-start(bf16[2880,512]{1,0:T(8,128)(2,1)} %param.23) | copy-start | bytes 8847364
  152.0 38.6 %copy-start.3 = (bf16[768,360]{0,1:T(8,128)(2,1)S(1)}, bf16[768,360]{0,1:T(8,128)(2,1)}, u32[]{:S(2)}) copy-start(bf16[768,360]{0,1:T(8,128)(2,1)} %fusion.35) | copy-start | bytes 1658884
  152.0 40.9 %copy-start.6 = (bf16[2880]{0:T(1024)(128)(2,1)S(1)}, bf16[2880]{0:T(1024)(128)(2,1)}, u32[]{:S(2)}) copy-start(bf16[2880]{0:T(1024)(128)(2,1)} %param.26) | copy-start | bytes 17284
  152.0 72.8 %all-gather.8.cloned.1.call-start = ((), (), s32[]{:S(2)}) async-start(), calls=%async_computation.7 | async-start | bytes 4976640 | tf_op jit(solution)/shard_map/all_gather | solution.py:279
  192.6 90.2 %reduce-scatter.5.cloned.1.call-start = ((), (), s32[]{:S(2)}) async-start(), calls=%async_computation.8 | async-start | bytes 4976640 | tf_op jit(solution)/shard_map/reduce_scatter | solution.py:284
  224.8 3.6 %copy-start.2 = (bf16[768,2880]{0,1:T(8,128)(2,1)S(1)}, bf16[768,2880]{0,1:T(8,128)(2,1)}, u32[]{:S(2)}) copy-start(bf16[768,2880]{0,1:T(8,128)(2,1)} %all-gather.8.cloned.1.call-done) | copy-start | bytes 13271044
  244.3 38.6 %copy-start.4 = (bf16[768,360]{0,1:T(8,128)(2,1)S(1)}, bf16[768,360]{0,1:T(8,128)(2,1)}, u32[]{:S(2)}) copy-start(bf16[768,360]{0,1:T(8,128)(2,1)} %add_convert_fusion.1) | copy-start | bytes 1658884
  289.7 28.3 %all-to-all-start.1 = ((bf16[16,112,360]{2,1,0:T(8,128)(2,1)}), bf16[16,112,360]{2,1,0:T(8,128)(2,1)}, u32[]{:S(2)}, u32[]{:S(2)}) async-start(bf16[16,112,360]{2,1,0:T(8,128)(2,1)} %bitcast.72), calls=%async_computation.3 | async-start | bytes 2752512 | tf_op jit(solution)/shard_map/all_to_all | solution.py:292
Sparse Core Ops, SparseCore 0:
  9.5 56.1 all-gather.5
  67.4 32.2 all-gather.3
  152.1 38.4 reduce-scatter.2
  192.8 31.9 all-gather.7
  244.4 38.4 reduce-scatter.4

commit v9 on v8

--- a/solution.py
+++ b/solution.py
@@ -248,9 +248,11 @@
     my_features = lax.dynamic_slice_in_dim(
         suffix_tokens, tensor_index * feature_share, feature_share, 2
     )
-    landed = lax.all_to_all(
-        my_features[send_order], "req", split_axis=0, concat_axis=0, tiled=True
-    )
+    send_pick = (send_order[:, None] == peer_ids[None, :]).astype(jnp.bfloat16)
+    outgoing = jnp.einsum(
+        "dk,ktf->dtf", send_pick, my_features, preferred_element_type=jnp.float32
+    ).astype(jnp.bfloat16)
+    landed = lax.all_to_all(outgoing, "req", split_axis=0, concat_axis=0, tiled=True)
     input_part = to_packed(landed.reshape(peers * slot_length, feature_share))
     input_rows = lax.all_gather(input_part, "tp", axis=1, tiled=True)
     row_total = input_part.shape[0]
@@ -290,7 +292,10 @@
     out_rows = (residual_part.astype(jnp.float32) + down_sum).astype(jnp.bfloat16)
     out_slots = to_slots(out_rows)
     returned = lax.all_to_all(out_slots, "req", split_axis=0, concat_axis=0, tiled=True)
-    return returned[my_row]
+    return_pick = (my_row[:, None] == peer_ids[None, :]).astype(jnp.bfloat16)
+    return jnp.einsum(
+        "kd,dtf->ktf", return_pick, returned, preferred_element_type=jnp.float32
+    ).astype(jnp.bfloat16)
 
 
 def solution(mesh):

time: 329 us -> 322 us (0.979)
  blocking collectives: 0 us -> 26.9 us
  waiting for transfers between devices: 191 us -> 173 us
  starting transfers between devices: 14.9 us -> 8.2 us
  local copies, waits for them, and re-layouts: 20.5 us -> 14.2 us
    all_to_all x0 -> x1, blocking collectives: none -> 26.9 us  [local(): lax.all_to_all(out_slots, 'req', split_axis=0, concat_axis=0, tiled=True)]
    all_to_all x2 -> x1, waiting for transfers between devices: 40.6 us -> 18.7 us  [local(): lax.all_to_all(outgoing, 'req', split_axis=0, concat_axis=0, tiled=True)]
    all_to_all x2 -> x1, starting transfers between devices: 14.5 us -> 7.81 us  [local(): lax.all_to_all(outgoing, 'req', split_axis=0, concat_axis=0, tiled=True)]
    gather x2 -> x0, local copies, waits for them, and re-layouts: 6.34 us -> none  [the longest x1 3.19 us: local(): my_features[send_order]]
    all_gather x1, waiting for transfers between devices: 12.3 us -> 16.4 us  [fetch_prefix(): shard_rows = lax.all_gather(prefix_cache, 'req', axis=0, tiled=True)]
  transfers between devices with their start and end apart: 7 -> 6, of which waited for: 7 -> 6; matrix products, arithmetic and copies ran while one was open for 8% -> 6% of each run, Pallas kernels for 0% -> 0%
where the time goes in v9:
time: 322 us; the launch traced here: 321 us
  waiting for transfers between devices  173 us (54%)
  matrix products  44.5 us (14%)
  Pallas kernels  28.6 us (9%)
  blocking collectives  26.9 us (8%)
  local copies, waits for them, and re-layouts  14.2 us (4%)
  between operations  13.4 us (4%)
  other arithmetic  12.4 us (4%)
  starting transfers between devices  8.2 us (3%)
    reduce_scatter x1, waiting for transfers between devices, local(): lax.psum_scatter(jnp.dot(hidden, w_down, preferred_element_type=jnp.float...  38.6 us
    reduce_scatter x1, waiting for transfers between devices, local(): lax.psum_scatter(partial_value.astype(jnp.bfloat16), 'tp', scatter_dimens...  38.5 us
    all_gather x1, waiting for transfers between devices, local(): residual = lax.all_gather(residual_part, 'tp', axis=1, tiled=True)  31.9 us
    pallas_call x1, Pallas kernels, attend_pallas(): pl.pallas_call(attend_kernel, grid=(peers // batch,), in_specs=[pl.BlockS...  28.6 us
    all_gather x1, waiting for transfers between devices, local(): input_rows = lax.all_gather(input_part, 'tp', axis=1, tiled=True)  28.2 us
    all_to_all x1, blocking collectives, local(): lax.all_to_all(out_slots, 'req', split_axis=0, concat_axis=0, tiled=True)  26.9 us
    all_to_all x1, waiting for transfers between devices, local(): lax.all_to_all(outgoing, 'req', split_axis=0, concat_axis=0, tiled=True)  18.7 us
    all_gather x1, waiting for transfers between devices, fetch_prefix(): shard_rows = lax.all_gather(prefix_cache, 'req', axis=0, tiled=True)  16.4 us
  transfers between devices with their start and end apart: 6, of which 6 were waited for; matrix products, arithmetic and copies ran while one was open for 6% of the time, Pallas kernels for 0%

profile of v9, /device:TPU:7, one launch (start us, length us, event | category | flops | bytes accessed | tf_op | source)
XLA Modules:
  0.0 321.3 jit_solution(10698392097621156287)
XLA Ops:
  6.5 0.7 all-gather.6.cloned.1.call-update
  7.3 0.8 fusion.76
  8.1 0.1 select_reduce_fusion.4
  8.2 2.1 constant_dynamic-slice_fusion
  10.3 0.6 convolution_convert_fusion.3
  10.9 1.4 copy.37
  12.3 7.8 %all-to-all-start = ((bf16[16,112,360]{2,1,0:T(8,128)(2,1)}), bf16[16,112,360]{2,1,0:T(8,128)(2,1)}, u32[]{:S(2)}, u32[]{:S(2)}) async-start(bf16[16,112,360]{2,1,0:T(8,128)(2,1)} %copy.37), calls=%async_computation | async-start | bytes 2752512 | tf_op jit(solution)/shard_map/all_to_all | solution.py:255
  20.1 0.0 all-gather.4.cloned.1.call-start
  20.2 0.7 fusion.93
  20.9 0.1 copy.35
  21.0 0.1 reduce
  21.1 0.1 reshape.487
  21.2 0.1 select_reduce_fusion.3
  21.3 0.1 convert_reduce_fusion
  21.4 0.7 fusion.79
  22.1 0.1 select_reduce_fusion
  22.2 18.7 %all-to-all-done = bf16[16,112,360]{2,1,0:T(8,128)(2,1)} async-done(((bf16[16,112,360]{2,1,0:T(8,128)(2,1)}), bf16[16,112,360]{2,1,0:T(8,128)(2,1)}, u32[]{:S(2)}, u32[]{:S(2)}) %all-to-all-start) | async-done | bytes 1290272 | tf_op jit(solution)/shard_map/all_to_all | solution.py:255
  40.9 3.7 %fusion.37 = bf16[768,360]{0,1:T(8,128)(2,1)} fusion(bf16[1792,360]{1,0:T(8,128)(2,1)} %bitcast.6, s32[768]{0:T(1024)S(1)} %get-tuple-element.14), kind=kOutput, calls=%fused_computation.43 | convolution fusion | flops 992557056 | bytes 1846272 | tf_op jit(solution)/shard_map/dot_general | solution.py:245
  44.6 0.0 all-gather.4.cloned.1.call-update
  44.6 0.0 reduce-scatter.3.cloned.1.call-start
  44.6 0.7 fusion.92
  45.3 0.1 iota_compare_fusion.19
  45.4 0.1 lt.62
  45.5 0.7 bitcast_subtract_fusion.1
  46.2 0.1 add_clamp_fusion
  46.3 0.1 min.28
  46.4 0.1 select_reduce_fusion.2
  46.5 0.7 gather_fusion.1
  47.2 0.7 gather_fusion
  47.9 0.1 copy.38
  47.9 0.1 reshape.514
  48.1 0.1 iota_add_fusion
  48.2 0.4 multiply_cosine_fusion.1
  48.6 16.4 %all-gather.6.cloned.1.call-done = bf16[64,128,1,128]{3,1,2,0:T(8,128)(2,1)} async-done(((bf16[4,128,1,128]{3,1,2,0:T(8,128)(2,1)}), bf16[64,128,1,128]{3,1,2,0:T(8,128)(2,1)}) %all-gather.6.cloned.1.call-update) | async-done | bytes 2097168 | tf_op jit(solution)/shard_map/all_gather | solution.py:174
  65.0 3.2 %gather_fusion.2 = bf16[32,128,128]{2,1,0:T(8,128)(2,1)} fusion(bf16[64,128,128]{2,1,0:T(8,128)(2,1)} %bitcast.74, s32[1024]{0:T(1024)S(1)} %pad_clamp_fusion), kind=kCustom, calls=%fused_computation.2 | custom fusion | bytes 2097280 | tf_op jit(solution)/shard_map/gather | solution.py:177
  68.3 2.5 fusion.38.tail_ref
  70.8 28.2 %all-gather.4.cloned.1.call-done = bf16[768,2880]{0,1:T(8,128)(2,1)} async-done(((bf16[768,360]{0,1:T(8,128)(2,1)}), bf16[768,2880]{0,1:T(8,128)(2,1)}) %all-gather.4.cloned.1.call-update) | async-done | bytes 4423696 | tf_op jit(solution)/shard_map/all_gather | solution.py:257
  99.0 3.3 %fusion = f32[768]{0:T(1024)S(1)} fusion(bf16[768,2880]{0,1:T(8,128)(2,1)} %all-gather.4.cloned.1.call-done), kind=kLoop, calls=%fused_computation.7 | loop fusion | flops 6634752 | bytes 4426752 | tf_op jit(solution)/shard_map/reduce_sum | solution.py:18
  102.4 0.2 copy-done.2
  102.6 2.8 fusion.46
  105.4 0.4 fusion.69
  105.9 3.1 fusion.44
  109.0 0.2 subtract_convert_fusion
  109.3 0.1 pad_maximum_fusion
  109.3 3.5 %fusion.15 = bf16[1792,512]{1,0:T(8,128)(2,1)} fusion(bf16[768,512]{0,1:T(8,128)(2,1)S(1)} %bitcast.73, s32[1792]{0:T(1024)S(1)} %min.28, pred[1792]{0:T(1024)(128)(4,1)S(1)} %lt.62), kind=kOutput, calls=%fused_computation.23 | convolution fusion | flops 1412956160 | bytes 2630400 | tf_op jit(solution)/shard_map/dot_general | solution.py:241
  112.8 2.4 fusion.29
  115.3 28.6 %shard_map.145 = bf16[16,112,512]{2,1,0:T(8,128)(2,1)} custom-call(f32[8]{0:T(128)} %sink_ref.1, bf16[16,112,512]{2,1,0:T(8,128)(2,1)} %bitcast.77, bf16[16,112,128]{2,1,0:T(8,128)(2,1)} %bitcast.79, bf16[16,128,128]{2,1,0:T(8,128)(2,1)} %fusion.38.tail_ref), custom_call_target="tpu_custom_call" | custom-call | flops 880803840 | bytes 4653056 | tf_op jit(solution)/shard_map/pallas_call | solution.py:145
  143.8 7.5 %convolution_convert_fusion = bf16[768,2880]{0,1:T(8,128)(2,1)} fusion(bf16[512,2880]{0,1:T(8,128)(2,1)S(1)} %copy-done, bf16[1792,512]{1,0:T(8,128)(2,1)} %bitcast.78, s32[768]{0:T(1024)S(1)} %get-tuple-element.14), kind=kOutput, calls=%fused_computation.21 | convolution fusion | flops 3678191616 | bytes 9210880 | tf_op jit(solution)/shard_map/dot_general | solution.py:276
  151.3 0.0 all-gather.8.cloned.1.call-start
  151.4 38.5 %reduce-scatter.3.cloned.1.call-done = bf16[768,360]{0,1:T(8,128)(2,1)} async-done(((bf16[768,2880]{0,1:T(8,128)(2,1)}), bf16[768,360]{0,1:T(8,128)(2,1)}) %reduce-scatter.3.cloned.1.call-update) | async-done | bytes 552976 | tf_op jit(solution)/shard_map/reduce_scatter | solution.py:277
  189.9 2.2 add_convert_fusion.1
  192.1 0.3 reduce-scatter.5.cloned.1.call-start
  192.4 31.9 %all-gather.8.cloned.1.call-done = bf16[768,2880]{0,1:T(8,128)(2,1)} async-done(((bf16[768,360]{0,1:T(8,128)(2,1)}), bf16[768,2880]{0,1:T(8,128)(2,1)}) %all-gather.8.cloned.1.call-update) | async-done | bytes 4423696 | tf_op jit(solution)/shard_map/all_gather | solution.py:281
  224.3 3.3 %fusion.3 = f32[768]{0:T(1024)S(1)} fusion(bf16[768,2880]{0,1:T(8,128)(2,1)} %all-gather.8.cloned.1.call-done), kind=kLoop, calls=%fused_computation.10 | loop fusion | flops 6634752 | bytes 4426752 | tf_op jit(solution)/shard_map/reduce_sum | solution.py:18
  227.6 0.2 copy-done.3
  227.9 3.1 fusion.40
  230.9 11.3 %convolution_convert_fusion.1 = bf16[768,2880]{0,1:T(8,128)(2,1)} fusion(bf16[360,2880]{1,0:T(8,128)(2,1)} %param.29, bf16[2880,360]{0,1:T(8,128)(2,1)} %param.28, bf16[768,2880]{0,1:T(8,128)(2,1)} %all-gather.8.cloned.1.call-done, f32[2880]{0:T(1024)S(1)} %convert_element_type.125, f32[768]{0:T(1024)S(1)} %add_rsqrt_fusion, f32[768,360]{0,1:T(8,128)} %fusion.40), kind=kOutput, calls=%fused_computation.22 | convolution fusion | flops 3197767680 | bytes 14115072 | tf_op jit(solution)/shard_map/dot_general | solution.py:287
  242.2 0.0 reduce-scatter.5.cloned.1.call-update
  242.3 38.6 %reduce-scatter.5.cloned.1.call-done = bf16[768,360]{0,1:T(8,128)(2,1)} async-done(((bf16[768,2880]{0,1:T(8,128)(2,1)}), bf16[768,360]{0,1:T(8,128)(2,1)}) %reduce-scatter.5.cloned.1.call-update) | async-done | bytes 552976 | tf_op jit(solution)/shard_map/reduce_scatter | solution.py:286
  280.8 3.5 %fusion.18 = bf16[1792,360]{0,1:T(8,128)(2,1)S(1)} fusion(s32[1792]{0:T(1024)S(1)} %min.28, pred[1792]{0:T(1024)(128)(4,1)S(1)} %lt.62, bf16[768,360]{0,1:T(8,128)(2,1)} %reduce-scatter.5.cloned.1.call-done, bf16[768,360]{0,1:T(8,128)(2,1)S(1)} %copy-done.5), kind=kOutput, calls=%fused_computation.24 | convolution fusion | flops 995407872 | bytes 2405120 | tf_op jit(solution)/shard_map/dot_general | solution.py:241
  284.3 1.5 copy.39
  285.9 26.9 %all_to_all.10 = bf16[16,112,360]{2,1,0:T(8,128)(2,1)S(1)} all-to-all(bf16[16,112,360]{2,1,0:T(8,128)(2,1)} %bitcast.70), channel_id=1, replica_groups=mesh['req'=16,'tp'=8] {'req'}, dimensions={0} | all-to-all | bytes 2580480 | tf_op jit(solution)/shard_map/all_to_all | solution.py:294
  312.8 0.6 convolution_convert_fusion.2
  313.4 1.4 copy.41
  (40 shorter events, 0.2 us)
Async XLA Ops:
  6.5 137.3 %copy-start = (bf16[512,2880]{0,1:T(8,128)(2,1)S(1)}, bf16[512,2880]{0,1:T(8,128)(2,1)}, u32[]{:S(2)}) copy-start(bf16[512,2880]{0,1:T(8,128)(2,1)} %param.25) | copy-start | bytes 8847364
  6.5 58.5 %all-gather.6.cloned.1.call-start = ((), (), s32[]{:S(2)}) async-start(), calls=%async_computation.5 | async-start | bytes 2228224 | tf_op jit(solution)/shard_map/all_gather | solution.py:174
  10.9 10.2 %copy-start.9 = (s32[256]{0:T(256)S(1)}, s32[256]{0:T(256)}, u32[]{:S(2)}) copy-start(s32[256]{0:T(256)} %param.18) | copy-start | bytes 3076
  10.9 10.3 %copy-start.6 = (s32[16,16]{1,0:T(8,128)S(1)}, s32[16,16]{1,0:T(8,128)}, u32[]{:S(2)}) copy-start(s32[16,16]{1,0:T(8,128)} %param.17) | copy-start | bytes 3076
  12.3 28.6 %all-to-all-start = ((bf16[16,112,360]{2,1,0:T(8,128)(2,1)}), bf16[16,112,360]{2,1,0:T(8,128)(2,1)}, u32[]{:S(2)}, u32[]{:S(2)}) async-start(bf16[16,112,360]{2,1,0:T(8,128)(2,1)} %copy.37), calls=%async_computation | async-start | bytes 2752512 | tf_op jit(solution)/shard_map/all_to_all | solution.py:255
  20.1 78.9 %all-gather.4.cloned.1.call-start = ((), (), s32[]{:S(2)}) async-start(), calls=%async_computation.4 | async-start | bytes 4976640 | tf_op jit(solution)/shard_map/all_gather | solution.py:257
  40.9 5.5 %copy-start.12 = (s32[64]{0:T(128)S(1)}, s32[64]{0:T(128)}, u32[]{:S(2)}) copy-start(s32[64]{0:T(128)} %param.20) | copy-start | bytes 772
  40.9 7.2 %copy-start.7 = (bf16[2880]{0:T(1024)(128)(2,1)S(1)}, bf16[2880]{0:T(1024)(128)(2,1)}, u32[]{:S(2)}) copy-start(bf16[2880]{0:T(1024)(128)(2,1)} %param.22) | copy-start | bytes 17284
  44.6 145.3 %reduce-scatter.3.cloned.1.call-start = ((), (), s32[]{:S(2)}) async-start(), calls=%async_computation.6 | async-start | bytes 4976640 | tf_op jit(solution)/shard_map/reduce_scatter | solution.py:277
  99.0 3.6 %copy-start.2 = (bf16[768,2880]{0,1:T(8,128)(2,1)S(1)}, bf16[768,2880]{0,1:T(8,128)(2,1)}, u32[]{:S(2)}) copy-start(bf16[768,2880]{0,1:T(8,128)(2,1)} %all-gather.4.cloned.1.call-done) | copy-start | bytes 13271044
  102.6 3.3 %copy-start.10 = (bf16[2880,512]{1,0:T(8,128)(2,1)S(1)}, bf16[2880,512]{1,0:T(8,128)(2,1)}, u32[]{:S(2)}) copy-start(bf16[2880,512]{1,0:T(8,128)(2,1)} %param.23) | copy-start | bytes 8847364
  151.3 38.6 %copy-start.4 = (bf16[768,360]{0,1:T(8,128)(2,1)S(1)}, bf16[768,360]{0,1:T(8,128)(2,1)}, u32[]{:S(2)}) copy-start(bf16[768,360]{0,1:T(8,128)(2,1)} %fusion.37) | copy-start | bytes 1658884
  151.3 41.1 %copy-start.8 = (bf16[2880]{0:T(1024)(128)(2,1)S(1)}, bf16[2880]{0:T(1024)(128)(2,1)}, u32[]{:S(2)}) copy-start(bf16[2880]{0:T(1024)(128)(2,1)} %param.26) | copy-start | bytes 17284
  151.3 73.0 %all-gather.8.cloned.1.call-start = ((), (), s32[]{:S(2)}) async-start(), calls=%async_computation.7 | async-start | bytes 4976640 | tf_op jit(solution)/shard_map/all_gather | solution.py:281
  189.9 37.8 %copy-start.11 = (bf16[2880,360]{0,1:T(8,128)(2,1)S(1)}, bf16[2880,360]{0,1:T(8,128)(2,1)}, u32[]{:S(2)}) copy-start(bf16[2880,360]{0,1:T(8,128)(2,1)} %param.27) | copy-start | bytes 6220804
  192.1 88.7 %reduce-scatter.5.cloned.1.call-start = ((), (), s32[]{:S(2)}) async-start(), calls=%async_computation.8 | async-start | bytes 4976640 | tf_op jit(solution)/shard_map/reduce_scatter | solution.py:286
  224.3 3.6 %copy-start.3 = (bf16[768,2880]{0,1:T(8,128)(2,1)S(1)}, bf16[768,2880]{0,1:T(8,128)(2,1)}, u32[]{:S(2)}) copy-start(bf16[768,2880]{0,1:T(8,128)(2,1)} %all-gather.8.cloned.1.call-done) | copy-start | bytes 13271044
  242.2 38.6 %copy-start.5 = (bf16[768,360]{0,1:T(8,128)(2,1)S(1)}, bf16[768,360]{0,1:T(8,128)(2,1)}, u32[]{:S(2)}) copy-start(bf16[768,360]{0,1:T(8,128)(2,1)} %add_convert_fusion.1) | copy-start | bytes 1658884
  285.9 28.9 %copy-start.1 = (bf16[512,2880]{0,1:T(8,128)(2,1)S(1)}, bf16[512,2880]{0,1:T(8,128)(2,1)}, u32[]{:S(2)}) copy-start(bf16[512,2880]{0,1:T(8,128)(2,1)} %param.25) | copy-start | bytes 8847364
Sparse Core Ops, SparseCore 0:
  9.5 55.4 all-gather.5
  66.7 32.2 all-gather.3
  151.4 38.4 reduce-scatter.2
  192.2 31.9 all-gather.7
  242.4 38.4 reduce-scatter.4

commit v10 on v9

--- a/solution.py
+++ b/solution.py
@@ -244,7 +244,6 @@
     def to_packed(values):
         return jnp.dot(pack_pick, values, preferred_element_type=jnp.float32).astype(values.dtype)
 
-    tail_rows = fetch_prefix(arriving_attach, prefix_cache, block_of_slot, WINDOW)
     my_features = lax.dynamic_slice_in_dim(
         suffix_tokens, tensor_index * feature_share, feature_share, 2
     )
@@ -256,6 +255,8 @@
     input_part = to_packed(landed.reshape(peers * slot_length, feature_share))
     input_rows = lax.all_gather(input_part, "tp", axis=1, tiled=True)
     row_total = input_part.shape[0]
+    prefix_after, input_rows = lax.optimization_barrier((prefix_cache, input_rows))
+    tail_rows = fetch_prefix(arriving_attach, prefix_after, block_of_slot, WINDOW)
     normed_in = norm_rows(input_rows, attn_gain)
     queries = jnp.dot(normed_in, w_query, preferred_element_type=jnp.float32).reshape(
         row_total, -1, head_dim

time: 322 us -> 334 us (1.037)
  waiting for transfers between devices: 173 us -> 183 us
    all_gather x1, waiting for transfers between devices: 16.4 us -> 29 us  [fetch_prefix(): shard_rows = lax.all_gather(prefix_cache, 'req', axis=0, tiled=True)]
  transfers between devices with their start and end apart: 6 -> 6, of which waited for: 6 -> 6; matrix products, arithmetic and copies ran while one was open for 6% -> 7% of each run, Pallas kernels for 0% -> 0%
where the time goes in v10:
time: 334 us; the launch traced here: 333 us
  waiting for transfers between devices  183 us (55%)
  matrix products  45 us (13%)
  Pallas kernels  28.6 us (9%)
  blocking collectives  26.9 us (8%)
  local copies, waits for them, and re-layouts  15 us (4%)
  between operations  13.4 us (4%)
  other arithmetic  12.4 us (4%)
  starting transfers between devices  8.24 us (2%)
    reduce_scatter x1, waiting for transfers between devices, local(): lax.psum_scatter(jnp.dot(hidden, w_down, preferred_element_type=jnp.float...  38.6 us
    reduce_scatter x1, waiting for transfers between devices, local(): lax.psum_scatter(partial_value.astype(jnp.bfloat16), 'tp', scatter_dimens...  37.9 us
    all_gather x1, waiting for transfers between devices, local(): residual = lax.all_gather(residual_part, 'tp', axis=1, tiled=True)  31.8 us
    all_gather x1, waiting for transfers between devices, fetch_prefix(): shard_rows = lax.all_gather(prefix_cache, 'req', axis=0, tiled=True)  29 us
    all_gather x1, waiting for transfers between devices, local(): input_rows = lax.all_gather(input_part, 'tp', axis=1, tiled=True)  29 us
    pallas_call x1, Pallas kernels, attend_pallas(): pl.pallas_call(attend_kernel, grid=(peers // batch,), in_specs=[pl.BlockS...  28.6 us
    all_to_all x1, blocking collectives, local(): lax.all_to_all(out_slots, 'req', split_axis=0, concat_axis=0, tiled=True)  26.9 us
    all_to_all x1, waiting for transfers between devices, local(): lax.all_to_all(outgoing, 'req', split_axis=0, concat_axis=0, tiled=True)  16.9 us
  transfers between devices with their start and end apart: 6, of which 6 were waited for; matrix products, arithmetic and copies ran while one was open for 7% of the time, Pallas kernels for 0%

profile of v10, /device:TPU:7, one launch (start us, length us, event | category | flops | bytes accessed | tf_op | source)
XLA Modules:
  0.0 332.8 jit_solution(2719406748595489675)
XLA Ops:
  6.5 0.8 fusion.76
  7.4 0.1 select_reduce_fusion.4
  7.5 2.1 constant_dynamic-slice_fusion
  9.6 0.6 convolution_convert_fusion.3
  10.2 1.4 copy.37
  11.6 7.8 %all-to-all-start = ((bf16[16,112,360]{2,1,0:T(8,128)(2,1)}), bf16[16,112,360]{2,1,0:T(8,128)(2,1)}, u32[]{:S(2)}, u32[]{:S(2)}) async-start(bf16[16,112,360]{2,1,0:T(8,128)(2,1)} %copy.37), calls=%async_computation | async-start | bytes 2752512 | tf_op jit(solution)/shard_map/all_to_all | solution.py:254
  19.4 0.0 all-gather.4.cloned.1.call-start
  19.4 0.7 fusion.93
  20.1 0.1 copy.35
  20.2 0.1 reduce
  20.4 0.1 reshape.487
  20.5 0.1 select_reduce_fusion.3
  20.6 0.1 convert_reduce_fusion
  20.7 0.7 fusion.79
  21.4 0.1 select_reduce_fusion
  21.5 16.9 %all-to-all-done = bf16[16,112,360]{2,1,0:T(8,128)(2,1)} async-done(((bf16[16,112,360]{2,1,0:T(8,128)(2,1)}), bf16[16,112,360]{2,1,0:T(8,128)(2,1)}, u32[]{:S(2)}, u32[]{:S(2)}) %all-to-all-start) | async-done | bytes 1290272 | tf_op jit(solution)/shard_map/all_to_all | solution.py:254
  38.3 3.7 %fusion.37 = bf16[768,360]{0,1:T(8,128)(2,1)} fusion(bf16[1792,360]{1,0:T(8,128)(2,1)} %bitcast.6, s32[768]{0:T(1024)S(1)} %get-tuple-element.18), kind=kOutput, calls=%fused_computation.43 | convolution fusion | flops 992557056 | bytes 1846272 | tf_op jit(solution)/shard_map/dot_general | solution.py:245
  42.0 0.0 all-gather.6.cloned.1.call-start
  42.1 0.7 fusion.92
  42.8 0.1 iota_compare_fusion.19
  42.9 0.1 lt.62
  43.0 0.7 bitcast_subtract_fusion.1
  43.7 0.1 add_clamp_fusion
  43.7 0.1 min.28
  43.9 0.1 select_reduce_fusion.2
  44.0 0.7 gather_fusion.1
  44.6 0.7 gather_fusion
  45.3 0.1 copy.38
  45.4 0.1 reshape.514
  45.5 29.0 %all-gather.4.cloned.1.call-done = bf16[768,2880]{0,1:T(8,128)(2,1)} async-done(((bf16[768,360]{0,1:T(8,128)(2,1)}), bf16[768,2880]{0,1:T(8,128)(2,1)}) %all-gather.4.cloned.1.call-update) | async-done | bytes 4423696 | tf_op jit(solution)/shard_map/all_gather | solution.py:256
  74.6 0.0 all-gather.6.cloned.1.call-update
  74.6 0.0 reduce-scatter.3.cloned.1.call-start
  74.6 0.1 iota_add_fusion
  74.7 0.4 multiply_cosine_fusion.1
  75.2 3.4 %fusion = f32[768]{0:T(1024)S(1)} fusion(bf16[768,2880]{0,1:T(8,128)(2,1)} %all-gather.4.cloned.1.call-done), kind=kLoop, calls=%fused_computation.7 | loop fusion | flops 6634752 | bytes 4426752 | tf_op jit(solution)/shard_map/reduce_sum | solution.py:18
  78.5 0.2 copy-done.2
  78.7 4.8 %fusion.44 = f32[768,512]{0,1:T(8,128)S(1)} fusion(bf16[2880,512]{1,0:T(8,128)(2,1)} %param.23, bf16[768,2880]{0,1:T(8,128)(2,1)S(1)} %copy-done.2, f32[2880]{0:T(1024)S(1)} %convert_element_type.111, f32[768]{0:T(1024)S(1)} %add_rsqrt_fusion.1), kind=kOutput, calls=%fused_computation.47 | convolution fusion | flops 2273771520 | bytes 8960256 | tf_op jit(solution)/shard_map/dot_general | solution.py:261
  83.6 0.2 subtract_convert_fusion
  83.8 0.1 pad_maximum_fusion
  83.9 0.8 copy-done.11
  84.7 1.6 fusion.46
  86.3 0.4 fusion.69
  86.7 2.6 fusion.29
  89.3 3.3 fusion.15
  92.6 29.0 %all-gather.6.cloned.1.call-done = bf16[64,128,1,128]{3,1,2,0:T(8,128)(2,1)} async-done(((bf16[4,128,1,128]{3,1,2,0:T(8,128)(2,1)}), bf16[64,128,1,128]{3,1,2,0:T(8,128)(2,1)}) %all-gather.6.cloned.1.call-update) | async-done | bytes 2097168 | tf_op jit(solution)/shard_map/all_gather | solution.py:174
  121.7 3.2 gather_fusion.2
  124.9 2.6 fusion.38.tail_ref
  127.5 28.6 %shard_map.145 = bf16[16,112,512]{2,1,0:T(8,128)(2,1)} custom-call(f32[8]{0:T(128)} %sink_ref.1, bf16[16,112,512]{2,1,0:T(8,128)(2,1)} %bitcast.77, bf16[16,112,128]{2,1,0:T(8,128)(2,1)} %bitcast.79, bf16[16,128,128]{2,1,0:T(8,128)(2,1)} %fusion.38.tail_ref), custom_call_target="tpu_custom_call" | custom-call | flops 880803840 | bytes 4653056 | tf_op jit(solution)/shard_map/pallas_call | solution.py:145
  156.0 7.5 %convolution_convert_fusion = bf16[768,2880]{0,1:T(8,128)(2,1)} fusion(bf16[512,2880]{0,1:T(8,128)(2,1)S(1)} %copy-done, bf16[1792,512]{1,0:T(8,128)(2,1)} %bitcast.78, s32[768]{0:T(1024)S(1)} %get-tuple-element.18), kind=kOutput, calls=%fused_computation.21 | convolution fusion | flops 3678191616 | bytes 9210880 | tf_op jit(solution)/shard_map/dot_general | solution.py:277
  163.5 0.0 all-gather.8.cloned.1.call-start
  163.6 37.9 %reduce-scatter.3.cloned.1.call-done = bf16[768,360]{0,1:T(8,128)(2,1)} async-done(((bf16[768,2880]{0,1:T(8,128)(2,1)}), bf16[768,360]{0,1:T(8,128)(2,1)}) %reduce-scatter.3.cloned.1.call-update) | async-done | bytes 552976 | tf_op jit(solution)/shard_map/reduce_scatter | solution.py:278
  201.5 2.2 add_convert_fusion.1
  203.7 0.3 reduce-scatter.5.cloned.1.call-start
  204.0 31.8 %all-gather.8.cloned.1.call-done = bf16[768,2880]{0,1:T(8,128)(2,1)} async-done(((bf16[768,360]{0,1:T(8,128)(2,1)}), bf16[768,2880]{0,1:T(8,128)(2,1)}) %all-gather.8.cloned.1.call-update) | async-done | bytes 4423696 | tf_op jit(solution)/shard_map/all_gather | solution.py:282
  235.8 3.3 %fusion.3 = f32[768]{0:T(1024)S(1)} fusion(bf16[768,2880]{0,1:T(8,128)(2,1)} %all-gather.8.cloned.1.call-done), kind=kLoop, calls=%fused_computation.10 | loop fusion | flops 6634752 | bytes 4426752 | tf_op jit(solution)/shard_map/reduce_sum | solution.py:18
  239.2 0.2 copy-done.3
  239.4 3.1 fusion.40
  242.5 11.3 %convolution_convert_fusion.1 = bf16[768,2880]{0,1:T(8,128)(2,1)} fusion(bf16[360,2880]{1,0:T(8,128)(2,1)} %param.29, bf16[2880,360]{0,1:T(8,128)(2,1)} %param.28, bf16[768,2880]{0,1:T(8,128)(2,1)} %all-gather.8.cloned.1.call-done, f32[2880]{0:T(1024)S(1)} %convert_element_type.125, f32[768]{0:T(1024)S(1)} %add_rsqrt_fusion, f32[768,360]{0,1:T(8,128)} %fusion.40), kind=kOutput, calls=%fused_computation.22 | convolution fusion | flops 3197767680 | bytes 14115072 | tf_op jit(solution)/shard_map/dot_general | solution.py:288
  253.8 38.6 %reduce-scatter.5.cloned.1.call-done = bf16[768,360]{0,1:T(8,128)(2,1)} async-done(((bf16[768,2880]{0,1:T(8,128)(2,1)}), bf16[768,360]{0,1:T(8,128)(2,1)}) %reduce-scatter.5.cloned.1.call-update) | async-done | bytes 552976 | tf_op jit(solution)/shard_map/reduce_scatter | solution.py:287
  292.4 3.5 %fusion.18 = bf16[1792,360]{0,1:T(8,128)(2,1)S(1)} fusion(s32[1792]{0:T(1024)S(1)} %min.28, pred[1792]{0:T(1024)(128)(4,1)S(1)} %lt.62, bf16[768,360]{0,1:T(8,128)(2,1)} %reduce-scatter.5.cloned.1.call-done, bf16[768,360]{0,1:T(8,128)(2,1)S(1)} %copy-done.5), kind=kOutput, calls=%fused_computation.24 | convolution fusion | flops 995407872 | bytes 2405120 | tf_op jit(solution)/shard_map/dot_general | solution.py:241
  295.9 1.5 copy.39
  297.4 26.9 %all_to_all.10 = bf16[16,112,360]{2,1,0:T(8,128)(2,1)S(1)} all-to-all(bf16[16,112,360]{2,1,0:T(8,128)(2,1)} %bitcast.70), channel_id=1, replica_groups=mesh['req'=16,'tp'=8] {'req'}, dimensions={0} | all-to-all | bytes 2580480 | tf_op jit(solution)/shard_map/all_to_all | solution.py:295
  324.3 0.6 convolution_convert_fusion.2
  324.9 1.4 copy.41
  (40 shorter events, 0.3 us)
Async XLA Ops:
  6.5 149.5 %copy-start = (bf16[512,2880]{0,1:T(8,128)(2,1)S(1)}, bf16[512,2880]{0,1:T(8,128)(2,1)}, u32[]{:S(2)}) copy-start(bf16[512,2880]{0,1:T(8,128)(2,1)} %param.25) | copy-start | bytes 8847364
  10.2 10.2 %copy-start.9 = (s32[256]{0:T(256)S(1)}, s32[256]{0:T(256)}, u32[]{:S(2)}) copy-start(s32[256]{0:T(256)} %param.18) | copy-start | bytes 3076
  10.2 10.3 %copy-start.6 = (s32[16,16]{1,0:T(8,128)S(1)}, s32[16,16]{1,0:T(8,128)}, u32[]{:S(2)}) copy-start(s32[16,16]{1,0:T(8,128)} %param.17) | copy-start | bytes 3076
  11.6 26.8 %all-to-all-start = ((bf16[16,112,360]{2,1,0:T(8,128)(2,1)}), bf16[16,112,360]{2,1,0:T(8,128)(2,1)}, u32[]{:S(2)}, u32[]{:S(2)}) async-start(bf16[16,112,360]{2,1,0:T(8,128)(2,1)} %copy.37), calls=%async_computation | async-start | bytes 2752512 | tf_op jit(solution)/shard_map/all_to_all | solution.py:254
  19.4 55.2 %all-gather.4.cloned.1.call-start = ((), (), s32[]{:S(2)}) async-start(), calls=%async_computation.4 | async-start | bytes 4976640 | tf_op jit(solution)/shard_map/all_gather | solution.py:256
  38.3 5.5 %copy-start.12 = (s32[64]{0:T(128)S(1)}, s32[64]{0:T(128)}, u32[]{:S(2)}) copy-start(s32[64]{0:T(128)} %param.20) | copy-start | bytes 772
  38.3 7.2 %copy-start.7 = (bf16[2880]{0:T(1024)(128)(2,1)S(1)}, bf16[2880]{0:T(1024)(128)(2,1)}, u32[]{:S(2)}) copy-start(bf16[2880]{0:T(1024)(128)(2,1)} %param.22) | copy-start | bytes 17284
  42.0 79.6 %all-gather.6.cloned.1.call-start = ((), (), s32[]{:S(2)}) async-start(), calls=%async_computation.5 | async-start | bytes 2228224 | tf_op jit(solution)/shard_map/all_gather | solution.py:174
  74.6 126.9 %reduce-scatter.3.cloned.1.call-start = ((), (), s32[]{:S(2)}) async-start(), calls=%async_computation.6 | async-start | bytes 4976640 | tf_op jit(solution)/shard_map/reduce_scatter | solution.py:278
  75.1 3.6 %copy-start.2 = (bf16[768,2880]{0,1:T(8,128)(2,1)S(1)}, bf16[768,2880]{0,1:T(8,128)(2,1)}, u32[]{:S(2)}) copy-start(bf16[768,2880]{0,1:T(8,128)(2,1)} %all-gather.4.cloned.1.call-done) | copy-start | bytes 13271044
  83.6 1.1 copy-start.11
  163.5 38.0 %copy-start.4 = (bf16[768,360]{0,1:T(8,128)(2,1)S(1)}, bf16[768,360]{0,1:T(8,128)(2,1)}, u32[]{:S(2)}) copy-start(bf16[768,360]{0,1:T(8,128)(2,1)} %fusion.37) | copy-start | bytes 1658884
  163.5 40.4 %copy-start.8 = (bf16[2880]{0:T(1024)(128)(2,1)S(1)}, bf16[2880]{0:T(1024)(128)(2,1)}, u32[]{:S(2)}) copy-start(bf16[2880]{0:T(1024)(128)(2,1)} %param.26) | copy-start | bytes 17284
  163.5 72.3 %all-gather.8.cloned.1.call-start = ((), (), s32[]{:S(2)}) async-start(), calls=%async_computation.7 | async-start | bytes 4976640 | tf_op jit(solution)/shard_map/all_gather | solution.py:282
  201.5 37.7 %copy-start.10 = (bf16[2880,360]{0,1:T(8,128)(2,1)S(1)}, bf16[2880,360]{0,1:T(8,128)(2,1)}, u32[]{:S(2)}) copy-start(bf16[2880,360]{0,1:T(8,128)(2,1)} %param.27) | copy-start | bytes 6220804
  203.7 88.7 %reduce-scatter.5.cloned.1.call-start = ((), (), s32[]{:S(2)}) async-start(), calls=%async_computation.8 | async-start | bytes 4976640 | tf_op jit(solution)/shard_map/reduce_scatter | solution.py:287
  235.8 3.6 %copy-start.3 = (bf16[768,2880]{0,1:T(8,128)(2,1)S(1)}, bf16[768,2880]{0,1:T(8,128)(2,1)}, u32[]{:S(2)}) copy-start(bf16[768,2880]{0,1:T(8,128)(2,1)} %all-gather.8.cloned.1.call-done) | copy-start | bytes 13271044
  253.8 38.6 %copy-start.5 = (bf16[768,360]{0,1:T(8,128)(2,1)S(1)}, bf16[768,360]{0,1:T(8,128)(2,1)}, u32[]{:S(2)}) copy-start(bf16[768,360]{0,1:T(8,128)(2,1)} %add_convert_fusion.1) | copy-start | bytes 1658884
  297.4 28.9 %copy-start.1 = (bf16[512,2880]{0,1:T(8,128)(2,1)S(1)}, bf16[512,2880]{0,1:T(8,128)(2,1)}, u32[]{:S(2)}) copy-start(bf16[512,2880]{0,1:T(8,128)(2,1)} %param.25) | copy-start | bytes 8847364
Sparse Core Ops, SparseCore 0:
  42.2 32.3 all-gather.3
  76.7 44.9 all-gather.5
  163.6 37.7 reduce-scatter.2
  203.8 31.9 all-gather.7
  253.9 38.4 reduce-scatter.4

commit v11 on v9

--- a/solution.py
+++ b/solution.py
@@ -161,9 +161,10 @@
     )(sink_logits.astype(jnp.float32), query_slots, paired_slots, tail_rows)
 
 
-def fetch_prefix(attach_slots, prefix_cache, block_of_slot, window):
+def fetch_prefix(attach_slots, early_rows, late_half, half, block_of_slot, window):
     total_blocks = block_of_slot.shape[0]
-    block_len = prefix_cache.shape[1]
+    block_len = early_rows.shape[1]
+    peers = lax.axis_size("req")
     catalog = jnp.arange(total_blocks)
     home_row = jnp.sum(
         jnp.where(block_of_slot[None, :] == catalog[:, None], catalog[None, :], 0), axis=1
@@ -171,9 +172,12 @@
     first_block = jnp.clip((attach_slots - window) // block_len, 0, total_blocks - 1)
     second_block = jnp.clip(first_block + 1, 0, total_blocks - 1)
     offset = attach_slots - window - first_block * block_len
-    shard_rows = lax.all_gather(prefix_cache, "req", axis=0, tiled=True)
+    late_rows = lax.all_gather(late_half, "req", axis=0, tiled=True)
+    shard_rows = jnp.concatenate([early_rows, late_rows], axis=0)
     shard_rows = shard_rows.reshape(total_blocks, block_len, -1)
-    pair = jnp.stack([home_row[first_block], home_row[second_block]], axis=1)
+    stored = jnp.stack([home_row[first_block], home_row[second_block]], axis=1)
+    owner, local_slot = stored // (2 * half), stored % (2 * half)
+    pair = (local_slot // half) * (peers * half) + owner * half + local_slot % half
     both = shard_rows[pair].reshape(attach_slots.shape[0], 2 * block_len, -1)
     picks = (
         jnp.arange(2 * block_len)[None, None, :]
@@ -244,7 +248,6 @@
     def to_packed(values):
         return jnp.dot(pack_pick, values, preferred_element_type=jnp.float32).astype(values.dtype)
 
-    tail_rows = fetch_prefix(arriving_attach, prefix_cache, block_of_slot, WINDOW)
     my_features = lax.dynamic_slice_in_dim(
         suffix_tokens, tensor_index * feature_share, feature_share, 2
     )
@@ -254,8 +257,17 @@
     ).astype(jnp.bfloat16)
     landed = lax.all_to_all(outgoing, "req", split_axis=0, concat_axis=0, tiled=True)
     input_part = to_packed(landed.reshape(peers * slot_length, feature_share))
+    held_here = prefix_cache.shape[0]
+    early_rows = lax.all_gather(prefix_cache[:held_here // 2], "req", axis=0, tiled=True)
+    input_part, early_rows = lax.optimization_barrier((input_part, early_rows))
     input_rows = lax.all_gather(input_part, "tp", axis=1, tiled=True)
     row_total = input_part.shape[0]
+    late_half, input_rows = lax.optimization_barrier(
+        (prefix_cache[held_here // 2:], input_rows)
+    )
+    tail_rows = fetch_prefix(
+        arriving_attach, early_rows, late_half, held_here // 2, block_of_slot, WINDOW
+    )
     normed_in = norm_rows(input_rows, attn_gain)
     queries = jnp.dot(normed_in, w_query, preferred_element_type=jnp.float32).reshape(
         row_total, -1, head_dim

time: 322 us -> 357 us (1.11)
  waiting for transfers between devices: 173 us -> 202 us
    all_gather x1 -> x2, waiting for transfers between devices: 16.4 us -> 45.1 us  [the longest x1 27 us: fetch_prefix(): late_rows = lax.all_gather(late_half, 'req', axis=0, tiled=True)]
  transfers between devices with their start and end apart: 6 -> 7, of which waited for: 6 -> 7; matrix products, arithmetic and copies ran while one was open for 6% -> 9% of each run, Pallas kernels for 0% -> 0%
where the time goes in v11:
time: 357 us; the launch traced here: 356 us
  waiting for transfers between devices  202 us (57%)
  matrix products  44.9 us (13%)
  Pallas kernels  28.5 us (8%)
  blocking collectives  26.9 us (8%)
  local copies, waits for them, and re-layouts  16.5 us (5%)
  other arithmetic  15.5 us (4%)
  between operations  13.7 us (4%)
  starting transfers between devices  8.24 us (2%)
    reduce_scatter x1, waiting for transfers between devices, local(): lax.psum_scatter(jnp.dot(hidden, w_down, preferred_element_type=jnp.float...  38.6 us
    reduce_scatter x1, waiting for transfers between devices, local(): lax.psum_scatter(partial_value.astype(jnp.bfloat16), 'tp', scatter_dimens...  38.1 us
    all_gather x1, waiting for transfers between devices, local(): residual = lax.all_gather(residual_part, 'tp', axis=1, tiled=True)  31.8 us
    all_gather x1, waiting for transfers between devices, local(): input_rows = lax.all_gather(input_part, 'tp', axis=1, tiled=True)  30.2 us
    pallas_call x1, Pallas kernels, attend_pallas(): pl.pallas_call(attend_kernel, grid=(peers // batch,), in_specs=[pl.BlockS...  28.5 us
    all_gather x1, waiting for transfers between devices, fetch_prefix(): late_rows = lax.all_gather(late_half, 'req', axis=0, tiled=True)  27 us
    all_to_all x1, blocking collectives, local(): lax.all_to_all(out_slots, 'req', split_axis=0, concat_axis=0, tiled=True)  26.9 us
    all_gather x1, waiting for transfers between devices, local(): lax.all_gather(prefix_cache[:held_here // 2], 'req', axis=0, tiled=True)  18.1 us
  transfers between devices with their start and end apart: 7, of which 7 were waited for; matrix products, arithmetic and copies ran while one was open for 9% of the time, Pallas kernels for 0%

profile of v11, /device:TPU:7, one launch (start us, length us, event | category | flops | bytes accessed | tf_op | source)
XLA Modules:
  0.0 356.1 jit_solution(50370914937767217)
XLA Ops:
  6.5 1.7 fusion.84
  8.2 0.7 fusion.77
  8.9 0.1 select_reduce_fusion.4
  9.1 2.1 constant_dynamic-slice_fusion
  11.2 0.6 convolution_convert_fusion.3
  11.8 1.4 copy.37
  13.1 7.8 %all-to-all-start = ((bf16[16,112,360]{2,1,0:T(8,128)(2,1)}), bf16[16,112,360]{2,1,0:T(8,128)(2,1)}, u32[]{:S(2)}, u32[]{:S(2)}) async-start(bf16[16,112,360]{2,1,0:T(8,128)(2,1)} %copy.37), calls=%async_computation | async-start | bytes 2752512 | tf_op jit(solution)/shard_map/all_to_all | solution.py:258
  20.9 0.0 all-gather.7.cloned.1.call-start
  21.0 0.7 fusion.95
  21.7 0.1 copy.35
  21.8 0.1 reduce
  21.9 0.1 reshape.675
  22.0 0.1 select_reduce_fusion.3
  22.1 0.1 convert_reduce_fusion
  22.2 0.7 fusion.80
  22.9 0.1 select_reduce_fusion
  23.0 17.9 %all-to-all-done = bf16[16,112,360]{2,1,0:T(8,128)(2,1)} async-done(((bf16[16,112,360]{2,1,0:T(8,128)(2,1)}), bf16[16,112,360]{2,1,0:T(8,128)(2,1)}, u32[]{:S(2)}, u32[]{:S(2)}) %all-to-all-start) | async-done | bytes 1290272 | tf_op jit(solution)/shard_map/all_to_all | solution.py:258
  40.9 3.7 %fusion.37 = bf16[768,360]{0,1:T(8,128)(2,1)} fusion(bf16[1792,360]{1,0:T(8,128)(2,1)} %bitcast.6, s32[768]{0:T(1024)S(1)} %get-tuple-element.24), kind=kOutput, calls=%fused_computation.44 | convolution fusion | flops 992557056 | bytes 1846272 | tf_op jit(solution)/shard_map/dot_general | solution.py:249
  44.6 18.1 %all-gather.5.cloned.1.call-done = bf16[32,128,1,128]{3,1,2,0:T(8,128)(2,1)} async-done(((bf16[2,128,1,128]{3,1,2,0:T(8,128)(2,1)}), bf16[32,128,1,128]{3,1,2,0:T(8,128)(2,1)}) %all-gather.5.cloned.1.call-update) | async-done | bytes 1048592 | tf_op jit(solution)/shard_map/all_gather | solution.py:261
  62.7 0.7 fusion.94
  63.4 0.1 iota_compare_fusion.19
  63.5 0.1 lt.70
  63.6 0.7 bitcast_subtract_fusion.1
  64.3 0.1 add_clamp_fusion
  64.4 0.1 min.28
  64.5 0.1 select_reduce_fusion.2
  64.6 0.7 gather_fusion.1
  65.3 0.7 gather_fusion
  66.0 0.1 copy.38
  66.1 0.1 reshape.702
  66.2 0.1 iota_add_fusion
  66.3 0.4 multiply_cosine_fusion.1
  66.7 30.2 %all-gather.7.cloned.1.call-done = bf16[768,2880]{0,1:T(8,128)(2,1)} async-done(((bf16[768,360]{0,1:T(8,128)(2,1)}), bf16[768,2880]{0,1:T(8,128)(2,1)}) %all-gather.7.cloned.1.call-update) | async-done | bytes 4423696 | tf_op jit(solution)/shard_map/all_gather | solution.py:263
  97.0 3.4 fusion
  100.4 0.2 copy-done.2
  100.6 4.8 %fusion.44 = f32[768,512]{0,1:T(8,128)S(1)} fusion(bf16[2880,512]{1,0:T(8,128)(2,1)} %param.23, bf16[768,2880]{0,1:T(8,128)(2,1)S(1)} %copy-done.2, f32[2880]{0:T(1024)S(1)} %convert_element_type.111, f32[768]{0:T(1024)S(1)} %add_rsqrt_fusion.1), kind=kOutput, calls=%fused_computation.48 | convolution fusion | flops 2273771520 | bytes 8960256 | tf_op jit(solution)/shard_map/dot_general | solution.py:272
  105.4 0.2 subtract_convert_fusion
  105.7 0.1 pad_maximum_fusion
  105.7 0.8 copy-done.11
  106.5 1.6 fusion.46
  108.1 0.4 fusion.69
  108.6 2.6 fusion.29
  111.2 3.3 fusion.15
  114.5 27.0 %all-gather.9.cloned.1.call-done = bf16[32,128,1,128]{3,1,2,0:T(8,128)(2,1)} async-done(((bf16[2,128,1,128]{3,1,2,0:T(8,128)(2,1)}), bf16[32,128,1,128]{3,1,2,0:T(8,128)(2,1)}) %all-gather.9.cloned.1.call-update) | async-done | bytes 1048592 | tf_op jit(solution)/shard_map/all_gather | solution.py:175
  141.4 3.1 maximum_bitcast_fusion
  144.5 3.2 gather_fusion.2
  147.7 2.6 fusion.38.tail_ref
  150.3 28.5 %shard_map.145 = bf16[16,112,512]{2,1,0:T(8,128)(2,1)} custom-call(f32[8]{0:T(128)} %sink_ref.1, bf16[16,112,512]{2,1,0:T(8,128)(2,1)} %bitcast.77, bf16[16,112,128]{2,1,0:T(8,128)(2,1)} %bitcast.79, bf16[16,128,128]{2,1,0:T(8,128)(2,1)} %fusion.38.tail_ref), custom_call_target="tpu_custom_call" | custom-call | flops 880803840 | bytes 4653056 | tf_op jit(solution)/shard_map/pallas_call | solution.py:145
  178.8 7.5 %convolution_convert_fusion = bf16[768,2880]{0,1:T(8,128)(2,1)} fusion(bf16[512,2880]{0,1:T(8,128)(2,1)S(1)} %copy-done, bf16[1792,512]{1,0:T(8,128)(2,1)} %bitcast.78, s32[768]{0:T(1024)S(1)} %get-tuple-element.24), kind=kOutput, calls=%fused_computation.21 | convolution fusion | flops 3678191616 | bytes 9210880 | tf_op jit(solution)/shard_map/dot_general | solution.py:288
  186.3 0.0 all-gather.11.cloned.1.call-start
  186.3 38.1 %reduce-scatter.3.cloned.1.call-done = bf16[768,360]{0,1:T(8,128)(2,1)} async-done(((bf16[768,2880]{0,1:T(8,128)(2,1)}), bf16[768,360]{0,1:T(8,128)(2,1)}) %reduce-scatter.3.cloned.1.call-update) | async-done | bytes 552976 | tf_op jit(solution)/shard_map/reduce_scatter | solution.py:289
  224.4 2.2 add_convert_fusion.1
  226.7 0.3 reduce-scatter.5.cloned.1.call-start
  227.0 31.8 %all-gather.11.cloned.1.call-done = bf16[768,2880]{0,1:T(8,128)(2,1)} async-done(((bf16[768,360]{0,1:T(8,128)(2,1)}), bf16[768,2880]{0,1:T(8,128)(2,1)}) %all-gather.11.cloned.1.call-update) | async-done | bytes 4423696 | tf_op jit(solution)/shard_map/all_gather | solution.py:293
  258.8 3.3 fusion.3
  262.2 0.2 copy-done.3
  262.4 3.1 fusion.40
  265.5 11.3 %convolution_convert_fusion.1 = bf16[768,2880]{0,1:T(8,128)(2,1)} fusion(bf16[360,2880]{1,0:T(8,128)(2,1)} %param.29, bf16[2880,360]{0,1:T(8,128)(2,1)} %param.28, bf16[768,2880]{0,1:T(8,128)(2,1)} %all-gather.11.cloned.1.call-done, f32[2880]{0:T(1024)S(1)} %convert_element_type.125, f32[768]{0:T(1024)S(1)} %add_rsqrt_fusion, f32[768,360]{0,1:T(8,128)} %fusion.40), kind=kOutput, calls=%fused_computation.22 | convolution fusion | flops 3197767680 | bytes 14115072 | tf_op jit(solution)/shard_map/dot_general | solution.py:299
  276.8 38.6 %reduce-scatter.5.cloned.1.call-done = bf16[768,360]{0,1:T(8,128)(2,1)} async-done(((bf16[768,2880]{0,1:T(8,128)(2,1)}), bf16[768,360]{0,1:T(8,128)(2,1)}) %reduce-scatter.5.cloned.1.call-update) | async-done | bytes 552976 | tf_op jit(solution)/shard_map/reduce_scatter | solution.py:298
  315.4 3.5 fusion.18
  318.9 1.5 copy.39
  320.4 26.9 %all_to_all.10 = bf16[16,112,360]{2,1,0:T(8,128)(2,1)S(1)} all-to-all(bf16[16,112,360]{2,1,0:T(8,128)(2,1)} %bitcast.71), channel_id=1, replica_groups=mesh['req'=16,'tp'=8] {'req'}, dimensions={0} | all-to-all | bytes 2580480 | tf_op jit(solution)/shard_map/all_to_all | solution.py:306
  347.3 0.6 convolution_convert_fusion.2
  347.9 1.4 copy.41
  (45 shorter events, 0.4 us)
Async XLA Ops:
  6.5 172.3 %copy-start = (bf16[512,2880]{0,1:T(8,128)(2,1)S(1)}, bf16[512,2880]{0,1:T(8,128)(2,1)}, u32[]{:S(2)}) copy-start(bf16[512,2880]{0,1:T(8,128)(2,1)} %param.25) | copy-start | bytes 8847364
  6.5 56.1 %all-gather.5.cloned.1.call-start = ((), (), s32[]{:S(2)}) async-start(), calls=%async_computation.4 | async-start | bytes 1114112 | tf_op jit(solution)/shard_map/all_gather | solution.py:261
  11.7 10.2 %copy-start.9 = (s32[256]{0:T(256)S(1)}, s32[256]{0:T(256)}, u32[]{:S(2)}) copy-start(s32[256]{0:T(256)} %param.18) | copy-start | bytes 3076
  11.7 10.3 %copy-start.6 = (s32[16,16]{1,0:T(8,128)S(1)}, s32[16,16]{1,0:T(8,128)}, u32[]{:S(2)}) copy-start(s32[16,16]{1,0:T(8,128)} %param.17) | copy-start | bytes 3076
  13.1 27.8 %all-to-all-start = ((bf16[16,112,360]{2,1,0:T(8,128)(2,1)}), bf16[16,112,360]{2,1,0:T(8,128)(2,1)}, u32[]{:S(2)}, u32[]{:S(2)}) async-start(bf16[16,112,360]{2,1,0:T(8,128)(2,1)} %copy.37), calls=%async_computation | async-start | bytes 2752512 | tf_op jit(solution)/shard_map/all_to_all | solution.py:258
  20.9 76.0 %all-gather.7.cloned.1.call-start = ((), (), s32[]{:S(2)}) async-start(), calls=%async_computation.5 | async-start | bytes 4976640 | tf_op jit(solution)/shard_map/all_gather | solution.py:263
  40.9 23.6 %copy-start.12 = (s32[64]{0:T(128)S(1)}, s32[64]{0:T(128)}, u32[]{:S(2)}) copy-start(s32[64]{0:T(128)} %param.20) | copy-start | bytes 772
  40.9 25.3 %copy-start.7 = (bf16[2880]{0:T(1024)(128)(2,1)S(1)}, bf16[2880]{0:T(1024)(128)(2,1)}, u32[]{:S(2)}) copy-start(bf16[2880]{0:T(1024)(128)(2,1)} %param.22) | copy-start | bytes 17284
  62.7 78.7 %all-gather.9.cloned.1.call-start = ((), (), s32[]{:S(2)}) async-start(), calls=%async_computation.6 | async-start | bytes 1114112 | tf_op jit(solution)/shard_map/all_gather | solution.py:175
  97.0 127.5 %reduce-scatter.3.cloned.1.call-start = ((), (), s32[]{:S(2)}) async-start(), calls=%async_computation.7 | async-start | bytes 4976640 | tf_op jit(solution)/shard_map/reduce_scatter | solution.py:289
  97.0 3.6 %copy-start.2 = (bf16[768,2880]{0,1:T(8,128)(2,1)S(1)}, bf16[768,2880]{0,1:T(8,128)(2,1)}, u32[]{:S(2)}) copy-start(bf16[768,2880]{0,1:T(8,128)(2,1)} %all-gather.7.cloned.1.call-done) | copy-start | bytes 13271044
  105.4 1.1 copy-start.11
  186.3 38.2 %copy-start.4 = (bf16[768,360]{0,1:T(8,128)(2,1)S(1)}, bf16[768,360]{0,1:T(8,128)(2,1)}, u32[]{:S(2)}) copy-start(bf16[768,360]{0,1:T(8,128)(2,1)} %fusion.37) | copy-start | bytes 1658884
  186.3 40.6 %copy-start.8 = (bf16[2880]{0:T(1024)(128)(2,1)S(1)}, bf16[2880]{0:T(1024)(128)(2,1)}, u32[]{:S(2)}) copy-start(bf16[2880]{0:T(1024)(128)(2,1)} %param.26) | copy-start | bytes 17284
  186.3 72.5 %all-gather.11.cloned.1.call-start = ((), (), s32[]{:S(2)}) async-start(), calls=%async_computation.8 | async-start | bytes 4976640 | tf_op jit(solution)/shard_map/all_gather | solution.py:293
  224.4 37.7 %copy-start.10 = (bf16[2880,360]{0,1:T(8,128)(2,1)S(1)}, bf16[2880,360]{0,1:T(8,128)(2,1)}, u32[]{:S(2)}) copy-start(bf16[2880,360]{0,1:T(8,128)(2,1)} %param.27) | copy-start | bytes 6220804
  226.7 88.7 %reduce-scatter.5.cloned.1.call-start = ((), (), s32[]{:S(2)}) async-start(), calls=%async_computation.9 | async-start | bytes 4976640 | tf_op jit(solution)/shard_map/reduce_scatter | solution.py:298
  258.8 3.6 %copy-start.3 = (bf16[768,2880]{0,1:T(8,128)(2,1)S(1)}, bf16[768,2880]{0,1:T(8,128)(2,1)}, u32[]{:S(2)}) copy-start(bf16[768,2880]{0,1:T(8,128)(2,1)} %all-gather.11.cloned.1.call-done) | copy-start | bytes 13271044
  276.8 38.6 %copy-start.5 = (bf16[768,360]{0,1:T(8,128)(2,1)S(1)}, bf16[768,360]{0,1:T(8,128)(2,1)}, u32[]{:S(2)}) copy-start(bf16[768,360]{0,1:T(8,128)(2,1)} %add_convert_fusion.1) | copy-start | bytes 1658884
  320.4 28.8 %copy-start.1 = (bf16[512,2880]{0,1:T(8,128)(2,1)S(1)}, bf16[512,2880]{0,1:T(8,128)(2,1)}, u32[]{:S(2)}) copy-start(bf16[512,2880]{0,1:T(8,128)(2,1)} %param.25) | copy-start | bytes 8847364
Sparse Core Ops, SparseCore 0:
  9.5 53.1 all-gather.4
  64.4 32.5 all-gather.6
  99.1 42.2 all-gather.8
  186.4 37.9 reduce-scatter.2
  226.8 31.9 all-gather.10
  276.9 38.4 reduce-scatter.4

commit v12 on v9

--- a/solution.py
+++ b/solution.py
@@ -161,9 +161,9 @@
     )(sink_logits.astype(jnp.float32), query_slots, paired_slots, tail_rows)
 
 
-def fetch_prefix(attach_slots, prefix_cache, block_of_slot, window):
+def fetch_prefix(attach_slots, shard_rows, block_of_slot, window):
     total_blocks = block_of_slot.shape[0]
-    block_len = prefix_cache.shape[1]
+    block_len = shard_rows.shape[1]
     catalog = jnp.arange(total_blocks)
     home_row = jnp.sum(
         jnp.where(block_of_slot[None, :] == catalog[:, None], catalog[None, :], 0), axis=1
@@ -171,8 +171,6 @@
     first_block = jnp.clip((attach_slots - window) // block_len, 0, total_blocks - 1)
     second_block = jnp.clip(first_block + 1, 0, total_blocks - 1)
     offset = attach_slots - window - first_block * block_len
-    shard_rows = lax.all_gather(prefix_cache, "req", axis=0, tiled=True)
-    shard_rows = shard_rows.reshape(total_blocks, block_len, -1)
     pair = jnp.stack([home_row[first_block], home_row[second_block]], axis=1)
     both = shard_rows[pair].reshape(attach_slots.shape[0], 2 * block_len, -1)
     picks = (
@@ -244,7 +242,6 @@
     def to_packed(values):
         return jnp.dot(pack_pick, values, preferred_element_type=jnp.float32).astype(values.dtype)
 
-    tail_rows = fetch_prefix(arriving_attach, prefix_cache, block_of_slot, WINDOW)
     my_features = lax.dynamic_slice_in_dim(
         suffix_tokens, tensor_index * feature_share, feature_share, 2
     )
@@ -254,6 +251,19 @@
     ).astype(jnp.bfloat16)
     landed = lax.all_to_all(outgoing, "req", split_axis=0, concat_axis=0, tiled=True)
     input_part = to_packed(landed.reshape(peers * slot_length, feature_share))
+    held_here, block_len = prefix_cache.shape[0], prefix_cache.shape[1]
+    spread = jnp.broadcast_to(
+        prefix_cache.reshape((1, held_here, block_len, -1)),
+        (peers, held_here, block_len, prefix_cache.shape[2] * prefix_cache.shape[3]),
+    )
+    spread, input_part = lax.optimization_barrier((spread, input_part))
+    prefix_rows = lax.all_to_all(spread, "req", split_axis=0, concat_axis=0, tiled=True)
+    tail_rows = fetch_prefix(
+        arriving_attach,
+        prefix_rows.reshape((peers * held_here, block_len, -1)),
+        block_of_slot,
+        WINDOW,
+    )
     input_rows = lax.all_gather(input_part, "tp", axis=1, tiled=True)
     row_total = input_part.shape[0]
     normed_in = norm_rows(input_rows, attn_gain)

time: 322 us -> 306 us (0.950)
  waiting for transfers between devices: 173 us -> 150 us
  starting transfers between devices: 8.2 us -> 13 us
    all_gather x1, waiting for transfers between devices: 28.2 us -> 0.01 us  [local(): input_rows = lax.all_gather(input_part, 'tp', axis=1, tiled=True)]
    all_to_all x0 -> x1, waiting for transfers between devices: none -> 22.1 us  [local(): lax.all_to_all(spread, 'req', split_axis=0, concat_axis=0, tiled=True)]
    all_gather x1 -> x0, waiting for transfers between devices: 16.4 us -> none  [fetch_prefix(): shard_rows = lax.all_gather(prefix_cache, 'req', axis=0, tiled=True)]
    all_to_all x0 -> x1, starting transfers between devices: none -> 4.84 us  [local(): lax.all_to_all(spread, 'req', split_axis=0, concat_axis=0, tiled=True)]
  transfers between devices with their start and end apart: 6 -> 6, of which waited for: 6 -> 5; matrix products, arithmetic and copies ran while one was open for 6% -> 4% of each run, Pallas kernels for 0% -> 0%
where the time goes in v12:
time: 306 us; the launch traced here: 305 us
  waiting for transfers between devices  150 us (49%)
  matrix products  44.6 us (15%)
  Pallas kernels  28.6 us (9%)
  blocking collectives  26.9 us (9%)
  local copies, waits for them, and re-layouts  16 us (5%)
  between operations  13.4 us (4%)
  starting transfers between devices  13 us (4%)
  other arithmetic  12.4 us (4%)
    reduce_scatter x1, waiting for transfers between devices, local(): lax.psum_scatter(partial_value.astype(jnp.bfloat16), 'tp', scatter_dimens...  40.6 us
    reduce_scatter x1, waiting for transfers between devices, local(): lax.psum_scatter(jnp.dot(hidden, w_down, preferred_element_type=jnp.float...  38.6 us
    all_gather x1, waiting for transfers between devices, local(): residual = lax.all_gather(residual_part, 'tp', axis=1, tiled=True)  31.8 us
    pallas_call x1, Pallas kernels, attend_pallas(): pl.pallas_call(attend_kernel, grid=(peers // batch,), in_specs=[pl.BlockS...  28.6 us
    all_to_all x1, blocking collectives, local(): lax.all_to_all(out_slots, 'req', split_axis=0, concat_axis=0, tiled=True)  26.9 us
    all_to_all x1, waiting for transfers between devices, local(): lax.all_to_all(spread, 'req', split_axis=0, concat_axis=0, tiled=True)  22.1 us
    all_to_all x1, waiting for transfers between devices, local(): lax.all_to_all(outgoing, 'req', split_axis=0, concat_axis=0, tiled=True)  16.9 us
    dot_general x1, matrix products, local(): jnp.dot(hidden, w_down, preferred_element_type=jnp.float32)  11.3 us
  transfers between devices with their start and end apart: 6, of which 5 were waited for; matrix products, arithmetic and copies ran while one was open for 4% of the time, Pallas kernels for 0%

profile of v12, /device:TPU:7, one launch (start us, length us, event | category | flops | bytes accessed | tf_op | source)
XLA Modules:
  0.0 304.9 jit_solution(7619590093601248153)
XLA Ops:
  6.5 0.8 fusion.76
  7.4 0.1 select_reduce_fusion.4
  7.5 2.1 constant_dynamic-slice_fusion
  9.6 0.6 convolution_convert_fusion.3
  10.2 1.4 copy.37
  11.6 7.8 %all-to-all-start = ((bf16[16,112,360]{2,1,0:T(8,128)(2,1)}), bf16[16,112,360]{2,1,0:T(8,128)(2,1)}, u32[]{:S(2)}, u32[]{:S(2)}) async-start(bf16[16,112,360]{2,1,0:T(8,128)(2,1)} %copy.37), calls=%async_computation | async-start | bytes 2752512 | tf_op jit(solution)/shard_map/all_to_all | solution.py:252
  19.4 0.0 all-gather.3.cloned.1.call-start
  19.4 0.7 fusion.93
  20.1 0.1 copy.35
  20.2 0.1 reduce
  20.4 0.1 reshape.489
  20.5 0.1 select_reduce_fusion.3
  20.6 0.1 convert_reduce_fusion
  20.7 0.7 fusion.79
  21.4 0.1 select_reduce_fusion
  21.5 16.9 %all-to-all-done = bf16[16,112,360]{2,1,0:T(8,128)(2,1)} async-done(((bf16[16,112,360]{2,1,0:T(8,128)(2,1)}), bf16[16,112,360]{2,1,0:T(8,128)(2,1)}, u32[]{:S(2)}, u32[]{:S(2)}) %all-to-all-start) | async-done | bytes 1290272 | tf_op jit(solution)/shard_map/all_to_all | solution.py:252
  38.3 3.7 %fusion.37 = bf16[768,360]{0,1:T(8,128)(2,1)} fusion(bf16[1792,360]{1,0:T(8,128)(2,1)} %bitcast.7, s32[768]{0:T(1024)S(1)} %get-tuple-element.18), kind=kOutput, calls=%fused_computation.43 | convolution fusion | flops 992557056 | bytes 1846272 | tf_op jit(solution)/shard_map/dot_general | solution.py:243
  42.1 1.9 broadcast_in_dim.23
  43.9 0.0 all-gather.3.cloned.1.call-update
  43.9 0.7 fusion.92
  44.6 4.8 %all-to-all-start.1 = ((bf16[16,4,128,128]{3,2,1,0:T(8,128)(2,1)}), bf16[16,4,128,128]{3,2,1,0:T(8,128)(2,1)}, u32[]{:S(2)}, u32[]{:S(2)}) async-start(bf16[16,4,128,128]{3,2,1,0:T(8,128)(2,1)} %broadcast_in_dim.23), calls=%async_computation.1 | async-start | bytes 4194304 | tf_op jit(solution)/shard_map/all_to_all | solution.py:260
  49.5 0.0 reduce-scatter.3.cloned.1.call-start
  49.5 0.1 iota_compare_fusion.19
  49.6 0.1 lt.62
  49.7 0.7 bitcast_subtract_fusion.1
  50.4 0.1 add_clamp_fusion
  50.5 0.1 min.28
  50.6 0.1 select_reduce_fusion.2
  50.7 0.7 gather_fusion.1
  51.4 0.7 gather_fusion
  52.1 0.1 copy.38
  52.1 0.1 reshape.516
  52.3 0.1 iota_add_fusion
  52.4 0.4 multiply_cosine_fusion.1
  52.8 22.1 %all-to-all-done.1 = bf16[16,4,128,128]{3,2,1,0:T(8,128)(2,1)} async-done(((bf16[16,4,128,128]{3,2,1,0:T(8,128)(2,1)}), bf16[16,4,128,128]{3,2,1,0:T(8,128)(2,1)}, u32[]{:S(2)}, u32[]{:S(2)}) %all-to-all-start.1) | async-done | bytes 2097184 | tf_op jit(solution)/shard_map/all_to_all | solution.py:260
  74.9 3.2 %gather_fusion.2 = bf16[32,128,128]{2,1,0:T(8,128)(2,1)} fusion(bf16[64,128,128]{2,1,0:T(8,128)(2,1)} %bitcast.17, s32[1024]{0:T(1024)S(1)} %pad_clamp_fusion), kind=kCustom, calls=%fused_computation.2 | custom fusion | bytes 2097280 | tf_op jit(solution)/shard_map/gather | solution.py:175
  78.1 2.6 fusion.38.tail_ref
  80.7 3.3 %fusion = f32[768]{0:T(1024)S(1)} fusion(bf16[768,2880]{0,1:T(8,128)(2,1)} %all-gather.3.cloned.1.call-done), kind=kLoop, calls=%fused_computation.7 | loop fusion | flops 6634752 | bytes 4426752 | tf_op jit(solution)/shard_map/reduce_sum | solution.py:18
  84.1 0.2 copy-done.2
  84.3 2.8 fusion.46
  87.1 0.4 fusion.69
  87.6 3.1 %fusion.44 = f32[768,512]{0,1:T(8,128)S(1)} fusion(bf16[2880,512]{1,0:T(8,128)(2,1)S(1)} %copy-done.11, bf16[768,2880]{0,1:T(8,128)(2,1)S(1)} %copy-done.2, f32[2880]{0:T(1024)S(1)} %convert_element_type.111, f32[768]{0:T(1024)S(1)} %add_rsqrt_fusion.1), kind=kOutput, calls=%fused_computation.47 | convolution fusion | flops 2273771520 | bytes 8960256 | tf_op jit(solution)/shard_map/dot_general | solution.py:270
  90.7 0.2 subtract_convert_fusion
  90.9 0.1 pad_maximum_fusion
  91.0 3.5 %fusion.15 = bf16[1792,512]{1,0:T(8,128)(2,1)} fusion(bf16[768,512]{0,1:T(8,128)(2,1)S(1)} %bitcast.74, s32[1792]{0:T(1024)S(1)} %min.28, pred[1792]{0:T(1024)(128)(4,1)S(1)} %lt.62), kind=kOutput, calls=%fused_computation.23 | convolution fusion | flops 1412956160 | bytes 2630400 | tf_op jit(solution)/shard_map/dot_general | solution.py:239
  94.5 2.4 fusion.29
  96.9 28.6 %shard_map.145 = bf16[16,112,512]{2,1,0:T(8,128)(2,1)} custom-call(f32[8]{0:T(128)} %sink_ref.1, bf16[16,112,512]{2,1,0:T(8,128)(2,1)} %bitcast.78, bf16[16,112,128]{2,1,0:T(8,128)(2,1)} %bitcast.80, bf16[16,128,128]{2,1,0:T(8,128)(2,1)} %fusion.38.tail_ref), custom_call_target="tpu_custom_call" | custom-call | flops 880803840 | bytes 4653056 | tf_op jit(solution)/shard_map/pallas_call | solution.py:145
  125.5 7.5 %convolution_convert_fusion = bf16[768,2880]{0,1:T(8,128)(2,1)} fusion(bf16[512,2880]{0,1:T(8,128)(2,1)S(1)} %copy-done, bf16[1792,512]{1,0:T(8,128)(2,1)} %bitcast.79, s32[768]{0:T(1024)S(1)} %get-tuple-element.18), kind=kOutput, calls=%fused_computation.21 | convolution fusion | flops 3678191616 | bytes 9210880 | tf_op jit(solution)/shard_map/dot_general | solution.py:286
  132.9 0.0 reduce-scatter.3.cloned.1.call-update
  133.0 0.0 all-gather.5.cloned.1.call-start
  133.0 40.6 %reduce-scatter.3.cloned.1.call-done = bf16[768,360]{0,1:T(8,128)(2,1)} async-done(((bf16[768,2880]{0,1:T(8,128)(2,1)}), bf16[768,360]{0,1:T(8,128)(2,1)}) %reduce-scatter.3.cloned.1.call-update) | async-done | bytes 552976 | tf_op jit(solution)/shard_map/reduce_scatter | solution.py:287
  173.6 2.2 add_convert_fusion.1
  175.8 0.3 reduce-scatter.5.cloned.1.call-start
  176.1 31.8 %all-gather.5.cloned.1.call-done = bf16[768,2880]{0,1:T(8,128)(2,1)} async-done(((bf16[768,360]{0,1:T(8,128)(2,1)}), bf16[768,2880]{0,1:T(8,128)(2,1)}) %all-gather.5.cloned.1.call-update) | async-done | bytes 4423696 | tf_op jit(solution)/shard_map/all_gather | solution.py:291
  207.9 3.3 %fusion.3 = f32[768]{0:T(1024)S(1)} fusion(bf16[768,2880]{0,1:T(8,128)(2,1)} %all-gather.5.cloned.1.call-done), kind=kLoop, calls=%fused_computation.10 | loop fusion | flops 6634752 | bytes 4426752 | tf_op jit(solution)/shard_map/reduce_sum | solution.py:18
  211.3 0.2 copy-done.3
  211.5 3.1 %fusion.40 = f32[768,360]{0,1:T(8,128)} fusion(bf16[2880,360]{0,1:T(8,128)(2,1)S(1)} %copy-done.12, bf16[768,2880]{0,1:T(8,128)(2,1)S(1)} %copy-done.3, f32[2880]{0:T(1024)S(1)} %convert_element_type.125, f32[768]{0:T(1024)S(1)} %add_rsqrt_fusion), kind=kOutput, calls=%fused_computation.45 | convolution fusion | flops 1601372160 | bytes 7617792 | tf_op jit(solution)/shard_map/dot_general | solution.py:293
  214.6 11.3 %convolution_convert_fusion.1 = bf16[768,2880]{0,1:T(8,128)(2,1)} fusion(bf16[360,2880]{1,0:T(8,128)(2,1)} %param.29, bf16[2880,360]{0,1:T(8,128)(2,1)} %param.28, bf16[768,2880]{0,1:T(8,128)(2,1)} %all-gather.5.cloned.1.call-done, f32[2880]{0:T(1024)S(1)} %convert_element_type.125, f32[768]{0:T(1024)S(1)} %add_rsqrt_fusion, f32[768,360]{0,1:T(8,128)} %fusion.40), kind=kOutput, calls=%fused_computation.22 | convolution fusion | flops 3197767680 | bytes 14115072 | tf_op jit(solution)/shard_map/dot_general | solution.py:297
  225.9 38.6 %reduce-scatter.5.cloned.1.call-done = bf16[768,360]{0,1:T(8,128)(2,1)} async-done(((bf16[768,2880]{0,1:T(8,128)(2,1)}), bf16[768,360]{0,1:T(8,128)(2,1)}) %reduce-scatter.5.cloned.1.call-update) | async-done | bytes 552976 | tf_op jit(solution)/shard_map/reduce_scatter | solution.py:296
  264.5 3.5 %fusion.18 = bf16[1792,360]{0,1:T(8,128)(2,1)S(1)} fusion(s32[1792]{0:T(1024)S(1)} %min.28, pred[1792]{0:T(1024)(128)(4,1)S(1)} %lt.62, bf16[768,360]{0,1:T(8,128)(2,1)} %reduce-scatter.5.cloned.1.call-done, bf16[768,360]{0,1:T(8,128)(2,1)S(1)} %copy-done.5), kind=kOutput, calls=%fused_computation.24 | convolution fusion | flops 995407872 | bytes 2405120 | tf_op jit(solution)/shard_map/dot_general | solution.py:239
  268.0 1.5 copy.39
  269.5 26.9 %all_to_all.15 = bf16[16,112,360]{2,1,0:T(8,128)(2,1)S(1)} all-to-all(bf16[16,112,360]{2,1,0:T(8,128)(2,1)} %bitcast.71), channel_id=1, replica_groups=mesh['req'=16,'tp'=8] {'req'}, dimensions={0} | all-to-all | bytes 2580480 | tf_op jit(solution)/shard_map/all_to_all | solution.py:304
  296.4 0.6 convolution_convert_fusion.2
  297.0 1.4 copy.41
  (42 shorter events, 0.2 us)
Async XLA Ops:
  6.5 118.9 %copy-start = (bf16[512,2880]{0,1:T(8,128)(2,1)S(1)}, bf16[512,2880]{0,1:T(8,128)(2,1)}, u32[]{:S(2)}) copy-start(bf16[512,2880]{0,1:T(8,128)(2,1)} %param.25) | copy-start | bytes 8847364
  10.2 10.2 %copy-start.10 = (s32[256]{0:T(256)S(1)}, s32[256]{0:T(256)}, u32[]{:S(2)}) copy-start(s32[256]{0:T(256)} %param.18) | copy-start | bytes 3076
  10.2 10.3 %copy-start.7 = (s32[16,16]{1,0:T(8,128)S(1)}, s32[16,16]{1,0:T(8,128)}, u32[]{:S(2)}) copy-start(s32[16,16]{1,0:T(8,128)} %param.17) | copy-start | bytes 3076
  11.6 26.8 %all-to-all-start = ((bf16[16,112,360]{2,1,0:T(8,128)(2,1)}), bf16[16,112,360]{2,1,0:T(8,128)(2,1)}, u32[]{:S(2)}, u32[]{:S(2)}) async-start(bf16[16,112,360]{2,1,0:T(8,128)(2,1)} %copy.37), calls=%async_computation | async-start | bytes 2752512 | tf_op jit(solution)/shard_map/all_to_all | solution.py:252
  19.4 61.3 %all-gather.3.cloned.1.call-start = ((), (), s32[]{:S(2)}) async-start(), calls=%async_computation.5 | async-start | bytes 4976640 | tf_op jit(solution)/shard_map/all_gather | solution.py:267
  38.3 3.7 %copy-start.6 = (bf16[4,128,1,128]{3,1,2,0:T(8,128)(2,1)S(1)}, bf16[4,128,1,128]{3,1,2,0:T(8,128)(2,1)}, u32[]{:S(2)}) copy-start(bf16[4,128,1,128]{3,1,2,0:T(8,128)(2,1)} %param.19) | copy-start | bytes 393220
  44.6 6.0 %copy-start.13 = (s32[64]{0:T(128)S(1)}, s32[64]{0:T(128)}, u32[]{:S(2)}) copy-start(s32[64]{0:T(128)} %param.20) | copy-start | bytes 772
  44.6 7.6 %copy-start.8 = (bf16[2880]{0:T(1024)(128)(2,1)S(1)}, bf16[2880]{0:T(1024)(128)(2,1)}, u32[]{:S(2)}) copy-start(bf16[2880]{0:T(1024)(128)(2,1)} %param.22) | copy-start | bytes 17284
  44.6 30.2 %all-to-all-start.1 = ((bf16[16,4,128,128]{3,2,1,0:T(8,128)(2,1)}), bf16[16,4,128,128]{3,2,1,0:T(8,128)(2,1)}, u32[]{:S(2)}, u32[]{:S(2)}) async-start(bf16[16,4,128,128]{3,2,1,0:T(8,128)(2,1)} %broadcast_in_dim.23), calls=%async_computation.1 | async-start | bytes 4194304 | tf_op jit(solution)/shard_map/all_to_all | solution.py:260
  49.5 124.1 %reduce-scatter.3.cloned.1.call-start = ((), (), s32[]{:S(2)}) async-start(), calls=%async_computation.6 | async-start | bytes 4976640 | tf_op jit(solution)/shard_map/reduce_scatter | solution.py:287
  80.7 3.6 %copy-start.2 = (bf16[768,2880]{0,1:T(8,128)(2,1)S(1)}, bf16[768,2880]{0,1:T(8,128)(2,1)}, u32[]{:S(2)}) copy-start(bf16[768,2880]{0,1:T(8,128)(2,1)} %all-gather.3.cloned.1.call-done) | copy-start | bytes 13271044
  84.3 3.3 %copy-start.11 = (bf16[2880,512]{1,0:T(8,128)(2,1)S(1)}, bf16[2880,512]{1,0:T(8,128)(2,1)}, u32[]{:S(2)}) copy-start(bf16[2880,512]{1,0:T(8,128)(2,1)} %param.23) | copy-start | bytes 8847364
  132.9 40.6 %copy-start.4 = (bf16[768,360]{0,1:T(8,128)(2,1)S(1)}, bf16[768,360]{0,1:T(8,128)(2,1)}, u32[]{:S(2)}) copy-start(bf16[768,360]{0,1:T(8,128)(2,1)} %fusion.37) | copy-start | bytes 1658884
  133.0 43.1 %copy-start.9 = (bf16[2880]{0:T(1024)(128)(2,1)S(1)}, bf16[2880]{0:T(1024)(128)(2,1)}, u32[]{:S(2)}) copy-start(bf16[2880]{0:T(1024)(128)(2,1)} %param.26) | copy-start | bytes 17284
  133.0 75.0 %all-gather.5.cloned.1.call-start = ((), (), s32[]{:S(2)}) async-start(), calls=%async_computation.7 | async-start | bytes 4976640 | tf_op jit(solution)/shard_map/all_gather | solution.py:291
  173.6 37.7 %copy-start.12 = (bf16[2880,360]{0,1:T(8,128)(2,1)S(1)}, bf16[2880,360]{0,1:T(8,128)(2,1)}, u32[]{:S(2)}) copy-start(bf16[2880,360]{0,1:T(8,128)(2,1)} %param.27) | copy-start | bytes 6220804
  175.8 88.7 %reduce-scatter.5.cloned.1.call-start = ((), (), s32[]{:S(2)}) async-start(), calls=%async_computation.8 | async-start | bytes 4976640 | tf_op jit(solution)/shard_map/reduce_scatter | solution.py:296
  207.9 3.6 %copy-start.3 = (bf16[768,2880]{0,1:T(8,128)(2,1)S(1)}, bf16[768,2880]{0,1:T(8,128)(2,1)}, u32[]{:S(2)}) copy-start(bf16[768,2880]{0,1:T(8,128)(2,1)} %all-gather.5.cloned.1.call-done) | copy-start | bytes 13271044
  225.9 38.6 %copy-start.5 = (bf16[768,360]{0,1:T(8,128)(2,1)S(1)}, bf16[768,360]{0,1:T(8,128)(2,1)}, u32[]{:S(2)}) copy-start(bf16[768,360]{0,1:T(8,128)(2,1)} %add_convert_fusion.1) | copy-start | bytes 1658884
  269.5 28.9 %copy-start.1 = (bf16[512,2880]{0,1:T(8,128)(2,1)S(1)}, bf16[512,2880]{0,1:T(8,128)(2,1)}, u32[]{:S(2)}) copy-start(bf16[512,2880]{0,1:T(8,128)(2,1)} %param.25) | copy-start | bytes 8847364
Sparse Core Ops, SparseCore 0:
  44.1 32.3 all-gather.2
  133.1 40.4 reduce-scatter.2
  175.9 31.9 all-gather.4
  226.0 38.4 reduce-scatter.4

commit v13 on v12

--- a/solution.py
+++ b/solution.py
@@ -134,21 +134,21 @@
             ]
 
 
-def attend_pallas(query_slots, paired_slots, tail_rows, sink_logits, batch=2):
-    peers, slot_length, width = query_slots.shape
+def attend_pallas(joined_slots, width, tail_rows, sink_logits, batch=2):
+    peers, slot_length, joined = joined_slots.shape
     window = tail_rows.shape[1]
-    pair_width = paired_slots.shape[2]
+    pair_width = joined - width
     head_dim = pair_width // 2
     heads = width // head_dim
     flops = peers * heads * 4 * slot_length * (window + slot_length) * head_dim
-    moved = 2 * (2 * query_slots.size + paired_slots.size + tail_rows.size)
+    moved = 2 * (joined_slots.size + peers * slot_length * width + tail_rows.size)
     return pl.pallas_call(
         attend_kernel,
         grid=(peers // batch,),
         in_specs=[
             pl.BlockSpec(memory_space=pltpu.SMEM),
             pl.BlockSpec((batch, slot_length, width), lambda n: (n, 0, 0)),
-            pl.BlockSpec((batch, slot_length, pair_width), lambda n: (n, 0, 0)),
+            pl.BlockSpec((batch, slot_length, pair_width), lambda n: (n, 0, width // pair_width)),
             pl.BlockSpec((batch, window, pair_width), lambda n: (n, 0, 0)),
         ],
         out_specs=pl.BlockSpec((batch, slot_length, width), lambda n: (n, 0, 0)),
@@ -158,7 +158,7 @@
             transcendentals=peers * heads * slot_length * (window + slot_length),
             bytes_accessed=moved,
         ),
-    )(sink_logits.astype(jnp.float32), query_slots, paired_slots, tail_rows)
+    )(sink_logits.astype(jnp.float32), joined_slots, joined_slots, tail_rows)
 
 
 def fetch_prefix(attach_slots, shard_rows, block_of_slot, window):
@@ -277,8 +277,12 @@
     rotated = rotate(paired[..., :head_dim], positions)
     paired = jnp.concatenate([rotated, paired[..., head_dim:]], axis=-1).astype(jnp.bfloat16)
     attended = attend_pallas(
-        to_slots(queries.reshape(row_total, -1)),
-        to_slots(paired.reshape(row_total, -1)),
+        to_slots(
+            jnp.concatenate(
+                [queries.reshape(row_total, -1), paired.reshape(row_total, -1)], axis=1
+            )
+        ),
+        queries.shape[1] * queries.shape[2],
         tail_rows,
         sink_logits,
     ).reshape(peers * slot_length, -1)

time: 306 us -> 304 us (level)
    dot_general x3 -> x2, matrix products: 9.4 us -> 7.64 us  [to_slots(): moved = jnp.dot(slot_pick, values, preferred_element_type=jnp.float32)]
where the time goes in v13:
time: 304 us; the launch traced here: 303 us
  waiting for transfers between devices  150 us (49%)
  matrix products  42.9 us (14%)
  Pallas kernels  28.6 us (9%)
  blocking collectives  26.9 us (9%)
  local copies, waits for them, and re-layouts  16 us (5%)
  between operations  13.4 us (4%)
  starting transfers between devices  13.3 us (4%)
  other arithmetic  12.4 us (4%)
    reduce_scatter x1, waiting for transfers between devices, local(): lax.psum_scatter(partial_value.astype(jnp.bfloat16), 'tp', scatter_dimens...  40.6 us
    reduce_scatter x1, waiting for transfers between devices, local(): lax.psum_scatter(jnp.dot(hidden, w_down, preferred_element_type=jnp.float...  38.6 us
    all_gather x1, waiting for transfers between devices, local(): residual = lax.all_gather(residual_part, 'tp', axis=1, tiled=True)  31.8 us
    pallas_call x1, Pallas kernels, attend_pallas(): pl.pallas_call(attend_kernel, grid=(peers // batch,), in_specs=[pl.BlockS...  28.6 us
    all_to_all x1, blocking collectives, local(): lax.all_to_all(out_slots, 'req', split_axis=0, concat_axis=0, tiled=True)  26.9 us
    all_to_all x1, waiting for transfers between devices, local(): lax.all_to_all(spread, 'req', split_axis=0, concat_axis=0, tiled=True)  21.9 us
    all_to_all x1, waiting for transfers between devices, local(): lax.all_to_all(outgoing, 'req', split_axis=0, concat_axis=0, tiled=True)  16.9 us
    dot_general x1, matrix products, local(): jnp.dot(hidden, w_down, preferred_element_type=jnp.float32)  11.3 us
  transfers between devices with their start and end apart: 6, of which 5 were waited for; matrix products, arithmetic and copies ran while one was open for 4% of the time, Pallas kernels for 0%

profile of v13, /device:TPU:7, one launch (start us, length us, event | category | flops | bytes accessed | tf_op | source)
XLA Modules:
  0.0 303.2 jit_solution(10812304043751064328)
XLA Ops:
  6.5 0.8 fusion.71
  7.4 0.1 select_reduce_fusion.4
  7.5 2.1 constant_dynamic-slice_fusion
  9.6 0.6 convolution_convert_fusion.3
  10.2 1.4 copy.37
  11.6 7.8 %all-to-all-start = ((bf16[16,112,360]{2,1,0:T(8,128)(2,1)}), bf16[16,112,360]{2,1,0:T(8,128)(2,1)}, u32[]{:S(2)}, u32[]{:S(2)}) async-start(bf16[16,112,360]{2,1,0:T(8,128)(2,1)} %copy.37), calls=%async_computation | async-start | bytes 2752512 | tf_op jit(solution)/shard_map/all_to_all | solution.py:252
  19.4 0.0 all-gather.3.cloned.1.call-start
  19.4 0.7 fusion.87
  20.1 0.1 copy.35
  20.2 0.1 reduce
  20.4 0.1 reshape.486
  20.5 0.1 select_reduce_fusion.3
  20.6 0.1 convert_reduce_fusion
  20.7 0.7 fusion.74
  21.4 0.1 select_reduce_fusion
  21.5 16.9 %all-to-all-done = bf16[16,112,360]{2,1,0:T(8,128)(2,1)} async-done(((bf16[16,112,360]{2,1,0:T(8,128)(2,1)}), bf16[16,112,360]{2,1,0:T(8,128)(2,1)}, u32[]{:S(2)}, u32[]{:S(2)}) %all-to-all-start) | async-done | bytes 1290272 | tf_op jit(solution)/shard_map/all_to_all | solution.py:252
  38.3 3.7 %fusion.30 = bf16[768,360]{0,1:T(8,128)(2,1)} fusion(bf16[1792,360]{1,0:T(8,128)(2,1)} %bitcast.7, s32[768]{0:T(1024)S(1)} %get-tuple-element.18), kind=kOutput, calls=%fused_computation.39 | convolution fusion | flops 992557056 | bytes 1846272 | tf_op jit(solution)/shard_map/dot_general | solution.py:243
  42.1 1.9 broadcast_in_dim.23
  43.9 0.0 all-gather.3.cloned.1.call-update
  43.9 0.7 fusion.86
  44.6 4.8 %all-to-all-start.1 = ((bf16[16,4,128,128]{3,2,1,0:T(8,128)(2,1)}), bf16[16,4,128,128]{3,2,1,0:T(8,128)(2,1)}, u32[]{:S(2)}, u32[]{:S(2)}) async-start(bf16[16,4,128,128]{3,2,1,0:T(8,128)(2,1)} %broadcast_in_dim.23), calls=%async_computation.1 | async-start | bytes 4194304 | tf_op jit(solution)/shard_map/all_to_all | solution.py:260
  49.5 0.2 reduce-scatter.3.cloned.1.call-start
  49.7 0.1 iota_compare_fusion.19
  49.8 0.1 lt.62
  49.9 0.7 bitcast_subtract_fusion.1
  50.6 0.1 add_clamp_fusion
  50.7 0.1 min.28
  50.8 0.1 select_reduce_fusion.2
  50.9 0.7 gather_fusion.1
  51.6 0.7 gather_fusion
  52.2 0.1 copy.38
  52.3 0.1 reshape.512
  52.5 0.1 iota_add_fusion
  52.6 0.4 multiply_cosine_fusion.1
  53.0 21.9 %all-to-all-done.1 = bf16[16,4,128,128]{3,2,1,0:T(8,128)(2,1)} async-done(((bf16[16,4,128,128]{3,2,1,0:T(8,128)(2,1)}), bf16[16,4,128,128]{3,2,1,0:T(8,128)(2,1)}, u32[]{:S(2)}, u32[]{:S(2)}) %all-to-all-start.1) | async-done | bytes 2097184 | tf_op jit(solution)/shard_map/all_to_all | solution.py:260
  74.9 3.2 %gather_fusion.2 = bf16[32,128,128]{2,1,0:T(8,128)(2,1)} fusion(bf16[64,128,128]{2,1,0:T(8,128)(2,1)} %bitcast.16, s32[1024]{0:T(1024)S(1)} %pad_clamp_fusion), kind=kCustom, calls=%fused_computation.2 | custom fusion | bytes 2097280 | tf_op jit(solution)/shard_map/gather | solution.py:175
  78.1 2.6 fusion.31.tail_ref
  80.7 3.3 %fusion = f32[768]{0:T(1024)S(1)} fusion(bf16[768,2880]{0,1:T(8,128)(2,1)} %all-gather.3.cloned.1.call-done), kind=kLoop, calls=%fused_computation.7 | loop fusion | flops 6634752 | bytes 4426752 | tf_op jit(solution)/shard_map/reduce_sum | solution.py:18
  84.1 0.2 copy-done.2
  84.3 2.8 fusion.39
  87.1 0.4 fusion.64
  87.6 3.1 %fusion.37 = f32[768,512]{0,1:T(8,128)S(1)} fusion(bf16[2880,512]{1,0:T(8,128)(2,1)S(1)} %copy-done.11, bf16[768,2880]{0,1:T(8,128)(2,1)S(1)} %copy-done.2, f32[2880]{0:T(1024)S(1)} %convert_element_type.108, f32[768]{0:T(1024)S(1)} %add_rsqrt_fusion.1), kind=kOutput, calls=%fused_computation.43 | convolution fusion | flops 2273771520 | bytes 8960256 | tf_op jit(solution)/shard_map/dot_general | solution.py:270
  90.7 0.2 subtract_convert_fusion
  90.9 0.1 pad_maximum_fusion
  91.0 4.2 %fusion.13 = bf16[1792,640]{1,0:T(8,128)(2,1)} fusion(s32[1792]{0:T(1024)S(1)} %min.28, pred[1792]{0:T(1024)(128)(4,1)S(1)} %lt.62, bf16[768,64]{0,1:T(8,128)(2,1)S(1)} %fusion.62, bf16[768,32]{0,1:T(8,128)(2,1)S(1)} %get-tuple-element.14, bf16[768,32]{0,1:T(8,128)(2,1)S(1)} %get-tuple-element.13, bf16[768,512]{0,1:T(8,128)(2,1)S(1)} %bitcast.75), kind=kOutput, calls=%fused_computation.22 | convolution fusion | flops 1769439232 | bytes 3285760 | tf_op jit(solution)/shard_map/dot_general | solution.py:239
  95.2 28.6 %shard_map.145 = bf16[16,112,512]{2,1,0:T(8,128)(2,1)} custom-call(f32[8]{0:T(128)} %sink_ref.1, bf16[16,112,640]{2,1,0:T(8,128)(2,1)} %bitcast.69, bf16[16,112,640]{2,1,0:T(8,128)(2,1)} %bitcast.70, bf16[16,128,128]{2,1,0:T(8,128)(2,1)} %fusion.31.tail_ref), custom_call_target="tpu_custom_call" | custom-call | flops 880803840 | bytes 4653056 | tf_op jit(solution)/shard_map/pallas_call | solution.py:145
  123.7 7.5 %convolution_convert_fusion = bf16[768,2880]{0,1:T(8,128)(2,1)} fusion(bf16[512,2880]{0,1:T(8,128)(2,1)S(1)} %copy-done, bf16[1792,512]{1,0:T(8,128)(2,1)} %bitcast.72, s32[768]{0:T(1024)S(1)} %get-tuple-element.18), kind=kOutput, calls=%fused_computation.20 | convolution fusion | flops 3678191616 | bytes 9210880 | tf_op jit(solution)/shard_map/dot_general | solution.py:290
  131.2 0.0 reduce-scatter.3.cloned.1.call-update
  131.2 0.0 all-gather.5.cloned.1.call-start
  131.3 40.6 %reduce-scatter.3.cloned.1.call-done = bf16[768,360]{0,1:T(8,128)(2,1)} async-done(((bf16[768,2880]{0,1:T(8,128)(2,1)}), bf16[768,360]{0,1:T(8,128)(2,1)}) %reduce-scatter.3.cloned.1.call-update) | async-done | bytes 552976 | tf_op jit(solution)/shard_map/reduce_scatter | solution.py:291
  171.8 2.2 add_convert_fusion.1
  174.0 0.0 all-gather.5.cloned.1.call-update
  174.1 0.3 reduce-scatter.5.cloned.1.call-start
  174.4 31.8 %all-gather.5.cloned.1.call-done = bf16[768,2880]{0,1:T(8,128)(2,1)} async-done(((bf16[768,360]{0,1:T(8,128)(2,1)}), bf16[768,2880]{0,1:T(8,128)(2,1)}) %all-gather.5.cloned.1.call-update) | async-done | bytes 4423696 | tf_op jit(solution)/shard_map/all_gather | solution.py:295
  206.2 3.3 %fusion.3 = f32[768]{0:T(1024)S(1)} fusion(bf16[768,2880]{0,1:T(8,128)(2,1)} %all-gather.5.cloned.1.call-done), kind=kLoop, calls=%fused_computation.10 | loop fusion | flops 6634752 | bytes 4426752 | tf_op jit(solution)/shard_map/reduce_sum | solution.py:18
  209.6 0.2 copy-done.3
  209.8 3.1 %fusion.33 = f32[768,360]{0,1:T(8,128)} fusion(bf16[2880,360]{0,1:T(8,128)(2,1)S(1)} %copy-done.12, bf16[768,2880]{0,1:T(8,128)(2,1)S(1)} %copy-done.3, f32[2880]{0:T(1024)S(1)} %convert_element_type.121, f32[768]{0:T(1024)S(1)} %add_rsqrt_fusion), kind=kOutput, calls=%fused_computation.41 | convolution fusion | flops 1601372160 | bytes 7617792 | tf_op jit(solution)/shard_map/dot_general | solution.py:297
  212.9 11.3 %convolution_convert_fusion.1 = bf16[768,2880]{0,1:T(8,128)(2,1)} fusion(bf16[360,2880]{1,0:T(8,128)(2,1)} %param.29, bf16[2880,360]{0,1:T(8,128)(2,1)} %param.28, bf16[768,2880]{0,1:T(8,128)(2,1)} %all-gather.5.cloned.1.call-done, f32[2880]{0:T(1024)S(1)} %convert_element_type.121, f32[768]{0:T(1024)S(1)} %add_rsqrt_fusion, f32[768,360]{0,1:T(8,128)} %fusion.33), kind=kOutput, calls=%fused_computation.21 | convolution fusion | flops 3197767680 | bytes 14115072 | tf_op jit(solution)/shard_map/dot_general | solution.py:301
  224.2 38.6 %reduce-scatter.5.cloned.1.call-done = bf16[768,360]{0,1:T(8,128)(2,1)} async-done(((bf16[768,2880]{0,1:T(8,128)(2,1)}), bf16[768,360]{0,1:T(8,128)(2,1)}) %reduce-scatter.5.cloned.1.call-update) | async-done | bytes 552976 | tf_op jit(solution)/shard_map/reduce_scatter | solution.py:300
  262.8 3.5 %fusion.16 = bf16[1792,360]{0,1:T(8,128)(2,1)S(1)} fusion(s32[1792]{0:T(1024)S(1)} %min.28, pred[1792]{0:T(1024)(128)(4,1)S(1)} %lt.62, bf16[768,360]{0,1:T(8,128)(2,1)} %reduce-scatter.5.cloned.1.call-done, bf16[768,360]{0,1:T(8,128)(2,1)S(1)} %copy-done.5), kind=kOutput, calls=%fused_computation.23 | convolution fusion | flops 995407872 | bytes 2405120 | tf_op jit(solution)/shard_map/dot_general | solution.py:239
  266.3 1.5 copy.39
  267.8 26.9 %all_to_all.15 = bf16[16,112,360]{2,1,0:T(8,128)(2,1)S(1)} all-to-all(bf16[16,112,360]{2,1,0:T(8,128)(2,1)} %bitcast.71), channel_id=1, replica_groups=mesh['req'=16,'tp'=8] {'req'}, dimensions={0} | all-to-all | bytes 2580480 | tf_op jit(solution)/shard_map/all_to_all | solution.py:308
  294.7 0.6 convolution_convert_fusion.2
  295.3 1.4 copy.41
  (41 shorter events, 0.2 us)
Async XLA Ops:
  6.5 117.2 %copy-start = (bf16[512,2880]{0,1:T(8,128)(2,1)S(1)}, bf16[512,2880]{0,1:T(8,128)(2,1)}, u32[]{:S(2)}) copy-start(bf16[512,2880]{0,1:T(8,128)(2,1)} %param.25) | copy-start | bytes 8847364
  10.2 10.2 %copy-start.10 = (s32[256]{0:T(256)S(1)}, s32[256]{0:T(256)}, u32[]{:S(2)}) copy-start(s32[256]{0:T(256)} %param.18) | copy-start | bytes 3076
  10.2 10.3 %copy-start.7 = (s32[16,16]{1,0:T(8,128)S(1)}, s32[16,16]{1,0:T(8,128)}, u32[]{:S(2)}) copy-start(s32[16,16]{1,0:T(8,128)} %param.17) | copy-start | bytes 3076
  11.6 26.8 %all-to-all-start = ((bf16[16,112,360]{2,1,0:T(8,128)(2,1)}), bf16[16,112,360]{2,1,0:T(8,128)(2,1)}, u32[]{:S(2)}, u32[]{:S(2)}) async-start(bf16[16,112,360]{2,1,0:T(8,128)(2,1)} %copy.37), calls=%async_computation | async-start | bytes 2752512 | tf_op jit(solution)/shard_map/all_to_all | solution.py:252
  19.4 61.3 %all-gather.3.cloned.1.call-start = ((), (), s32[]{:S(2)}) async-start(), calls=%async_computation.5 | async-start | bytes 4976640 | tf_op jit(solution)/shard_map/all_gather | solution.py:267
  38.3 3.7 %copy-start.6 = (bf16[4,128,1,128]{3,1,2,0:T(8,128)(2,1)S(1)}, bf16[4,128,1,128]{3,1,2,0:T(8,128)(2,1)}, u32[]{:S(2)}) copy-start(bf16[4,128,1,128]{3,1,2,0:T(8,128)(2,1)} %param.19) | copy-start | bytes 393220
  44.6 6.1 %copy-start.13 = (s32[64]{0:T(128)S(1)}, s32[64]{0:T(128)}, u32[]{:S(2)}) copy-start(s32[64]{0:T(128)} %param.20) | copy-start | bytes 772
  44.6 7.8 %copy-start.8 = (bf16[2880]{0:T(1024)(128)(2,1)S(1)}, bf16[2880]{0:T(1024)(128)(2,1)}, u32[]{:S(2)}) copy-start(bf16[2880]{0:T(1024)(128)(2,1)} %param.22) | copy-start | bytes 17284
  44.6 30.2 %all-to-all-start.1 = ((bf16[16,4,128,128]{3,2,1,0:T(8,128)(2,1)}), bf16[16,4,128,128]{3,2,1,0:T(8,128)(2,1)}, u32[]{:S(2)}, u32[]{:S(2)}) async-start(bf16[16,4,128,128]{3,2,1,0:T(8,128)(2,1)} %broadcast_in_dim.23), calls=%async_computation.1 | async-start | bytes 4194304 | tf_op jit(solution)/shard_map/all_to_all | solution.py:260
  49.5 122.3 %reduce-scatter.3.cloned.1.call-start = ((), (), s32[]{:S(2)}) async-start(), calls=%async_computation.6 | async-start | bytes 4976640 | tf_op jit(solution)/shard_map/reduce_scatter | solution.py:291
  80.7 3.6 %copy-start.2 = (bf16[768,2880]{0,1:T(8,128)(2,1)S(1)}, bf16[768,2880]{0,1:T(8,128)(2,1)}, u32[]{:S(2)}) copy-start(bf16[768,2880]{0,1:T(8,128)(2,1)} %all-gather.3.cloned.1.call-done) | copy-start | bytes 13271044
  84.3 3.3 %copy-start.11 = (bf16[2880,512]{1,0:T(8,128)(2,1)S(1)}, bf16[2880,512]{1,0:T(8,128)(2,1)}, u32[]{:S(2)}) copy-start(bf16[2880,512]{1,0:T(8,128)(2,1)} %param.23) | copy-start | bytes 8847364
  131.2 40.6 %copy-start.4 = (bf16[768,360]{0,1:T(8,128)(2,1)S(1)}, bf16[768,360]{0,1:T(8,128)(2,1)}, u32[]{:S(2)}) copy-start(bf16[768,360]{0,1:T(8,128)(2,1)} %fusion.30) | copy-start | bytes 1658884
  131.2 43.2 %copy-start.9 = (bf16[2880]{0:T(1024)(128)(2,1)S(1)}, bf16[2880]{0:T(1024)(128)(2,1)}, u32[]{:S(2)}) copy-start(bf16[2880]{0:T(1024)(128)(2,1)} %param.26) | copy-start | bytes 17284
  131.2 75.0 %all-gather.5.cloned.1.call-start = ((), (), s32[]{:S(2)}) async-start(), calls=%async_computation.7 | async-start | bytes 4976640 | tf_op jit(solution)/shard_map/all_gather | solution.py:295
  171.8 37.7 %copy-start.12 = (bf16[2880,360]{0,1:T(8,128)(2,1)S(1)}, bf16[2880,360]{0,1:T(8,128)(2,1)}, u32[]{:S(2)}) copy-start(bf16[2880,360]{0,1:T(8,128)(2,1)} %param.27) | copy-start | bytes 6220804
  174.1 88.7 %reduce-scatter.5.cloned.1.call-start = ((), (), s32[]{:S(2)}) async-start(), calls=%async_computation.8 | async-start | bytes 4976640 | tf_op jit(solution)/shard_map/reduce_scatter | solution.py:300
  206.2 3.6 %copy-start.3 = (bf16[768,2880]{0,1:T(8,128)(2,1)S(1)}, bf16[768,2880]{0,1:T(8,128)(2,1)}, u32[]{:S(2)}) copy-start(bf16[768,2880]{0,1:T(8,128)(2,1)} %all-gather.5.cloned.1.call-done) | copy-start | bytes 13271044
  224.2 38.6 %copy-start.5 = (bf16[768,360]{0,1:T(8,128)(2,1)S(1)}, bf16[768,360]{0,1:T(8,128)(2,1)}, u32[]{:S(2)}) copy-start(bf16[768,360]{0,1:T(8,128)(2,1)} %add_convert_fusion.1) | copy-start | bytes 1658884
  267.8 28.9 %copy-start.1 = (bf16[512,2880]{0,1:T(8,128)(2,1)S(1)}, bf16[512,2880]{0,1:T(8,128)(2,1)}, u32[]{:S(2)}) copy-start(bf16[512,2880]{0,1:T(8,128)(2,1)} %param.25) | copy-start | bytes 8847364
Sparse Core Ops, SparseCore 0:
  44.1 32.3 all-gather.2
  131.3 40.4 reduce-scatter.2
  174.2 31.9 all-gather.4
  224.3 38.4 reduce-scatter.4
